TPU v7x, 128 devices: a whole 4x4x4 slice. The times are simulated.
128 devices in a mesh: scan: 16 (over y, x), tile: 8 (over z, core).
Axes of the slice: x: 4, y: 4, z: 4, core: 2. Of those that a mesh axis runs over, the one named last changes fastest.
Arguments:
- pointing: bfloat16 [16, 4096, 2048], P('tile', 'scan'), may hold values from -0.125 to 0.125
- ground_bin: int32 [16, 4096], P('tile', 'scan'), may hold values from 0 to 23
- degrees: int32 [16], P('tile'), may hold values from 2 to 8
- lengths: int32 [16], P('tile'), may hold values from 1 to 4096, 40960 in all
- tile_lists: int32 [16, 16], P('tile'), may hold values from 0 to 127, as said below
- owner_map: int32 [128], replicated, may hold values from 0 to 7, as said below
Outputs:
- obs_matrix: float32 [16384, 16384], P('tile', 'scan')
Inputs may be any that keep to these rules, and one draw needn't show every extreme that they name: `owner_map`: for each j < 16, entries j * 8 to (j + 1) * 8 - 1 hold every owner 0 to 7 once. `tile_lists`: in each row, entries j * 1 to (j + 1) - 1 are distinct tiles of j * 8 to (j + 1) * 8 - 1; over the 2 rows of one index of tile, every owner is named (through owner_map) by exactly 4 entries.
All inputs are finite; a program needn't handle non-finite values. No bound on the sum of `lengths` on one device may be relied on, other than what follows from the above.
Results may differ from a plain program's by a relative error of at most 0.0003.
Values may be sent and summed in bfloat16 or wider, within the bound.
No kernel may reach another device: no remote copies, remote signals or barrier semaphores. Data moves between devices by JAX's collectives and lax.ppermute only.
A program may use at most 128 MiB of HBM per device.

v0:
```python
import jax
import jax.numpy as jnp
from jax import lax
from jax.sharding import PartitionSpec as P

DEG_MAX = 8
NGB = 24


def build_templates(ground_rows, lengths, degrees):
    sample_rows = ground_rows.shape[1]
    position = jnp.arange(sample_rows).astype(jnp.float32)
    length_value = lengths.astype(jnp.float32)[:, None]
    inside = position[None, :] < length_value
    coord = 2.0 * (position[None, :] + 0.5) / length_value - 1.0
    columns = []
    previous = jnp.ones_like(coord)
    current = coord
    for degree in range(1, DEG_MAX + 1):
        keep = jnp.logical_and(inside, (degree <= degrees)[:, None])
        columns.append(jnp.where(keep, current, jnp.float32(0.0)))
        following = ((2.0 * degree + 1.0) * coord * current - degree * previous) / (degree + 1.0)
        previous, current = (current, following)
    poly_part = jnp.stack(columns, axis=2)
    bins = jnp.logical_and(
        ground_rows[:, :, None] == jnp.arange(NGB)[None, None, :], inside[:, :, None]
    ).astype(jnp.float32)
    return jnp.concatenate([poly_part, bins], axis=2).astype(jnp.bfloat16)


def per_device(pointing, ground_bin, degrees, lengths, tile_lists, owner_map):
    scan_count, sample_rows, width = pointing.shape
    n_scan = lax.axis_size("scan")
    n_tile = lax.axis_size("tile")
    scan_index = lax.axis_index("scan")
    k_tiles = tile_lists.shape[1]
    k_cols = k_tiles // n_scan
    tile_pixels = width // k_tiles
    col_width = k_cols * tile_pixels
    template_cols = DEG_MAX + NGB
    first_local = scan_index * sample_rows
    position = first_local + jnp.arange(sample_rows)
    inside = position[None, :] < lengths[:, None]
    masked = jnp.where(inside[:, :, None], pointing, jnp.zeros_like(pointing))
    first_col = scan_index * col_width
    point_rows = lax.all_gather(masked, "scan", axis=1, tiled=True)
    ground_rows = lax.all_gather(ground_bin, "scan", axis=1, tiled=True)
    template = build_templates(ground_rows, lengths, degrees)
    own_cols = lax.dynamic_slice_in_dim(point_rows, first_col, col_width, 2)
    gram_part = jnp.einsum("snp,snq->spq", point_rows, own_cols, preferred_element_type=jnp.float32)
    proj_part = jnp.einsum("snt,snp->stp", template, point_rows, preferred_element_type=jnp.float32)
    norm_part = jnp.einsum("snt,snu->stu", template, template, preferred_element_type=jnp.float32)
    normal = norm_part + jnp.eye(template_cols, dtype=jnp.float32)[None, :, :]
    factor = jnp.linalg.cholesky(normal)
    whitened = jax.scipy.linalg.solve_triangular(factor, proj_part, lower=True)
    whitened_cols = lax.dynamic_slice_in_dim(whitened, first_col, col_width, 2)
    correction = jnp.einsum(
        "stp,stq->spq", whitened, whitened_cols, precision=lax.Precision.HIGHEST
    )
    contrib = gram_part - correction
    tile_rows = contrib.reshape(scan_count * k_tiles, tile_pixels, col_width)
    row_tiles = tile_lists.reshape(-1)
    matches = row_tiles[:, None] == jnp.arange(owner_map.shape[0])[None, :]
    owners = jnp.sum(jnp.where(matches, owner_map[None, :], 0), axis=1)
    row_total = scan_count * k_tiles
    capacity = row_total // n_tile
    ordering = jnp.argsort(owners * row_total + jnp.arange(row_total), stable=True)
    local_cols = (
        lax.dynamic_slice_in_dim(tile_lists, scan_index * k_cols, k_cols, 1) - scan_index * n_tile
    )
    local_cols = jnp.repeat(local_cols, k_tiles, axis=0)
    labels = jnp.concatenate([(row_tiles // n_tile)[:, None], local_cols], axis=1)
    send_rows = tile_rows[ordering].reshape(n_tile, capacity, tile_pixels, col_width)
    send_labels = labels[ordering].reshape(n_tile, capacity, 1 + k_cols)
    recv_rows, recv_labels = (
        lax.all_to_all(send_rows, "tile", split_axis=0, concat_axis=0, tiled=True),
        lax.all_to_all(send_labels, "tile", split_axis=0, concat_axis=0, tiled=True),
    )
    item_total = n_tile * capacity
    recv_rows = recv_rows.reshape(item_total, tile_pixels, k_cols, tile_pixels)
    recv_labels = recv_labels.reshape(item_total, 1 + k_cols)
    row_select = (recv_labels[:, 0:1] == jnp.arange(n_scan)[None, :]).astype(jnp.float32)
    col_select = (recv_labels[:, 1:, None] == jnp.arange(n_tile)[None, None, :]).astype(jnp.float32)
    placing = row_select[:, :, None, None] * col_select[:, None, :, :]
    placed = jnp.einsum("irkc,ixky->rxcy", placing, recv_rows, precision=lax.Precision.HIGHEST)
    return placed.reshape(n_scan * tile_pixels, n_tile * tile_pixels)


def solution(mesh):
    return jax.shard_map(
        per_device,
        mesh=mesh,
        in_specs=(
            P("tile", "scan", None),
            P("tile", "scan"),
            P("tile"),
            P("tile"),
            P("tile", None),
            P(),
        ),
        out_specs=P("tile", "scan"),
        check_vma=False,
    )
```

profile of v0, /device:TPU:1, one launch (start us, length us, event | category | flops | bytes accessed | tf_op | source)
XLA Modules:
  0.0 305.9 jit_solution(982954570127545856)
XLA Ops:
  6.5 0.7 broadcast_compare_fusion.1
  7.3 3.1 %broadcast_select_fusion = bf16[2,256,2048]{2,1,0:T(8,128)(2,1)} fusion(bf16[2,256,2048]{2,1,0:T(8,128)(2,1)} %param.6, pred[2,256]{1,0:T(4,128)(4,1)S(1)} %broadcast_compare_fusion.1), kind=kLoop, calls=%fused_computation.7 | loop fusion | flops 1048576 | bytes 4194816 | tf_op jit(solution)/shard_map/jit(_where)/select_n | solution.py:44
  10.4 0.6 copy-done.1
  11.9 1.7 sort.17
  14.1 0.7 copy.54
  14.9 6.8 %all-to-all-start.1 = ((s32[8,4,2]{1,2,0:T(2,128)}), s32[8,4,2]{1,2,0:T(2,128)S(1)}, u32[]{:S(2)}, u32[]{:S(2)}) async-start(s32[8,4,2]{1,2,0:T(2,128)} %copy.54), calls=%async_computation.1 | async-start | bytes 16384 | tf_op jit(solution)/shard_map/all_to_all | solution.py:77
  21.7 20.8 %all_gather.7 = s32[2,4096]{1,0:T(2,128)S(1)} all-gather(s32[2,256]{1,0:T(2,128)S(1)} %copy-done), channel_id=1, replica_groups=mesh['scan'=16,'tile'=8] {'scan'}, dimensions={1}, use_global_device_ids=true | all-gather | bytes 34816 | tf_op jit(solution)/shard_map/all_gather | solution.py:47
  42.6 0.7 fusion.28
  43.5 0.7 concatenate.7
  44.6 5.9 %custom-call.8 = f32[2,32,32]{2,1,0:T(8,128)S(1)} custom-call(f32[2,32,32]{2,1,0:T(8,128)S(1)} %fusion.17), custom_call_target="Cholesky" | custom-call | tf_op jit(solution)/shard_map/jit(cholesky)/cholesky | solution.py:54
  50.7 4.9 %custom-call.9 = f32[2,1,32,32]{2,3,1,0:T(8,128)S(1)} custom-call(f32[2,1,32,32]{3,2,1,0:T(8,128)S(1)} %select_bitcast_fusion), custom_call_target="InvertDiagBlocksLowerTriangular" | custom-call | tf_op jit(solution)/shard_map/jit(_solve_triangular)/vmap()/triangular_solve | solution.py:55
  55.6 155.0 %all-gather.2.cloned.1.call-done = bf16[2,4096,2048]{2,1,0:T(8,128)(2,1)} async-done(((bf16[2,256,2048]{2,1,0:T(8,128)(2,1)}), bf16[2,4096,2048]{2,1,0:T(8,128)(2,1)}) %all-gather.2.cloned.1.call-update) | async-done | bytes 33554448 | tf_op jit(solution)/shard_map/all_gather | solution.py:46
  210.6 13.5 %fusion.36 = f32[2,32,2048]{2,1,0:T(8,128)S(1)} fusion(bf16[2,4096,32]{1,2,0:T(8,128)(2,1)S(1)} %concatenate.7, bf16[2,4096,2048]{2,1,0:T(8,128)(2,1)} %all-gather.2.cloned.1.call-done), kind=kOutput, calls=%fused_computation.94 | convolution fusion | flops 1073741824 | bytes 34603008 | tf_op jit(solution)/shard_map/snt,snp->stp/dot_general | solution.py:51
  224.1 0.6 fusion.14
  224.8 17.5 %fusion = f32[2,2048,128]{2,1,0:T(8,128)S(1)} fusion(bf16[2,4096,2048]{2,1,0:T(8,128)(2,1)} %all-gather.2.cloned.1.call-done, s32[]{:T(128)S(6)} %select_n.117), kind=kOutput, calls=%fused_computation.5 | convolution fusion | flops 4294967296 | bytes 37748740 | tf_op jit(solution)/shard_map/snp,snq->spq/dot_general | solution.py:50
  242.2 3.4 %convolution_subtract_fusion = f32[2,2048,128]{2,1,0:T(8,128)S(1)} fusion(f32[2,2048,128]{2,1,0:T(8,128)S(1)} %fusion, f32[2,32,2048]{2,1,0:T(8,128)S(1)} %fusion.14, s32[]{:T(128)S(6)} %select_n.117), kind=kOutput, calls=%fused_computation.4 | convolution fusion | flops 201850880 | bytes 4751364 | tf_op jit(solution)/shard_map/stp,stq->spq/dot_general | solution.py:57
  245.7 2.0 gather_fusion
  247.7 4.3 %copy.50 = f32[8,4,128,128]{3,1,2,0:T(4,128)} copy(f32[8,4,128,128]{3,2,1,0:T(8,128)} %bitcast.45) | data formatting | bytes 4194304 | tf_op jit(solution)/shard_map/reshape | solution.py:73
  252.0 5.3 %all-to-all-start = ((f32[8,4,128,128]{3,1,2,0:T(4,128)}), f32[8,4,128,128]{3,1,2,0:T(4,128)S(1)}, u32[]{:S(2)}, u32[]{:S(2)}) async-start(f32[8,4,128,128]{3,1,2,0:T(4,128)} %copy.50), calls=%async_computation | async-start | bytes 4194304 | tf_op jit(solution)/shard_map/all_to_all | solution.py:76
  257.4 26.1 %all-to-all-done = f32[8,4,128,128]{3,1,2,0:T(4,128)S(1)} async-done(((f32[8,4,128,128]{3,1,2,0:T(4,128)}), f32[8,4,128,128]{3,1,2,0:T(4,128)S(1)}, u32[]{:S(2)}, u32[]{:S(2)}) %all-to-all-start) | async-done | bytes 2097184 | tf_op jit(solution)/shard_map/all_to_all | solution.py:76
  283.5 0.6 copy.51
  284.1 6.9 %convolution_bitcast_fusion = f32[16,128,8,128]{3,0,2,1:T(8,128)S(1)} fusion(f32[32,128,128,1]{2,0,3,1:T(8,128)S(1)} %bitcast.46, f32[32,8]{0,1:T(8,128)S(1)} %fusion.32, f32[32,16]{0,1:T(8,128)S(1)} %fusion.30), kind=kOutput, calls=%fused_computation.3 | convolution fusion | flops 805310464 | bytes 10488832 | tf_op jit(solution)/shard_map/irkc,ixky->rxcy/dot_general | solution.py:85
  290.9 2.7 copy.56
  293.6 5.5 %copy.64 = f32[256,8,8,128]{3,1,2,0:T(8,128)} copy(f32[256,8,8,128]{3,2,1,0:T(8,128)S(1)} %bitcast.43) | data formatting | bytes 16777216
  (47 shorter events, 2.4 us)
Async XLA Ops:
  6.5 204.1 %all-gather.2.cloned.1.call-start = ((), (), s32[]{:S(2)}) async-start(), calls=%async_computation.2 | async-start | bytes 35651584 | tf_op jit(solution)/shard_map/all_gather | solution.py:46
  10.4 0.7 copy-start.1
  10.4 1.3 copy-start.4
  10.4 11.3 %copy-start.2 = (s32[2]{0:T(128)S(1)}, s32[2]{0:T(128)}, u32[]{:S(2)}) copy-start(s32[2]{0:T(128)} %param.9) | copy-start | bytes 28
  10.4 11.3 %copy-start = (s32[2,256]{1,0:T(2,128)S(1)}, s32[2,256]{1,0:T(2,128)}, u32[]{:S(2)}) copy-start(s32[2,256]{1,0:T(2,128)} %param.7) | copy-start | bytes 6148
  10.4 32.1 %copy-start.3 = (s32[2]{0:T(128)S(1)}, s32[2]{0:T(128)}, u32[]{:S(2)}) copy-start(s32[2]{0:T(128)} %param.8) | copy-start | bytes 28
  14.9 237.1 %all-to-all-start.1 = ((s32[8,4,2]{1,2,0:T(2,128)}), s32[8,4,2]{1,2,0:T(2,128)S(1)}, u32[]{:S(2)}, u32[]{:S(2)}) async-start(s32[8,4,2]{1,2,0:T(2,128)} %copy.54), calls=%async_computation.1 | async-start | bytes 16384 | tf_op jit(solution)/shard_map/all_to_all | solution.py:77
  252.0 31.5 %all-to-all-start = ((f32[8,4,128,128]{3,1,2,0:T(4,128)}), f32[8,4,128,128]{3,1,2,0:T(4,128)S(1)}, u32[]{:S(2)}, u32[]{:S(2)}) async-start(f32[8,4,128,128]{3,1,2,0:T(4,128)} %copy.50), calls=%async_computation | async-start | bytes 4194304 | tf_op jit(solution)/shard_map/all_to_all | solution.py:76
Sparse Core Ops, SparseCore 0:
  10.6 200.0 all-gather.1
where the time goes:
time: 306 us
  waiting for transfers between devices  181 us (59%)
  matrix products  42.2 us (14%)
  blocking collectives  20.8 us (7%)
  local copies, waits for them, and re-layouts  18.3 us (6%)
  other arithmetic  17.9 us (6%)
  between operations  13.6 us (4%)
  starting transfers between devices  12.1 us (4%)
    all_gather x1, waiting for transfers between devices, per_device(): point_rows = lax.all_gather(masked, 'scan', axis=1, tiled=True)  155 us
    all_to_all x1, waiting for transfers between devices, per_device(): lax.all_to_all(send_rows, 'tile', split_axis=0, concat_axis=0, tiled=True)  26.1 us
    all_gather x1, blocking collectives, per_device(): ground_rows = lax.all_gather(ground_bin, 'scan', axis=1, tiled=True)  20.8 us
    dot_general x1, matrix products, per_device(): jnp.einsum('snp,snq->spq', point_rows, own_cols, preferred_element_type=j...  17.5 us
    dot_general x1, matrix products, per_device(): jnp.einsum('snt,snp->stp', template, point_rows, preferred_element_type=j...  13.5 us
    dot_general x1, matrix products, per_device(): jnp.einsum('irkc,ixky->rxcy', placing, recv_rows, precision=lax.Precision...  6.85 us
    all_to_all x1, starting transfers between devices, per_device(): lax.all_to_all(send_labels, 'tile', split_axis=0, concat_axis=0, tiled=True)  6.8 us
    unnamed x11, local copies, waits for them, and re-layouts  6.13 us
  transfers between devices with their start and end apart: 3, of which 2 were waited for; matrix products, arithmetic and copies ran while one was open for 19% of the time, Pallas kernels for 0%

commit v1 on v0

--- a/solution.py
+++ b/solution.py
@@ -1,15 +1,15 @@
 import jax
 import jax.numpy as jnp
 from jax import lax
-from jax.sharding import PartitionSpec as P
+from jax.sharding import Mesh, PartitionSpec as P
 
 DEG_MAX = 8
 NGB = 24
+SCAN_AXES = ("sy", "sx")
 
 
-def build_templates(ground_rows, lengths, degrees):
-    sample_rows = ground_rows.shape[1]
-    position = jnp.arange(sample_rows).astype(jnp.float32)
+def build_templates(ground_rows, position, lengths, degrees):
+    position = position.astype(jnp.float32)
     length_value = lengths.astype(jnp.float32)[:, None]
     inside = position[None, :] < length_value
     coord = 2.0 * (position[None, :] + 0.5) / length_value - 1.0
@@ -30,34 +30,58 @@
 
 def per_device(pointing, ground_bin, degrees, lengths, tile_lists, owner_map):
     scan_count, sample_rows, width = pointing.shape
-    n_scan = lax.axis_size("scan")
+    n_sy = lax.axis_size("sy")
+    n_sx = lax.axis_size("sx")
+    n_scan = n_sy * n_sx
     n_tile = lax.axis_size("tile")
-    scan_index = lax.axis_index("scan")
+    sy = lax.axis_index("sy")
+    sx = lax.axis_index("sx")
+    scan_index = sy * n_sx + sx
     k_tiles = tile_lists.shape[1]
-    k_cols = k_tiles // n_scan
     tile_pixels = width // k_tiles
-    col_width = k_cols * tile_pixels
+    col_width = tile_pixels
+    half = k_tiles // 2 + 1
     template_cols = DEG_MAX + NGB
-    first_local = scan_index * sample_rows
-    position = first_local + jnp.arange(sample_rows)
+
+    position = scan_index * sample_rows + jnp.arange(sample_rows)
     inside = position[None, :] < lengths[:, None]
     masked = jnp.where(inside[:, :, None], pointing, jnp.zeros_like(pointing))
-    first_col = scan_index * col_width
-    point_rows = lax.all_gather(masked, "scan", axis=1, tiled=True)
-    ground_rows = lax.all_gather(ground_bin, "scan", axis=1, tiled=True)
-    template = build_templates(ground_rows, lengths, degrees)
-    own_cols = lax.dynamic_slice_in_dim(point_rows, first_col, col_width, 2)
-    gram_part = jnp.einsum("snp,snq->spq", point_rows, own_cols, preferred_element_type=jnp.float32)
-    proj_part = jnp.einsum("snt,snp->stp", template, point_rows, preferred_element_type=jnp.float32)
+    template = build_templates(ground_bin, position, lengths, degrees)
+    proj_part = jnp.einsum("snt,snp->stp", template, masked, preferred_element_type=jnp.float32)
     norm_part = jnp.einsum("snt,snu->stu", template, template, preferred_element_type=jnp.float32)
-    normal = norm_part + jnp.eye(template_cols, dtype=jnp.float32)[None, :, :]
+    proj, norm = lax.psum((proj_part, norm_part), SCAN_AXES)
+
+    rows_x = lax.all_gather(masked, "sx", axis=1, tiled=True)
+    wrapped = jnp.concatenate([rows_x, rows_x[:, :, : half * tile_pixels]], axis=2)
+    parts = []
+    for y in range(n_sy):
+        col = y * n_sx + sx
+        row_blocks = lax.dynamic_slice_in_dim(wrapped, col * tile_pixels, half * tile_pixels, 2)
+        col_block = lax.dynamic_slice_in_dim(rows_x, col * tile_pixels, tile_pixels, 2)
+        parts.append(
+            jnp.einsum("snp,snq->spq", row_blocks, col_block, preferred_element_type=jnp.float32)
+        )
+    gram_part = lax.psum_scatter(jnp.stack(parts), "sy", scatter_dimension=0, tiled=False)
+
+    normal = norm + jnp.eye(template_cols, dtype=jnp.float32)[None, :, :]
     factor = jnp.linalg.cholesky(normal)
-    whitened = jax.scipy.linalg.solve_triangular(factor, proj_part, lower=True)
-    whitened_cols = lax.dynamic_slice_in_dim(whitened, first_col, col_width, 2)
-    correction = jnp.einsum(
-        "stp,stq->spq", whitened, whitened_cols, precision=lax.Precision.HIGHEST
-    )
-    contrib = gram_part - correction
+    whitened = jax.scipy.linalg.solve_triangular(factor, proj, lower=True)
+    w_wrapped = jnp.concatenate([whitened, whitened[:, :, : half * tile_pixels]], axis=2)
+    w_rows = lax.dynamic_slice_in_dim(w_wrapped, scan_index * tile_pixels, half * tile_pixels, 2)
+    w_col = lax.dynamic_slice_in_dim(whitened, scan_index * tile_pixels, tile_pixels, 2)
+    correction = jnp.einsum("stp,stq->spq", w_rows, w_col, precision=lax.Precision.HIGHEST)
+    own = (gram_part - correction).reshape(scan_count, half, tile_pixels, col_width)
+
+    received = []
+    for d in range(k_tiles - half, 0, -1):
+        block = jnp.swapaxes(own[:, d], 1, 2)
+        perm = [(i, (i + d) % n_scan) for i in range(n_scan)]
+        received.append(lax.ppermute(block, SCAN_AXES, perm))
+    relative = jnp.concatenate([own, jnp.stack(received, axis=1)], axis=1)
+    column = jnp.roll(relative, scan_index, axis=1)
+    contrib = column.reshape(scan_count, width, col_width)
+
+    k_cols = 1
     tile_rows = contrib.reshape(scan_count * k_tiles, tile_pixels, col_width)
     row_tiles = tile_lists.reshape(-1)
     matches = row_tiles[:, None] == jnp.arange(owner_map.shape[0])[None, :]
@@ -87,17 +111,21 @@
 
 
 def solution(mesh):
+    devices = mesh.devices.transpose([mesh.axis_names.index("scan"), mesh.axis_names.index("tile")])
+    n_scan, n_tile = devices.shape
+    n_sx = 4 if n_scan % 4 == 0 else 1
+    sub = Mesh(devices.reshape(n_scan // n_sx, n_sx, n_tile), ("sy", "sx", "tile"))
     return jax.shard_map(
         per_device,
-        mesh=mesh,
+        mesh=sub,
         in_specs=(
-            P("tile", "scan", None),
-            P("tile", "scan"),
+            P("tile", SCAN_AXES, None),
+            P("tile", SCAN_AXES),
             P("tile"),
             P("tile"),
             P("tile", None),
             P(),
         ),
-        out_specs=P("tile", "scan"),
+        out_specs=P("tile", SCAN_AXES),
         check_vma=False,
     )

time: 306 us -> 297 us (0.971)
  waiting for transfers between devices: 181 us -> 119 us
  blocking collectives: 20.8 us -> 59.9 us
  starting transfers between devices: 12.1 us -> 32.7 us
  matrix products: 42.2 us -> 26 us
  local copies, waits for them, and re-layouts: 18.3 us -> 23.8 us
    all_gather x1, waiting for transfers between devices: 155 us -> 84.5 us  [per_device(): rows_x = lax.all_gather(masked, 'sx', axis=1, tiled=True)]
    psum x0 -> x1, blocking collectives: none -> 59.9 us  [per_device(): proj, norm = lax.psum((proj_part, norm_part), SCAN_AXES)]
    all_gather x1 -> x0, blocking collectives: 20.8 us -> none  [per_device(): ground_rows = lax.all_gather(ground_bin, 'scan', axis=1, tiled=True)]
    dot_general x3 -> x6, matrix products: 34.4 us -> 17.4 us  [the longest x4 11.2 us: per_device(): jnp.einsum('snp,snq->spq', row_blocks, col_block, preferred_element_type=...]
    all_to_all x1, starting transfers between devices: 5.26 us -> 20.8 us  [per_device(): lax.all_to_all(send_rows, 'tile', split_axis=0, concat_axis=0, tiled=True)]
    ppermute x0 -> x7, waiting for transfers between devices: none -> 8.81 us  [per_device(): received.append(lax.ppermute(block, SCAN_AXES, perm))]
    ppermute x0 -> x7, starting transfers between devices: none -> 6.44 us  [per_device(): received.append(lax.ppermute(block, SCAN_AXES, perm))]
    unnamed x11 -> x35, local copies, waits for them, and re-layouts: 6.13 us -> 9.09 us
  transfers between devices with their start and end apart: 3 -> 12, of which waited for: 2 -> 7; matrix products, arithmetic and copies ran while one was open for 19% -> 16% of each run, Pallas kernels for 0% -> 0%
where the time goes in v1:
time: 297 us
  waiting for transfers between devices  119 us (40%)
  blocking collectives  59.9 us (20%)
  starting transfers between devices  32.7 us (11%)
  matrix products  26 us (9%)
  local copies, waits for them, and re-layouts  23.8 us (8%)
  other arithmetic  19.7 us (7%)
  between operations  15.3 us (5%)
    all_gather x1, waiting for transfers between devices, per_device(): rows_x = lax.all_gather(masked, 'sx', axis=1, tiled=True)  84.5 us
    psum x1, blocking collectives, per_device(): proj, norm = lax.psum((proj_part, norm_part), SCAN_AXES)  59.9 us
    all_to_all x1, waiting for transfers between devices, per_device(): lax.all_to_all(send_rows, 'tile', split_axis=0, concat_axis=0, tiled=True)  26.1 us
    all_to_all x1, starting transfers between devices, per_device(): lax.all_to_all(send_rows, 'tile', split_axis=0, concat_axis=0, tiled=True)  20.8 us
    dot_general x4, matrix products, per_device(): jnp.einsum('snp,snq->spq', row_blocks, col_block, preferred_element_type=...  11.2 us
    unnamed x35, local copies, waits for them, and re-layouts  9.09 us
    ppermute x7, waiting for transfers between devices, per_device(): received.append(lax.ppermute(block, SCAN_AXES, perm))  8.81 us
    dot_general x1, matrix products, per_device(): jnp.einsum('irkc,ixky->rxcy', placing, recv_rows, precision=lax.Precision...  6.85 us
  transfers between devices with their start and end apart: 12, of which 7 were waited for; matrix products, arithmetic and copies ran while one was open for 16% of the time, Pallas kernels for 0%

profile of v1, /device:TPU:1, one launch (start us, length us, event | category | flops | bytes accessed | tf_op | source)
XLA Modules:
  0.0 296.9 jit_solution(12758545865262066095)
XLA Ops:
  8.2 3.1 %broadcast_select_fusion = bf16[2,256,2048]{2,1,0:T(8,128)(2,1)} fusion(bf16[2,256,2048]{2,1,0:T(8,128)(2,1)} %param.6, pred[2,256]{1,0:T(4,128)(4,1)S(1)} %broadcast_compare_fusion.1), kind=kLoop, calls=%fused_computation.26 | loop fusion | flops 1048576 | bytes 4194816 | tf_op jit(solution)/shard_map/jit(_where)/select_n | solution.py:48
  11.7 2.9 fusion.74
  14.7 84.5 %all-gather.2.cloned.1.call-done = bf16[2,1024,2048]{2,1,0:T(8,128)(2,1)} async-done(((bf16[2,256,2048]{2,1,0:T(8,128)(2,1)}), bf16[2,1024,2048]{2,1,0:T(8,128)(2,1)}) %all-gather.2.cloned.1.call-update) | async-done | bytes 8388624 | tf_op jit(solution)/shard_map/all_gather | solution.py:54
  99.2 2.9 slice.63
  104.0 2.7 fusion.15
  106.7 2.8 fusion.18
  109.6 2.8 fusion.21
  112.4 2.8 fusion.12
  115.2 2.5 pad_maximum_fusion
  122.1 5.4 %all-to-all-start.1 = ((s32[8,4,2]{1,2,0:T(2,128)}), s32[8,4,2]{1,2,0:T(2,128)S(1)}, u32[]{:S(2)}, u32[]{:S(2)}) async-start(s32[8,4,2]{1,2,0:T(2,128)} %copy.92), calls=%async_computation.2 | async-start | bytes 16384 | tf_op jit(solution)/shard_map/all_to_all | solution.py:101
  127.7 59.9 %psum.14 = f32[2,32,32]{1,2,0:T(8,128)S(1)} all-reduce(f32[2,32,32]{1,2,0:T(8,128)S(1)} %fusion.73), channel_id=1, replica_groups=mesh['sy'=4,'sx'=4,'tile'=8] {'sy','sx'}, use_global_device_ids=true, to_apply=%region_1.2 | all-reduce | flops 2048 | bytes 16384 | tf_op jit(solution)/shard_map/psum | solution.py:52
  187.7 5.9 %custom-call.8 = f32[2,32,32]{2,1,0:T(8,128)S(1)} custom-call(f32[2,32,32]{2,1,0:T(8,128)S(1)} %fusion.35), custom_call_target="Cholesky" | custom-call | tf_op jit(solution)/shard_map/jit(cholesky)/cholesky | solution.py:67
  193.9 4.9 %custom-call.9 = f32[2,1,32,32]{2,3,1,0:T(8,128)S(1)} custom-call(f32[2,1,32,32]{3,2,1,0:T(8,128)S(1)} %select_bitcast_fusion), custom_call_target="InvertDiagBlocksLowerTriangular" | custom-call | tf_op jit(solution)/shard_map/jit(_solve_triangular)/vmap()/triangular_solve | solution.py:68
  200.5 3.3 %convolution_subtract_fusion = f32[2,1152,128]{2,1,0:T(8,128)S(1)} fusion(f32[1,2,1152,128]{3,2,1,0:T(8,128)} %reduce-scatter.2.cloned.1.call-done, s32[]{:T(128)S(6)} %select_n.173, f32[2,32,2048]{2,1,0:T(8,128)S(1)} %fusion.33, f32[2,32,1152]{2,1,0:T(8,128)S(1)} %slice.64, s32[]{:T(128)S(6)} %select_n.174), kind=kOutput, calls=%fused_computation.21 | convolution fusion | flops 113614848 | bytes 3211272 | tf_op jit(solution)/shard_map/stp,stq->spq/dot_general | solution.py:72
  205.8 2.4 collective-permute-start.3
  208.2 2.7 collective-permute-start.4
  213.0 2.3 collective-permute-done.2
  215.3 3.1 %collective-permute-done.3 = f32[2,128,128]{2,1,0:T(8,128)S(1)} collective-permute-done((f32[2,128,128]{2,1,0:T(8,128)S(1)}, f32[2,128,128]{2,1,0:T(8,128)S(1)}, u32[]{:S(2)}, u32[]{:S(2)}) %collective-permute-start.3) | collective-permute-done | bytes 131104 | tf_op jit(solution)/shard_map/ppermute | solution.py:79
  222.6 4.3 %copy.88 = f32[8,4,128,128]{3,1,2,0:T(4,128)} copy(f32[8,4,128,128]{3,2,1,0:T(8,128)} %bitcast.97) | data formatting | bytes 4194304 | tf_op jit(solution)/shard_map/reshape | solution.py:97
  226.9 20.8 %all-to-all-start = ((f32[8,4,128,128]{3,1,2,0:T(4,128)}), f32[8,4,128,128]{3,1,2,0:T(4,128)S(1)}, u32[]{:S(2)}, u32[]{:S(2)}) async-start(f32[8,4,128,128]{3,1,2,0:T(4,128)} %copy.88), calls=%async_computation.1 | async-start | bytes 4194304 | tf_op jit(solution)/shard_map/all_to_all | solution.py:100
  247.8 26.1 %all-to-all-done = f32[8,4,128,128]{3,1,2,0:T(4,128)S(1)} async-done(((f32[8,4,128,128]{3,1,2,0:T(4,128)}), f32[8,4,128,128]{3,1,2,0:T(4,128)S(1)}, u32[]{:S(2)}, u32[]{:S(2)}) %all-to-all-start) | async-done | bytes 2097184 | tf_op jit(solution)/shard_map/all_to_all | solution.py:100
  274.5 6.9 %convolution_bitcast_fusion = f32[16,128,8,128]{3,0,2,1:T(8,128)S(1)} fusion(f32[32,128,128,1]{2,0,3,1:T(8,128)S(1)} %bitcast.98, f32[32,8]{0,1:T(8,128)S(1)} %fusion.54, f32[32,16]{0,1:T(8,128)S(1)} %fusion.47), kind=kOutput, calls=%fused_computation.20 | convolution fusion | flops 805310464 | bytes 10488832 | tf_op jit(solution)/shard_map/irkc,ixky->rxcy/dot_general | solution.py:109
  281.3 2.7 copy.94
  284.0 5.5 %copy.113 = f32[256,8,8,128]{3,1,2,0:T(8,128)} copy(f32[256,8,8,128]{3,2,1,0:T(8,128)S(1)} %bitcast.92) | data formatting | bytes 16777216
  (101 shorter events, 18.5 us)
Async XLA Ops:
  7.4 4.0 %copy-start.3 = (s32[2]{0:T(128)S(1)}, s32[2]{0:T(128)}, u32[]{:S(2)}) copy-start(s32[2]{0:T(128)} %param.9) | copy-start | bytes 28
  7.4 4.1 %copy-start.4 = (s32[2]{0:T(128)S(1)}, s32[2]{0:T(128)}, u32[]{:S(2)}) copy-start(s32[2]{0:T(128)} %param.8) | copy-start | bytes 28
  7.4 4.2 %copy-start.1 = (s32[2,256]{1,0:T(2,128)S(1)}, s32[2,256]{1,0:T(2,128)}, u32[]{:S(2)}) copy-start(s32[2,256]{1,0:T(2,128)} %param.7) | copy-start | bytes 6148
  7.4 91.8 %all-gather.2.cloned.1.call-start = ((), (), s32[]{:S(2)}) async-start(), calls=%async_computation.3 | async-start | bytes 10485760 | tf_op jit(solution)/shard_map/all_gather | solution.py:54
  11.3 187.5 %all-reduce.2.cloned.1.call-start = ((), (), s32[]{:S(2)}) async-start(), calls=%async_computation.5 | async-start | bytes 1048576 | tf_op jit(solution)/shard_map/psum | solution.py:52
  14.6 185.9 %reduce-scatter.2.cloned.1.call-start = ((), (), s32[]{:S(2)}) async-start(), calls=%async_computation.4 | async-start | bytes 5898240 | tf_op jit(solution)/shard_map/reduce_scatter | solution.py:64
  99.2 4.8 %copy-start = (bf16[2,1024,2048]{2,1,0:T(8,128)(2,1)S(1)}, bf16[2,1024,2048]{2,1,0:T(8,128)(2,1)}, u32[]{:S(2)}) copy-start(bf16[2,1024,2048]{2,1,0:T(8,128)(2,1)} %all-gather.2.cloned.1.call-done) | copy-start | bytes 25165828
  117.7 0.7 copy-start.2
  117.7 1.3 copy-start.5
  122.1 104.7 %all-to-all-start.1 = ((s32[8,4,2]{1,2,0:T(2,128)}), s32[8,4,2]{1,2,0:T(2,128)S(1)}, u32[]{:S(2)}, u32[]{:S(2)}) async-start(s32[8,4,2]{1,2,0:T(2,128)} %copy.92), calls=%async_computation.2 | async-start | bytes 16384 | tf_op jit(solution)/shard_map/all_to_all | solution.py:101
  204.6 6.5 %collective-permute-start = (f32[2,128,128]{2,1,0:T(8,128)S(1)}, f32[2,128,128]{2,1,0:T(8,128)S(1)}, u32[]{:S(2)}, u32[]{:S(2)}) collective-permute-start(f32[2,128,128]{2,1,0:T(8,128)S(1)} %bitcast.105), channel_id=1, source_target_pairs={{0,56},{8,64},{16,72},{24,80},{32,88},{40,96},{48,104},{56,112},{6... | collective-permute-start | bytes 393224 | tf_op jit(solution)/shard_map/ppermute | solution.py:79
  204.7 8.2 %collective-permute-start.1 = (f32[2,128,128]{2,1,0:T(8,128)S(1)}, f32[2,128,128]{2,1,0:T(8,128)S(1)}, u32[]{:S(2)}, u32[]{:S(2)}) collective-permute-start(f32[2,128,128]{2,1,0:T(8,128)S(1)} %bitcast.104), channel_id=1, source_target_pairs={{0,48},{8,56},{16,64},{24,72},{32,80},{40,88},{48,96},{56,104},{64... | collective-permute-start | bytes 393224 | tf_op jit(solution)/shard_map/ppermute | solution.py:79
  204.8 10.5 %collective-permute-start.2 = (f32[2,128,128]{2,1,0:T(8,128)S(1)}, f32[2,128,128]{2,1,0:T(8,128)S(1)}, u32[]{:S(2)}, u32[]{:S(2)}) collective-permute-start(f32[2,128,128]{2,1,0:T(8,128)S(1)} %bitcast.103), channel_id=1, source_target_pairs={{0,40},{8,48},{16,56},{24,64},{32,72},{40,80},{48,88},{56,96},{64,... | collective-permute-start | bytes 393224 | tf_op jit(solution)/shard_map/ppermute | solution.py:79
  205.8 12.6 %collective-permute-start.3 = (f32[2,128,128]{2,1,0:T(8,128)S(1)}, f32[2,128,128]{2,1,0:T(8,128)S(1)}, u32[]{:S(2)}, u32[]{:S(2)}) collective-permute-start(f32[2,128,128]{2,1,0:T(8,128)S(1)} %bitcast.102), channel_id=1, source_target_pairs={{0,32},{8,40},{16,48},{24,56},{32,64},{40,72},{48,80},{56,88},{64,... | collective-permute-start | bytes 393224 | tf_op jit(solution)/shard_map/ppermute | solution.py:79
  208.2 10.2 %collective-permute-start.4 = (f32[2,128,128]{2,1,0:T(8,128)S(1)}, f32[2,128,128]{2,1,0:T(8,128)S(1)}, u32[]{:S(2)}, u32[]{:S(2)}) collective-permute-start(f32[2,128,128]{2,1,0:T(8,128)S(1)} %bitcast.101), channel_id=1, source_target_pairs={{0,24},{8,32},{16,40},{24,48},{32,56},{40,64},{48,72},{56,80},{64,... | collective-permute-start | bytes 393224 | tf_op jit(solution)/shard_map/ppermute | solution.py:79
  211.1 7.5 %collective-permute-start.5 = (f32[2,128,128]{2,1,0:T(8,128)S(1)}, f32[2,128,128]{2,1,0:T(8,128)S(1)}, u32[]{:S(2)}, u32[]{:S(2)}) collective-permute-start(f32[2,128,128]{2,1,0:T(8,128)S(1)} %bitcast.100), channel_id=1, source_target_pairs={{0,16},{8,24},{16,32},{24,40},{32,48},{40,56},{48,64},{56,72},{64,... | collective-permute-start | bytes 393224 | tf_op jit(solution)/shard_map/ppermute | solution.py:79
  212.9 7.1 %collective-permute-start.6 = (f32[2,128,128]{2,1,0:T(8,128)S(1)}, f32[2,128,128]{2,1,0:T(8,128)S(1)}, u32[]{:S(2)}, u32[]{:S(2)}) collective-permute-start(f32[2,128,128]{2,1,0:T(8,128)S(1)} %bitcast.99), channel_id=1, source_target_pairs={{0,8},{8,16},{16,24},{24,32},{32,40},{40,48},{48,56},{56,64},{64,7... | collective-permute-start | bytes 393224 | tf_op jit(solution)/shard_map/ppermute | solution.py:79
  226.9 47.0 %all-to-all-start = ((f32[8,4,128,128]{3,1,2,0:T(4,128)}), f32[8,4,128,128]{3,1,2,0:T(4,128)S(1)}, u32[]{:S(2)}, u32[]{:S(2)}) async-start(f32[8,4,128,128]{3,1,2,0:T(4,128)} %copy.88), calls=%async_computation.1 | async-start | bytes 4194304 | tf_op jit(solution)/shard_map/all_to_all | solution.py:100
Sparse Core Ops, SparseCore 0:
  11.4 87.6 all-gather.1
  117.8 53.7 reduce-scatter.1
Sparse Core Ops, SparseCore 1:
  15.0 159.2 all-reduce.1

commit v2 on v1

--- a/solution.py
+++ b/solution.py
@@ -47,30 +47,42 @@
     inside = position[None, :] < lengths[:, None]
     masked = jnp.where(inside[:, :, None], pointing, jnp.zeros_like(pointing))
     template = build_templates(ground_bin, position, lengths, degrees)
-    proj_part = jnp.einsum("snt,snp->stp", template, masked, preferred_element_type=jnp.float32)
-    norm_part = jnp.einsum("snt,snu->stu", template, template, preferred_element_type=jnp.float32)
-    proj, norm = lax.psum((proj_part, norm_part), SCAN_AXES)
+    local = jnp.concatenate([masked, template], axis=2)
 
-    rows_x = lax.all_gather(masked, "sx", axis=1, tiled=True)
-    wrapped = jnp.concatenate([rows_x, rows_x[:, :, : half * tile_pixels]], axis=2)
-    parts = []
-    for y in range(n_sy):
-        col = y * n_sx + sx
-        row_blocks = lax.dynamic_slice_in_dim(wrapped, col * tile_pixels, half * tile_pixels, 2)
-        col_block = lax.dynamic_slice_in_dim(rows_x, col * tile_pixels, tile_pixels, 2)
-        parts.append(
-            jnp.einsum("snp,snq->spq", row_blocks, col_block, preferred_element_type=jnp.float32)
+    def column_blocks(one, gather_axis, reduce_axis, n_group):
+        rows_all = lax.all_gather(one, gather_axis, axis=1, tiled=True)
+        rows = rows_all[:, :, :width]
+        tpl = rows_all[:, :, width:]
+        wrapped = jnp.concatenate([rows, rows[:, :, : half * tile_pixels]], axis=2)
+        norm = jnp.einsum("snt,snu->stu", tpl, tpl, preferred_element_type=jnp.float32)
+        norm = jnp.pad(norm, ((0, 0), (0, 0), (0, col_width)))
+        parts = []
+        for g in range(n_group):
+            col = g * n_sx + sx if reduce_axis == "sy" else sy * n_sx + g
+            row_blocks = lax.dynamic_slice_in_dim(wrapped, col * tile_pixels, half * tile_pixels, 2)
+            col_block = lax.dynamic_slice_in_dim(rows, col * tile_pixels, tile_pixels, 2)
+            gram = jnp.einsum("snp,snq->spq", row_blocks, col_block, preferred_element_type=jnp.float32)
+            proj = jnp.einsum("snp,snt->spt", row_blocks, tpl, preferred_element_type=jnp.float32)
+            parts.append(jnp.concatenate([jnp.concatenate([gram, proj], axis=2), norm], axis=1))
+        summed = lax.psum_scatter(jnp.stack(parts), reduce_axis, scatter_dimension=0, tiled=False)
+        gram = summed[:, : half * tile_pixels, :col_width]
+        proj = jnp.swapaxes(summed[:, : half * tile_pixels, col_width:], 1, 2)
+        normal = summed[:, half * tile_pixels :, :template_cols]
+        normal = normal + jnp.eye(template_cols, dtype=jnp.float32)[None, :, :]
+        factor = jnp.linalg.cholesky(normal)
+        whitened = jax.scipy.linalg.solve_triangular(factor, proj, lower=True)
+        correction = jnp.einsum(
+            "stp,stq->spq", whitened, whitened[:, :, :tile_pixels], precision=lax.Precision.HIGHEST
         )
-    gram_part = lax.psum_scatter(jnp.stack(parts), "sy", scatter_dimension=0, tiled=False)
+        return gram - correction
 
-    normal = norm + jnp.eye(template_cols, dtype=jnp.float32)[None, :, :]
-    factor = jnp.linalg.cholesky(normal)
-    whitened = jax.scipy.linalg.solve_triangular(factor, proj, lower=True)
-    w_wrapped = jnp.concatenate([whitened, whitened[:, :, : half * tile_pixels]], axis=2)
-    w_rows = lax.dynamic_slice_in_dim(w_wrapped, scan_index * tile_pixels, half * tile_pixels, 2)
-    w_col = lax.dynamic_slice_in_dim(whitened, scan_index * tile_pixels, tile_pixels, 2)
-    correction = jnp.einsum("stp,stq->spq", w_rows, w_col, precision=lax.Precision.HIGHEST)
-    own = (gram_part - correction).reshape(scan_count, half, tile_pixels, col_width)
+    own = jnp.concatenate(
+        [
+            column_blocks(local[0:1], "sx", "sy", n_sy),
+            column_blocks(local[1:2], "sy", "sx", n_sx),
+        ],
+        axis=0,
+    ).reshape(scan_count, half, tile_pixels, col_width)
 
     received = []
     for d in range(k_tiles - half, 0, -1):

time: 297 us -> 307 us (1.034)
  blocking collectives: 59.9 us -> 0 us
  waiting for transfers between devices: 119 us -> 176 us
  other arithmetic: 19.7 us -> 38 us
  local copies, waits for them, and re-layouts: 23.8 us -> 34.1 us
  starting transfers between devices: 32.7 us -> 22.5 us
  matrix products: 26 us -> 21.8 us
    psum x1 -> x0, blocking collectives: 59.9 us -> none  [per_device(): proj, norm = lax.psum((proj_part, norm_part), SCAN_AXES)]
    reduce_scatter x1 -> x2, waiting for transfers between devices: 0.02 us -> 47.5 us  [column_blocks(): lax.psum_scatter(jnp.stack(parts), reduce_axis, scatter_dimension=0, tile...]
    all_to_all x1, starting transfers between devices: 20.8 us -> 4.87 us  [per_device(): lax.all_to_all(send_rows, 'tile', split_axis=0, concat_axis=0, tiled=True)]
    another operation x10 -> x18, other arithmetic: 13.7 us -> 27.7 us  [the longest x4 6.03 us: per_device(): factor = jnp.linalg.cholesky(normal)]
    ppermute x7, starting transfers between devices: 6.44 us -> 12.1 us  [per_device(): received.append(lax.ppermute(block, SCAN_AXES, perm))]
    dot_general x7 -> x20, matrix products: 17.5 us -> 12.5 us  [the longest x8 4.56 us: column_blocks(): jnp.einsum('snp,snq->spq', row_blocks, col_block, preferred_element_type=...]
    all_gather x1 -> x2, waiting for transfers between devices: 84.5 us -> 89.1 us  [column_blocks(): rows_all = lax.all_gather(one, gather_axis, axis=1, tiled=True)]
    concatenate x1 -> x2, local copies, waits for them, and re-layouts: 0.04 us -> 4.41 us  [the longest x1 4.05 us: per_device(): local = jnp.concatenate([masked, template], axis=2)]
  transfers between devices with their start and end apart: 12 -> 13, of which waited for: 7 -> 7; matrix products, arithmetic and copies ran while one was open for 16% -> 20% of each run, Pallas kernels for 0% -> 0%
where the time goes in v2:
time: 307 us; the launch traced here: 306 us
  waiting for transfers between devices  176 us (57%)
  other arithmetic  38 us (12%)
  local copies, waits for them, and re-layouts  34.1 us (11%)
  starting transfers between devices  22.5 us (7%)
  matrix products  21.8 us (7%)
  between operations  13.7 us (4%)
    all_gather x2, waiting for transfers between devices, column_blocks(): rows_all = lax.all_gather(one, gather_axis, axis=1, tiled=True)  89.1 us
    reduce_scatter x2, waiting for transfers between devices, column_blocks(): lax.psum_scatter(jnp.stack(parts), reduce_axis, scatter_dimension=0, tile...  47.5 us
    all_to_all x1, waiting for transfers between devices, per_device(): lax.all_to_all(send_rows, 'tile', split_axis=0, concat_axis=0, tiled=True)  26.1 us
    ppermute x7, waiting for transfers between devices, per_device(): received.append(lax.ppermute(block, SCAN_AXES, perm))  12.3 us
    ppermute x7, starting transfers between devices, per_device(): received.append(lax.ppermute(block, SCAN_AXES, perm))  12.1 us
    unnamed x31, local copies, waits for them, and re-layouts  11 us
    another operation x4, other arithmetic  9.76 us
    another operation x6, other arithmetic, column_blocks(): factor = jnp.linalg.cholesky(normal)  7.24 us
  transfers between devices with their start and end apart: 13, of which 7 were waited for; matrix products, arithmetic and copies ran while one was open for 20% of the time, Pallas kernels for 0%

profile of v2, /device:TPU:1, one launch (start us, length us, event | category | flops | bytes accessed | tf_op | source)
XLA Modules:
  0.0 305.9 jit_solution(3156022006981305870)
XLA Ops:
  9.6 3.1 %broadcast_select_fusion = bf16[2,256,2048]{2,1,0:T(8,128)(2,1)} fusion(bf16[2,256,2048]{2,1,0:T(8,128)(2,1)} %param.9, pred[2,256]{1,0:T(4,128)(4,1)S(1)} %broadcast_compare_fusion.1), kind=kLoop, calls=%fused_computation.58 | loop fusion | flops 1048576 | bytes 4194816 | tf_op jit(solution)/shard_map/jit(_where)/select_n | solution.py:48
  13.4 4.1 %concatenate.72 = bf16[2,256,2080]{2,1,0:T(8,128)(2,1)S(1)} concatenate(bf16[2,256,2048]{2,1,0:T(8,128)(2,1)} %broadcast_select_fusion, bf16[2,256,1]{2,1,0:T(8,128)(2,1)S(1)} %get-tuple-element.41, bf16[2,256,1]{2,1,0:T(8,128)(2,1)S(1)} %get-tuple-element.40, bf16[2,256,1]{2,1,0:T(8,128)(2,1)S(1)} %get-tuple-element.39, bf16[2,256,1]{2,1,0:T(8,128)(2,1)S(1)} %get-tuple-element.38, ...), dimensions={2} | concatenate | bytes 4259840 | tf_op jit(solution)/shard_map/concatenate | solution.py:50
  19.8 52.7 %all-gather.3.cloned.1.call-done = bf16[1,1024,2080]{2,1,0:T(8,128)(2,1)} async-done(((bf16[1,256,2080]{2,1,0:T(8,128)(2,1)}), bf16[1,1024,2080]{2,1,0:T(8,128)(2,1)}) %all-gather.3.cloned.1.call-update) | async-done | bytes 4259856 | tf_op jit(solution)/shard_map/all_gather | solution.py:53
  72.6 2.6 slice.118
  77.7 4.1 %fusion.13 = (bf16[1024,1152]{1,0:T(8,128)(2,1)S(1)}, bf16[1024,1152]{1,0:T(8,128)(2,1)S(1)}, bf16[1024,1152]{1,0:T(8,128)(2,1)S(1)}, bf16[1024,1152]{1,0:T(8,128)(2,1)S(1)}) fusion(s32[]{:T(128)S(6)} %select_n.181, bf16[1,1024,2048]{2,1,0:T(8,128)(2,1)S(1)} %slice.118, bf16[1,1024,1152]{2,1,0:T(8,128)(2,1)S(1)} %slice-done.1, s32[]{:T(128)S(6)} %select_n.183, ...), kind=kLoop, calls=%fused_computation.45 | loop fusion | flops 18874368 | bytes 15990800 | tf_op jit(solution)/shard_map/reshape.17
  88.7 36.4 %all-gather.5.cloned.1.call-done = bf16[1,1024,2080]{2,1,0:T(8,128)(2,1)} async-done(((bf16[1,256,2080]{2,1,0:T(8,128)(2,1)}), bf16[1,1024,2080]{2,1,0:T(8,128)(2,1)}) %all-gather.5.cloned.1.call-update) | async-done | bytes 4259856 | tf_op jit(solution)/shard_map/all_gather | solution.py:53
  125.0 2.6 slice.126
  130.2 4.1 %fusion.5 = (bf16[1024,1152]{1,0:T(8,128)(2,1)S(1)}, bf16[1024,1152]{1,0:T(8,128)(2,1)S(1)}, bf16[1024,1152]{1,0:T(8,128)(2,1)S(1)}, bf16[1024,1152]{1,0:T(8,128)(2,1)S(1)}) fusion(s32[]{:T(128)S(6)} %select_n.189, bf16[1,1024,2048]{2,1,0:T(8,128)(2,1)S(1)} %slice.126, bf16[1,1024,1152]{2,1,0:T(8,128)(2,1)S(1)} %slice-done, s32[]{:T(128)S(6)} %select_n.191, ...), kind=kLoop, calls=%fused_computation.37 | loop fusion | flops 18874368 | bytes 15990800 | tf_op jit(solution)/shard_map/reshape.47
  144.7 5.3 %all-to-all-start.1 = ((s32[8,4,2]{1,2,0:T(2,128)}), s32[8,4,2]{1,2,0:T(2,128)S(1)}, u32[]{:S(2)}, u32[]{:S(2)}) async-start(s32[8,4,2]{1,2,0:T(2,128)} %copy.87), calls=%async_computation.3 | async-start | bytes 16384 | tf_op jit(solution)/shard_map/all_to_all | solution.py:113
  150.0 17.4 %reduce-scatter.3.cloned.1.call-done = f32[1,1,1184,160]{2,3,1,0:T(8,128)} async-done(((f32[4,1,1184,160]{2,3,1,0:T(8,128)}), f32[1,1,1184,160]{2,3,1,0:T(8,128)}) %reduce-scatter.3.cloned.1.call-update) | async-done | bytes 757776 | tf_op jit(solution)/shard_map/reduce_scatter | solution.py:67
  168.9 2.9 custom-call.8
  173.2 2.4 custom-call.9
  178.6 30.1 %reduce-scatter.5.cloned.1.call-done = f32[1,1,1184,160]{2,3,1,0:T(8,128)} async-done(((f32[4,1,1184,160]{2,3,1,0:T(8,128)}), f32[1,1,1184,160]{2,3,1,0:T(8,128)}) %reduce-scatter.5.cloned.1.call-update) | async-done | bytes 757776 | tf_op jit(solution)/shard_map/reduce_scatter | solution.py:67
  210.3 2.9 custom-call.10
  214.6 2.4 custom-call.11
  222.3 2.8 collective-permute-start.1
  227.0 4.0 %collective-permute-start.4 = (f32[2,128,128]{2,1,0:T(8,128)S(1)}, f32[2,128,128]{2,1,0:T(8,128)S(1)}, u32[]{:S(2)}, u32[]{:S(2)}) collective-permute-start(f32[2,128,128]{2,1,0:T(8,128)S(1)} %bitcast.254), channel_id=1, source_target_pairs={{0,24},{8,32},{16,40},{24,48},{32,56},{40,64},{48,72},{56,80},{64,... | collective-permute-start | bytes 393224 | tf_op jit(solution)/shard_map/ppermute | solution.py:91
  234.5 11.3 %collective-permute-done.3 = f32[2,128,128]{2,1,0:T(8,128)S(1)} collective-permute-done((f32[2,128,128]{2,1,0:T(8,128)S(1)}, f32[2,128,128]{2,1,0:T(8,128)S(1)}, u32[]{:S(2)}, u32[]{:S(2)}) %collective-permute-start.3) | collective-permute-done | bytes 131104 | tf_op jit(solution)/shard_map/ppermute | solution.py:91
  248.4 4.3 %copy.83 = f32[8,4,128,128]{3,1,2,0:T(4,128)} copy(f32[8,4,128,128]{3,2,1,0:T(8,128)} %bitcast.239) | data formatting | bytes 4194304 | tf_op jit(solution)/shard_map/reshape | solution.py:109
  252.7 4.9 %all-to-all-start = ((f32[8,4,128,128]{3,1,2,0:T(4,128)}), f32[8,4,128,128]{3,1,2,0:T(4,128)S(1)}, u32[]{:S(2)}, u32[]{:S(2)}) async-start(f32[8,4,128,128]{3,1,2,0:T(4,128)} %copy.83), calls=%async_computation.2 | async-start | bytes 4194304 | tf_op jit(solution)/shard_map/all_to_all | solution.py:112
  257.7 26.1 %all-to-all-done = f32[8,4,128,128]{3,1,2,0:T(4,128)S(1)} async-done(((f32[8,4,128,128]{3,1,2,0:T(4,128)}), f32[8,4,128,128]{3,1,2,0:T(4,128)S(1)}, u32[]{:S(2)}, u32[]{:S(2)}) %all-to-all-start) | async-done | bytes 2097184 | tf_op jit(solution)/shard_map/all_to_all | solution.py:112
  284.4 6.9 %convolution_bitcast_fusion = f32[16,128,8,128]{3,0,2,1:T(8,128)S(1)} fusion(f32[32,128,128,1]{2,0,3,1:T(8,128)S(1)} %bitcast.240, f32[32,8]{0,1:T(8,128)S(1)} %fusion.72, f32[32,16]{0,1:T(8,128)S(1)} %fusion.63), kind=kOutput, calls=%fused_computation.21 | convolution fusion | flops 805310464 | bytes 10488832 | tf_op jit(solution)/shard_map/irkc,ixky->rxcy/dot_general | solution.py:121
  291.2 2.7 copy.89
  293.9 5.5 %copy.106 = f32[256,8,8,128]{3,1,2,0:T(8,128)} copy(f32[256,8,8,128]{3,2,1,0:T(8,128)S(1)} %bitcast.234) | data formatting | bytes 16777216
  (129 shorter events, 50.7 us)
Async XLA Ops:
  6.5 66.0 %all-gather.3.cloned.1.call-start = ((), (), s32[]{:S(2)}) async-start(), calls=%async_computation.4 | async-start | bytes 5570560 | tf_op jit(solution)/shard_map/all_gather | solution.py:53
  19.0 106.0 %all-gather.5.cloned.1.call-start = ((), (), s32[]{:S(2)}) async-start(), calls=%async_computation.6 | async-start | bytes 5570560 | tf_op jit(solution)/shard_map/all_gather | solution.py:53
  19.8 147.6 %reduce-scatter.3.cloned.1.call-start = ((), (), s32[]{:S(2)}) async-start(), calls=%async_computation.5 | async-start | bytes 4096000 | tf_op jit(solution)/shard_map/reduce_scatter | solution.py:67
  72.6 5.1 %slice-start.1 = ((bf16[1,1024,2080]{2,1,0:T(8,128)(2,1)}), bf16[1,1024,1152]{2,1,0:T(8,128)(2,1)S(1)}, s32[]{:S(2)}) async-start(bf16[1,1024,2080]{2,1,0:T(8,128)(2,1)} %all-gather.3.cloned.1.call-done), calls=%async_computation.9 | async-start | bytes 4718592 | tf_op jit(solution)/shard_map/slice | solution.py:56
  75.2 2.3 copy-start.1
  88.4 120.4 %reduce-scatter.5.cloned.1.call-start = ((), (), s32[]{:S(2)}) async-start(), calls=%async_computation.7 | async-start | bytes 4096000 | tf_op jit(solution)/shard_map/reduce_scatter | solution.py:67
  125.0 5.1 %slice-start = ((bf16[1,1024,2080]{2,1,0:T(8,128)(2,1)}), bf16[1,1024,1152]{2,1,0:T(8,128)(2,1)S(1)}, s32[]{:S(2)}) async-start(bf16[1,1024,2080]{2,1,0:T(8,128)(2,1)} %all-gather.5.cloned.1.call-done), calls=%async_computation.8 | async-start | bytes 4718592 | tf_op jit(solution)/shard_map/slice | solution.py:56
  127.7 2.3 copy-start
  138.8 2.0 copy-start.2
  138.9 2.6 copy-start.3
  144.7 108.0 %all-to-all-start.1 = ((s32[8,4,2]{1,2,0:T(2,128)}), s32[8,4,2]{1,2,0:T(2,128)S(1)}, u32[]{:S(2)}, u32[]{:S(2)}) async-start(s32[8,4,2]{1,2,0:T(2,128)} %copy.87), calls=%async_computation.3 | async-start | bytes 16384 | tf_op jit(solution)/shard_map/all_to_all | solution.py:113
  220.6 10.6 %collective-permute-start = (f32[2,128,128]{2,1,0:T(8,128)S(1)}, f32[2,128,128]{2,1,0:T(8,128)S(1)}, u32[]{:S(2)}, u32[]{:S(2)}) collective-permute-start(f32[2,128,128]{2,1,0:T(8,128)S(1)} %bitcast.257), channel_id=1, source_target_pairs={{0,56},{8,64},{16,72},{24,80},{32,88},{40,96},{48,104},{56,112},{6... | collective-permute-start | bytes 393224 | tf_op jit(solution)/shard_map/ppermute | solution.py:91
  222.3 9.1 %collective-permute-start.1 = (f32[2,128,128]{2,1,0:T(8,128)S(1)}, f32[2,128,128]{2,1,0:T(8,128)S(1)}, u32[]{:S(2)}, u32[]{:S(2)}) collective-permute-start(f32[2,128,128]{2,1,0:T(8,128)S(1)} %bitcast.256), channel_id=1, source_target_pairs={{0,48},{8,56},{16,64},{24,72},{32,80},{40,88},{48,96},{56,104},{64... | collective-permute-start | bytes 393224 | tf_op jit(solution)/shard_map/ppermute | solution.py:91
  225.2 9.3 %collective-permute-start.2 = (f32[2,128,128]{2,1,0:T(8,128)S(1)}, f32[2,128,128]{2,1,0:T(8,128)S(1)}, u32[]{:S(2)}, u32[]{:S(2)}) collective-permute-start(f32[2,128,128]{2,1,0:T(8,128)S(1)} %bitcast.252), channel_id=1, source_target_pairs={{0,40},{8,48},{16,56},{24,64},{32,72},{40,80},{48,88},{56,96},{64,... | collective-permute-start | bytes 393224 | tf_op jit(solution)/shard_map/ppermute | solution.py:91
  225.4 20.5 %collective-permute-start.3 = (f32[2,128,128]{2,1,0:T(8,128)S(1)}, f32[2,128,128]{2,1,0:T(8,128)S(1)}, u32[]{:S(2)}, u32[]{:S(2)}) collective-permute-start(f32[2,128,128]{2,1,0:T(8,128)S(1)} %bitcast.253), channel_id=1, source_target_pairs={{0,32},{8,40},{16,48},{24,56},{32,64},{40,72},{48,80},{56,88},{64,... | collective-permute-start | bytes 393224 | tf_op jit(solution)/shard_map/ppermute | solution.py:91
  227.0 18.9 %collective-permute-start.4 = (f32[2,128,128]{2,1,0:T(8,128)S(1)}, f32[2,128,128]{2,1,0:T(8,128)S(1)}, u32[]{:S(2)}, u32[]{:S(2)}) collective-permute-start(f32[2,128,128]{2,1,0:T(8,128)S(1)} %bitcast.254), channel_id=1, source_target_pairs={{0,24},{8,32},{16,40},{24,48},{32,56},{40,64},{48,72},{56,80},{64,... | collective-permute-start | bytes 393224 | tf_op jit(solution)/shard_map/ppermute | solution.py:91
  231.2 14.6 %collective-permute-start.5 = (f32[2,128,128]{2,1,0:T(8,128)S(1)}, f32[2,128,128]{2,1,0:T(8,128)S(1)}, u32[]{:S(2)}, u32[]{:S(2)}) collective-permute-start(f32[2,128,128]{2,1,0:T(8,128)S(1)} %bitcast.255), channel_id=1, source_target_pairs={{0,16},{8,24},{16,32},{24,40},{32,48},{40,56},{48,64},{56,72},{64,... | collective-permute-start | bytes 393224 | tf_op jit(solution)/shard_map/ppermute | solution.py:91
  231.4 14.6 %collective-permute-start.6 = (f32[2,128,128]{2,1,0:T(8,128)S(1)}, f32[2,128,128]{2,1,0:T(8,128)S(1)}, u32[]{:S(2)}, u32[]{:S(2)}) collective-permute-start(f32[2,128,128]{2,1,0:T(8,128)S(1)} %bitcast.251), channel_id=1, source_target_pairs={{0,8},{8,16},{16,24},{24,32},{32,40},{40,48},{48,56},{56,64},{64,7... | collective-permute-start | bytes 393224 | tf_op jit(solution)/shard_map/ppermute | solution.py:91
  252.7 31.1 %all-to-all-start = ((f32[8,4,128,128]{3,1,2,0:T(4,128)}), f32[8,4,128,128]{3,1,2,0:T(4,128)S(1)}, u32[]{:S(2)}, u32[]{:S(2)}) async-start(f32[8,4,128,128]{3,1,2,0:T(4,128)} %copy.83), calls=%async_computation.2 | async-start | bytes 4194304 | tf_op jit(solution)/shard_map/all_to_all | solution.py:112
Sparse Core Ops, SparseCore 0:
  19.1 53.3 all-gather.2
  74.2 50.7 all-gather.4
  127.5 39.8 reduce-scatter.2
  169.6 39.1 reduce-scatter.4

commit v3 on v2

--- a/solution.py
+++ b/solution.py
@@ -49,22 +49,40 @@
     template = build_templates(ground_bin, position, lengths, degrees)
     local = jnp.concatenate([masked, template], axis=2)
 
-    def column_blocks(one, gather_axis, reduce_axis, n_group):
-        rows_all = lax.all_gather(one, gather_axis, axis=1, tiled=True)
+    def shifted(x, axis, n, d):
+        return lax.ppermute(x, axis, [(i, (i + d) % n) for i in range(n)])
+
+    def column_blocks(one, gather_axis, n_gather, reduce_axis, n_reduce, reduce_index):
+        rows_all = jnp.concatenate(
+            [one] + [shifted(one, gather_axis, n_gather, d) for d in range(1, n_gather)], axis=1
+        )
         rows = rows_all[:, :, :width]
         tpl = rows_all[:, :, width:]
-        wrapped = jnp.concatenate([rows, rows[:, :, : half * tile_pixels]], axis=2)
+        grid = rows.reshape(1, rows.shape[1], n_sy, n_sx, tile_pixels)
+        if reduce_axis == "sy":
+            cols = lax.dynamic_index_in_dim(grid, sx, 3, keepdims=False)
+            firsts = [g * n_sx + sx for g in range(n_reduce)]
+        else:
+            cols = lax.dynamic_index_in_dim(grid, sy, 2, keepdims=False)
+            firsts = [sy * n_sx + g for g in range(n_reduce)]
+        grams = jnp.einsum("snp,sngq->sgpq", rows, cols, preferred_element_type=jnp.float32)
+        projs = jnp.einsum("snp,snt->spt", rows, tpl, preferred_element_type=jnp.float32)
         norm = jnp.einsum("snt,snu->stu", tpl, tpl, preferred_element_type=jnp.float32)
         norm = jnp.pad(norm, ((0, 0), (0, 0), (0, col_width)))
-        parts = []
-        for g in range(n_group):
-            col = g * n_sx + sx if reduce_axis == "sy" else sy * n_sx + g
-            row_blocks = lax.dynamic_slice_in_dim(wrapped, col * tile_pixels, half * tile_pixels, 2)
-            col_block = lax.dynamic_slice_in_dim(rows, col * tile_pixels, tile_pixels, 2)
-            gram = jnp.einsum("snp,snq->spq", row_blocks, col_block, preferred_element_type=jnp.float32)
-            proj = jnp.einsum("snp,snt->spt", row_blocks, tpl, preferred_element_type=jnp.float32)
-            parts.append(jnp.concatenate([jnp.concatenate([gram, proj], axis=2), norm], axis=1))
-        summed = lax.psum_scatter(jnp.stack(parts), reduce_axis, scatter_dimension=0, tiled=False)
+        both = jnp.concatenate(
+            [grams, jnp.broadcast_to(projs[:, None], (1, n_reduce) + projs.shape[1:])], axis=3
+        )
+        both = jnp.concatenate([both, both[:, :, : half * tile_pixels]], axis=2)
+        payloads = []
+        for g in range(n_reduce):
+            slab = lax.dynamic_slice_in_dim(both[:, g], firsts[g] * tile_pixels, half * tile_pixels, 1)
+            payloads.append(jnp.concatenate([slab, norm], axis=1))
+        payloads = jnp.stack(payloads)
+        summed = None
+        for d in range(n_reduce):
+            part = lax.dynamic_index_in_dim(payloads, (reduce_index + d) % n_reduce, 0, keepdims=False)
+            part = part if d == 0 else shifted(part, reduce_axis, n_reduce, d)
+            summed = part if summed is None else summed + part
         gram = summed[:, : half * tile_pixels, :col_width]
         proj = jnp.swapaxes(summed[:, : half * tile_pixels, col_width:], 1, 2)
         normal = summed[:, half * tile_pixels :, :template_cols]
@@ -78,8 +96,8 @@
 
     own = jnp.concatenate(
         [
-            column_blocks(local[0:1], "sx", "sy", n_sy),
-            column_blocks(local[1:2], "sy", "sx", n_sx),
+            column_blocks(local[0:1], "sx", n_sx, "sy", n_sy, sy),
+            column_blocks(local[1:2], "sy", n_sy, "sx", n_sx, sx),
         ],
         axis=0,
     ).reshape(scan_count, half, tile_pixels, col_width)

time: 307 us -> 289 us (0.941); the launches traced: 306 us -> 284 us
  waiting for transfers between devices: 176 us -> 92.5 us
  local copies, waits for them, and re-layouts: 34.1 us -> 82.4 us
  starting transfers between devices: 22.5 us -> 44.7 us
  between operations: 13.7 us -> 1.21 us
  other arithmetic: 38 us -> 42.4 us
    all_gather x2 -> x0, waiting for transfers between devices: 89.1 us -> none  [column_blocks(): rows_all = lax.all_gather(one, gather_axis, axis=1, tiled=True)]
    ppermute x0 -> x12, waiting for transfers between devices: none -> 57 us  [shifted(): return lax.ppermute(x, axis, [(i, (i + d) % n) for i in range(n)])]
    reduce_scatter x2 -> x0, waiting for transfers between devices: 47.5 us -> none  [column_blocks(): lax.psum_scatter(jnp.stack(parts), reduce_axis, scatter_dimension=0, tile...]
    ppermute x0 -> x12, starting transfers between devices: none -> 16.9 us  [shifted(): return lax.ppermute(x, axis, [(i, (i + d) % n) for i in range(n)])]
    reshape x0 -> x2, local copies, waits for them, and re-layouts: none -> 15.4 us  [column_blocks(): grid = rows.reshape(1, rows.shape[1], n_sy, n_sx, tile_pixels)]
    concatenate x1 -> x5, other arithmetic: 0.08 us -> 15.2 us  [the longest x2 13.8 us: column_blocks(): jnp.concatenate([one] + [shifted(one, gather_axis, n_gather, d) for d in...]
    ppermute x0 -> x6, local copies, waits for them, and re-layouts: none -> 13.4 us  [shifted(): return lax.ppermute(x, axis, [(i, (i + d) % n) for i in range(n)])]
    another operation x8, other arithmetic: 14.3 us -> 4.06 us
  transfers between devices with their start and end apart: 13 -> 21, of which waited for: 7 -> 6; matrix products, arithmetic and copies ran while one was open for 20% -> 39% of each run, Pallas kernels for 0% -> 0%
where the time goes in v3:
time: 289 us; the launch traced here: 284 us
  waiting for transfers between devices  92.5 us (32%)
  local copies, waits for them, and re-layouts  82.4 us (29%)
  starting transfers between devices  44.7 us (15%)
  other arithmetic  42.4 us (15%)
  matrix products  20.8 us (7%)
    ppermute x12, waiting for transfers between devices, shifted(): return lax.ppermute(x, axis, [(i, (i + d) % n) for i in range(n)])  57 us
    all_to_all x1, waiting for transfers between devices, per_device(): lax.all_to_all(send_rows, 'tile', split_axis=0, concat_axis=0, tiled=True)  25.8 us
    ppermute x12, starting transfers between devices, shifted(): return lax.ppermute(x, axis, [(i, (i + d) % n) for i in range(n)])  16.9 us
    reshape x2, local copies, waits for them, and re-layouts, column_blocks(): grid = rows.reshape(1, rows.shape[1], n_sy, n_sx, tile_pixels)  15.4 us
    ppermute x7, starting transfers between devices, per_device(): received.append(lax.ppermute(block, SCAN_AXES, perm))  14.5 us
    concatenate x2, other arithmetic, column_blocks(): jnp.concatenate([one] + [shifted(one, gather_axis, n_gather, d) for d in...  13.8 us
    unnamed x49, local copies, waits for them, and re-layouts  13.5 us
    ppermute x6, local copies, waits for them, and re-layouts, shifted(): return lax.ppermute(x, axis, [(i, (i + d) % n) for i in range(n)])  13.4 us
  transfers between devices with their start and end apart: 21, of which 6 were waited for; matrix products, arithmetic and copies ran while one was open for 39% of the time, Pallas kernels for 0%

profile of v3, /device:TPU:1, one launch (start us, length us, event | category | flops | bytes accessed | tf_op | source)
XLA Modules:
  0.0 284.0 jit_solution(17808145630285051869)
XLA Ops:
  4.9 4.1 %concatenate.60 = bf16[2,256,2080]{2,1,0:T(8,128)(2,1)} concatenate(bf16[2,256,2048]{2,1,0:T(8,128)(2,1)S(1)} %broadcast_select_fusion, bf16[2,256,1]{2,1,0:T(8,128)(2,1)S(1)} %get-tuple-element.47, bf16[2,256,1]{2,1,0:T(8,128)(2,1)S(1)} %get-tuple-element.46, bf16[2,256,1]{2,1,0:T(8,128)(2,1)S(1)} %get-tuple-element.45, bf16[2,256,1]{2,1,0:T(8,128)(2,1)S(1)} %get-tuple-element.44, ...), dimensions={2} | concatenate | bytes 4259840 | tf_op jit(solution)/shard_map/concatenate | solution.py:50
  12.1 3.6 %collective-permute-start.8 = (bf16[1,256,2080]{1,2,0:T(8,128)(2,1)}, bf16[1,256,2080]{1,2,0:T(8,128)(2,1)S(1)}, u32[]{:S(2)}, u32[]{:S(2)}) collective-permute-start(bf16[1,256,2080]{1,2,0:T(8,128)(2,1)} %copy.118), channel_id=1, source_target_pairs={{0,96},{32,0},{64,32},{96,64},{1,97},{33,1},{65,33},{97,65},{2,98}... | collective-permute-start | bytes 3194888 | tf_op jit(solution)/shard_map/ppermute | solution.py:53
  24.8 7.4 %all-to-all-start.1 = ((s32[8,4,2]{1,2,0:T(2,128)}), s32[8,4,2]{1,2,0:T(2,128)S(1)}, u32[]{:S(2)}, u32[]{:S(2)}) async-start(s32[8,4,2]{1,2,0:T(2,128)} %copy.143), calls=%async_computation.1 | async-start | bytes 16384 | tf_op jit(solution)/shard_map/all_to_all | solution.py:131
  32.2 28.7 %collective-permute-done.8 = bf16[1,256,2080]{1,2,0:T(8,128)(2,1)S(1)} collective-permute-done((bf16[1,256,2080]{1,2,0:T(8,128)(2,1)}, bf16[1,256,2080]{1,2,0:T(8,128)(2,1)S(1)}, u32[]{:S(2)}, u32[]{:S(2)}) %collective-permute-start.8) | collective-permute-done | bytes 1064992 | tf_op jit(solution)/shard_map/ppermute | solution.py:53
  68.7 7.0 %pad_maximum_fusion.3 = bf16[1,1024,2080]{2,1,0:T(8,128)(2,1)S(1)} fusion(bf16[1,256,2080]{2,1,0:T(8,128)(2,1)S(1)} %copy.123, bf16[1,256,2080]{2,1,0:T(8,128)(2,1)} %copy.122, bf16[1,256,2080]{2,1,0:T(8,128)(2,1)} %copy.121, bf16[1,256,2080]{2,1,0:T(8,128)(2,1)S(1)} %get-tuple-element.24), kind=kLoop, calls=%fused_computation.8 | loop fusion | flops 17039360 | bytes 8519680 | tf_op jit(solution)/shard_map/concatenate | solution.py:56
  92.6 6.7 %pad_maximum_fusion.2 = bf16[1,1024,2080]{2,1,0:T(8,128)(2,1)S(1)} fusion(bf16[1,256,2080]{2,1,0:T(8,128)(2,1)S(1)} %copy-done.5, bf16[1,256,2080]{2,1,0:T(8,128)(2,1)S(1)} %copy-done.6, bf16[1,256,2080]{2,1,0:T(8,128)(2,1)S(1)} %copy-done.7, bf16[1,256,2080]{2,1,0:T(8,128)(2,1)S(1)} %get-tuple-element.23), kind=kLoop, calls=%fused_computation.7 | loop fusion | flops 17039360 | bytes 8519680 | tf_op jit(solution)/shard_map/concatenate | solution.py:56
  104.0 7.7 %reshape.1318 = bf16[1,1024,4,4,128]{4,3,2,1,0:T(4,128)(2,1)} reshape(bf16[1,1024,2048]{2,1,0:T(8,128)(2,1)} %slice.158) | data formatting | bytes 8388608 | tf_op jit(solution)/shard_map/reshape | solution.py:61
  114.1 4.6 %fusion.13 = f32[1,4,2048,128]{2,3,1,0:T(8,128)S(1)} fusion(bf16[1,1024,1,4,128]{1,4,3,2,0:T(8,128)(2,1)S(1)} %copy.124, bf16[1,1024,2080]{2,1,0:T(8,128)(2,1)} %copy-done.1), kind=kOutput, calls=%fused_computation.20 | convolution fusion | flops 2147483648 | bytes 9437184 | tf_op jit(solution)/shard_map/snp,sngq->sgpq/dot_general | solution.py:68
  127.3 7.7 %reshape.1312 = bf16[1,1024,4,4,128]{4,3,2,1,0:T(4,128)(2,1)} reshape(bf16[1,1024,2048]{2,1,0:T(8,128)(2,1)} %slice.148) | data formatting | bytes 8388608 | tf_op jit(solution)/shard_map/reshape | solution.py:61
  135.0 4.3 %constant_dynamic-slice_fusion.3 = bf16[1,1024,4,1,128]{4,3,2,1,0:T(2,128)(2,1)S(1)} fusion(bf16[1,1024,4,4,128]{4,3,2,1,0:T(4,128)(2,1)} %reshape.1312, s32[]{:T(128)S(6)} %select_n.224), kind=kLoop, calls=%fused_computation.148 | loop fusion | bytes 2097156 | tf_op jit(solution)/shard_map/jit(dynamic_index_in_dim)/dynamic_slice | solution.py:63
  141.9 4.5 %fusion.10 = f32[1,4,2048,128]{2,3,1,0:T(8,128)S(1)} fusion(bf16[1,1024,4,1,128]{1,4,2,3,0:T(8,128)(2,1)S(1)} %copy.111, bf16[1,1024,2080]{2,1,0:T(8,128)(2,1)} %copy-done), kind=kOutput, calls=%fused_computation.19 | convolution fusion | flops 2147483648 | bytes 9437184 | tf_op jit(solution)/shard_map/snp,sngq->sgpq/dot_general | solution.py:68
  150.2 4.8 %collective-permute-start.5 = (f32[1,1184,160]{1,2,0:T(8,128)}, f32[1,1184,160]{1,2,0:T(8,128)S(1)}, u32[]{:S(2)}, u32[]{:S(2)}) collective-permute-start(f32[1,1184,160]{1,2,0:T(8,128)} %get-tuple-element.18), channel_id=1, source_target_pairs={{0,96},{32,0},{64,32},{96,64},{1,97},{33,1},{65,33},{97,65},{2,98}... | collective-permute-start | bytes 2273288 | tf_op jit(solution)/shard_map/ppermute | solution.py:53
  155.8 9.9 %collective-permute-done.9 = f32[1,1184,160]{1,2,0:T(8,128)} collective-permute-done((f32[1,1184,160]{1,2,0:T(8,128)}, f32[1,1184,160]{1,2,0:T(8,128)}, u32[]{:S(2)}, u32[]{:S(2)}) %collective-permute-start.9) | collective-permute-done | bytes 757792 | tf_op jit(solution)/shard_map/ppermute | solution.py:53
  167.8 2.9 %custom-call.10 = f32[1,32,32]{2,1,0:T(8,128)S(1)} custom-call(f32[1,32,32]{2,1,0:T(8,128)S(1)} %fusion.48), custom_call_target="Cholesky" | custom-call | tf_op jit(solution)/shard_map/jit(cholesky)/cholesky | solution.py:90
  175.5 12.3 %collective-permute-done.5 = f32[1,1184,160]{1,2,0:T(8,128)S(1)} collective-permute-done((f32[1,1184,160]{1,2,0:T(8,128)}, f32[1,1184,160]{1,2,0:T(8,128)S(1)}, u32[]{:S(2)}, u32[]{:S(2)}) %collective-permute-start.5) | collective-permute-done | bytes 757792 | tf_op jit(solution)/shard_map/ppermute | solution.py:53
  187.8 6.1 %collective-permute-done.3 = f32[1,1184,160]{1,2,0:T(8,128)} collective-permute-done((f32[1,1184,160]{1,2,0:T(8,128)S(1)}, f32[1,1184,160]{1,2,0:T(8,128)}, u32[]{:S(2)}, u32[]{:S(2)}) %collective-permute-start.3) | collective-permute-done | bytes 757792 | tf_op jit(solution)/shard_map/ppermute | solution.py:53
  209.5 3.7 %collective-permute-start.16 = (f32[2,128,128]{2,1,0:T(8,128)S(1)}, f32[2,128,128]{2,1,0:T(8,128)S(1)}, u32[]{:S(2)}, u32[]{:S(2)}) collective-permute-start(f32[2,128,128]{2,1,0:T(8,128)S(1)} %bitcast.228), channel_id=1, source_target_pairs={{0,24},{8,32},{16,40},{24,48},{32,56},{40,64},{48,72},{56,80},{64,... | collective-permute-start | bytes 393224 | tf_op jit(solution)/shard_map/ppermute | solution.py:109
  214.5 4.9 %collective-permute-start.18 = (f32[2,128,128]{2,1,0:T(8,128)S(1)}, f32[2,128,128]{2,1,0:T(8,128)S(1)}, u32[]{:S(2)}, u32[]{:S(2)}) collective-permute-start(f32[2,128,128]{2,1,0:T(8,128)S(1)} %bitcast.225), channel_id=1, source_target_pairs={{0,8},{8,16},{16,24},{24,32},{32,40},{40,48},{48,56},{56,64},{64,7... | collective-permute-start | bytes 393224 | tf_op jit(solution)/shard_map/ppermute | solution.py:109
  219.5 9.6 %collective-permute-done.15 = f32[2,128,128]{2,1,0:T(8,128)S(1)} collective-permute-done((f32[2,128,128]{2,1,0:T(8,128)S(1)}, f32[2,128,128]{2,1,0:T(8,128)S(1)}, u32[]{:S(2)}, u32[]{:S(2)}) %collective-permute-start.15) | collective-permute-done | bytes 131104 | tf_op jit(solution)/shard_map/ppermute | solution.py:109
  231.6 4.3 %copy.139 = f32[8,4,128,128]{3,1,2,0:T(4,128)} copy(f32[8,4,128,128]{3,2,1,0:T(8,128)} %bitcast.221) | data formatting | bytes 4194304 | tf_op jit(solution)/shard_map/reshape | solution.py:127
  235.9 6.0 %all-to-all-start = ((f32[8,4,128,128]{3,1,2,0:T(4,128)}), f32[8,4,128,128]{3,1,2,0:T(4,128)S(1)}, u32[]{:S(2)}, u32[]{:S(2)}) async-start(f32[8,4,128,128]{3,1,2,0:T(4,128)} %copy.139), calls=%async_computation | async-start | bytes 4194304 | tf_op jit(solution)/shard_map/all_to_all | solution.py:130
  242.1 25.8 %all-to-all-done = f32[8,4,128,128]{3,1,2,0:T(4,128)S(1)} async-done(((f32[8,4,128,128]{3,1,2,0:T(4,128)}), f32[8,4,128,128]{3,1,2,0:T(4,128)S(1)}, u32[]{:S(2)}, u32[]{:S(2)}) %all-to-all-start) | async-done | bytes 2097184 | tf_op jit(solution)/shard_map/all_to_all | solution.py:130
  268.5 6.9 %convolution_bitcast_fusion = f32[16,128,8,128]{3,0,2,1:T(8,128)S(1)} fusion(f32[32,128,128,1]{2,0,3,1:T(8,128)S(1)} %bitcast.222, f32[32,8]{0,1:T(8,128)S(1)} %fusion.52, f32[32,16]{0,1:T(8,128)S(1)} %fusion.51), kind=kOutput, calls=%fused_computation.21 | convolution fusion | flops 805310464 | bytes 10488832 | tf_op jit(solution)/shard_map/irkc,ixky->rxcy/dot_general | solution.py:139
  278.1 5.5 %copy.162 = f32[256,8,8,128]{3,1,2,0:T(8,128)} copy(f32[256,8,8,128]{3,2,1,0:T(8,128)S(1)} %bitcast.216) | data formatting | bytes 16777216
  (177 shorter events, 93.7 us)
Async XLA Ops:
  9.0 12.1 %copy-start.11 = (s32[2,16]{1,0:T(2,128)S(1)}, s32[2,16]{1,0:T(2,128)}, u32[]{:S(2)}) copy-start(s32[2,16]{1,0:T(2,128)} %param.13) | copy-start | bytes 388
  9.0 12.7 %copy-start.12 = (s32[128]{0:T(128)S(1)}, s32[128]{0:T(128)}, u32[]{:S(2)}) copy-start(s32[128]{0:T(128)} %param.14) | copy-start | bytes 1540
  12.1 48.7 %collective-permute-start.8 = (bf16[1,256,2080]{1,2,0:T(8,128)(2,1)}, bf16[1,256,2080]{1,2,0:T(8,128)(2,1)S(1)}, u32[]{:S(2)}, u32[]{:S(2)}) collective-permute-start(bf16[1,256,2080]{1,2,0:T(8,128)(2,1)} %copy.118), channel_id=1, source_target_pairs={{0,96},{32,0},{64,32},{96,64},{1,97},{33,1},{65,33},{97,65},{2,98}... | collective-permute-start | bytes 3194888 | tf_op jit(solution)/shard_map/ppermute | solution.py:53
  15.7 48.3 %collective-permute-start.7 = (bf16[1,256,2080]{1,2,0:T(8,128)(2,1)}, bf16[1,256,2080]{1,2,0:T(8,128)(2,1)}, u32[]{:S(2)}, u32[]{:S(2)}) collective-permute-start(bf16[1,256,2080]{1,2,0:T(8,128)(2,1)} %copy.118), channel_id=1, source_target_pairs={{0,64},{32,96},{64,0},{96,32},{1,65},{33,97},{65,1},{97,33},{2,66}... | collective-permute-start | bytes 3194888 | tf_op jit(solution)/shard_map/ppermute | solution.py:53
  16.0 50.3 %collective-permute-start.6 = (bf16[1,256,2080]{1,2,0:T(8,128)(2,1)}, bf16[1,256,2080]{1,2,0:T(8,128)(2,1)}, u32[]{:S(2)}, u32[]{:S(2)}) collective-permute-start(bf16[1,256,2080]{1,2,0:T(8,128)(2,1)} %copy.118), channel_id=1, source_target_pairs={{0,32},{32,64},{64,96},{96,0},{1,33},{33,65},{65,97},{97,1},{2,34}... | collective-permute-start | bytes 3194888 | tf_op jit(solution)/shard_map/ppermute | solution.py:53
  18.1 62.3 %collective-permute-start.2 = (bf16[1,256,2080]{1,2,0:T(8,128)(2,1)}, bf16[1,256,2080]{1,2,0:T(8,128)(2,1)}, u32[]{:S(2)}, u32[]{:S(2)}) collective-permute-start(bf16[1,256,2080]{1,2,0:T(8,128)(2,1)} %copy.105), channel_id=1, source_target_pairs={{0,24},{8,0},{16,8},{24,16},{1,25},{9,1},{17,9},{25,17},{2,26},{10... | collective-permute-start | bytes 3194888 | tf_op jit(solution)/shard_map/ppermute | solution.py:53
  20.6 62.2 %collective-permute-start.1 = (bf16[1,256,2080]{1,2,0:T(8,128)(2,1)}, bf16[1,256,2080]{1,2,0:T(8,128)(2,1)}, u32[]{:S(2)}, u32[]{:S(2)}) collective-permute-start(bf16[1,256,2080]{1,2,0:T(8,128)(2,1)} %copy.105), channel_id=1, source_target_pairs={{0,16},{8,24},{16,0},{24,8},{1,17},{9,25},{17,1},{25,9},{2,18},{10... | collective-permute-start | bytes 3194888 | tf_op jit(solution)/shard_map/ppermute | solution.py:53
  24.8 211.1 %all-to-all-start.1 = ((s32[8,4,2]{1,2,0:T(2,128)}), s32[8,4,2]{1,2,0:T(2,128)S(1)}, u32[]{:S(2)}, u32[]{:S(2)}) async-start(s32[8,4,2]{1,2,0:T(2,128)} %copy.143), calls=%async_computation.1 | async-start | bytes 16384 | tf_op jit(solution)/shard_map/all_to_all | solution.py:131
  61.8 27.1 %collective-permute-start = (bf16[1,256,2080]{1,2,0:T(8,128)(2,1)}, bf16[1,256,2080]{1,2,0:T(8,128)(2,1)}, u32[]{:S(2)}, u32[]{:S(2)}) collective-permute-start(bf16[1,256,2080]{1,2,0:T(8,128)(2,1)} %copy.105), channel_id=1, source_target_pairs={{0,8},{8,16},{16,24},{24,0},{1,9},{9,17},{17,25},{25,1},{2,10},{10... | collective-permute-start | bytes 3194888 | tf_op jit(solution)/shard_map/ppermute | solution.py:53
  124.0 31.0 %collective-permute-start.11 = (f32[1,1184,160]{1,2,0:T(8,128)}, f32[1,1184,160]{1,2,0:T(8,128)}, u32[]{:S(2)}, u32[]{:S(2)}) collective-permute-start(f32[1,1184,160]{1,2,0:T(8,128)} %get-tuple-element.21), channel_id=1, source_target_pairs={{0,24},{8,0},{16,8},{24,16},{1,25},{9,1},{17,9},{25,17},{2,26},{10... | collective-permute-start | bytes 2273288 | tf_op jit(solution)/shard_map/ppermute | solution.py:53
  126.7 29.1 %collective-permute-start.10 = (f32[1,1184,160]{1,2,0:T(8,128)}, f32[1,1184,160]{1,2,0:T(8,128)}, u32[]{:S(2)}, u32[]{:S(2)}) collective-permute-start(f32[1,1184,160]{1,2,0:T(8,128)} %get-tuple-element.22), channel_id=1, source_target_pairs={{0,16},{8,24},{16,0},{24,8},{1,17},{9,25},{17,1},{25,9},{2,18},{10... | collective-permute-start | bytes 2273288 | tf_op jit(solution)/shard_map/ppermute | solution.py:53
  126.7 39.0 %collective-permute-start.9 = (f32[1,1184,160]{1,2,0:T(8,128)}, f32[1,1184,160]{1,2,0:T(8,128)}, u32[]{:S(2)}, u32[]{:S(2)}) collective-permute-start(f32[1,1184,160]{1,2,0:T(8,128)} %get-tuple-element.20), channel_id=1, source_target_pairs={{0,8},{8,16},{16,24},{24,0},{1,9},{9,17},{17,25},{25,1},{2,10},{10... | collective-permute-start | bytes 2273288 | tf_op jit(solution)/shard_map/ppermute | solution.py:53
  148.6 19.1 %copy-start.4 = (f32[4,1,1184,160]{2,3,1,0:T(8,128)}, f32[4,1,1184,160]{2,3,1,0:T(8,128)S(1)}, u32[]{:S(2)}) copy-start(f32[4,1,1184,160]{2,3,1,0:T(8,128)S(1)} %pad_maximum_fusion.4) | copy-start | bytes 9093124
  150.2 37.6 %collective-permute-start.5 = (f32[1,1184,160]{1,2,0:T(8,128)}, f32[1,1184,160]{1,2,0:T(8,128)S(1)}, u32[]{:S(2)}, u32[]{:S(2)}) collective-permute-start(f32[1,1184,160]{1,2,0:T(8,128)} %get-tuple-element.18), channel_id=1, source_target_pairs={{0,96},{32,0},{64,32},{96,64},{1,97},{33,1},{65,33},{97,65},{2,98}... | collective-permute-start | bytes 2273288 | tf_op jit(solution)/shard_map/ppermute | solution.py:53
  155.0 32.8 %collective-permute-start.4 = (f32[1,1184,160]{1,2,0:T(8,128)}, f32[1,1184,160]{1,2,0:T(8,128)}, u32[]{:S(2)}, u32[]{:S(2)}) collective-permute-start(f32[1,1184,160]{1,2,0:T(8,128)} %get-tuple-element.19), channel_id=1, source_target_pairs={{0,64},{32,96},{64,0},{96,32},{1,65},{33,97},{65,1},{97,33},{2,66}... | collective-permute-start | bytes 2273288 | tf_op jit(solution)/shard_map/ppermute | solution.py:53
  155.0 38.9 %collective-permute-start.3 = (f32[1,1184,160]{1,2,0:T(8,128)S(1)}, f32[1,1184,160]{1,2,0:T(8,128)}, u32[]{:S(2)}, u32[]{:S(2)}) collective-permute-start(f32[1,1184,160]{1,2,0:T(8,128)S(1)} %get-tuple-element.17), channel_id=1, source_target_pairs={{0,32},{32,64},{64,96},{96,0},{1,33},{33,65},{65,97},{97,1},{2,34}... | collective-permute-start | bytes 2273288 | tf_op jit(solution)/shard_map/ppermute | solution.py:53
  204.2 9.3 %collective-permute-start.12 = (f32[2,128,128]{2,1,0:T(8,128)S(1)}, f32[2,128,128]{2,1,0:T(8,128)S(1)}, u32[]{:S(2)}, u32[]{:S(2)}) collective-permute-start(f32[2,128,128]{2,1,0:T(8,128)S(1)} %bitcast.231), channel_id=1, source_target_pairs={{0,56},{8,64},{16,72},{24,80},{32,88},{40,96},{48,104},{56,112},{6... | collective-permute-start | bytes 393224 | tf_op jit(solution)/shard_map/ppermute | solution.py:109
  204.4 10.1 %collective-permute-start.13 = (f32[2,128,128]{2,1,0:T(8,128)S(1)}, f32[2,128,128]{2,1,0:T(8,128)S(1)}, u32[]{:S(2)}, u32[]{:S(2)}) collective-permute-start(f32[2,128,128]{2,1,0:T(8,128)S(1)} %bitcast.230), channel_id=1, source_target_pairs={{0,48},{8,56},{16,64},{24,72},{32,80},{40,88},{48,96},{56,104},{64... | collective-permute-start | bytes 393224 | tf_op jit(solution)/shard_map/ppermute | solution.py:109
  206.2 13.2 %collective-permute-start.14 = (f32[2,128,128]{2,1,0:T(8,128)S(1)}, f32[2,128,128]{2,1,0:T(8,128)S(1)}, u32[]{:S(2)}, u32[]{:S(2)}) collective-permute-start(f32[2,128,128]{2,1,0:T(8,128)S(1)} %bitcast.226), channel_id=1, source_target_pairs={{0,40},{8,48},{16,56},{24,64},{32,72},{40,80},{48,88},{56,96},{64,... | collective-permute-start | bytes 393224 | tf_op jit(solution)/shard_map/ppermute | solution.py:109
  209.0 20.1 %collective-permute-start.15 = (f32[2,128,128]{2,1,0:T(8,128)S(1)}, f32[2,128,128]{2,1,0:T(8,128)S(1)}, u32[]{:S(2)}, u32[]{:S(2)}) collective-permute-start(f32[2,128,128]{2,1,0:T(8,128)S(1)} %bitcast.227), channel_id=1, source_target_pairs={{0,32},{8,40},{16,48},{24,56},{32,64},{40,72},{48,80},{56,88},{64,... | collective-permute-start | bytes 393224 | tf_op jit(solution)/shard_map/ppermute | solution.py:109
  209.5 19.6 %collective-permute-start.16 = (f32[2,128,128]{2,1,0:T(8,128)S(1)}, f32[2,128,128]{2,1,0:T(8,128)S(1)}, u32[]{:S(2)}, u32[]{:S(2)}) collective-permute-start(f32[2,128,128]{2,1,0:T(8,128)S(1)} %bitcast.228), channel_id=1, source_target_pairs={{0,24},{8,32},{16,40},{24,48},{32,56},{40,64},{48,72},{56,80},{64,... | collective-permute-start | bytes 393224 | tf_op jit(solution)/shard_map/ppermute | solution.py:109
  213.5 15.6 %collective-permute-start.17 = (f32[2,128,128]{2,1,0:T(8,128)S(1)}, f32[2,128,128]{2,1,0:T(8,128)S(1)}, u32[]{:S(2)}, u32[]{:S(2)}) collective-permute-start(f32[2,128,128]{2,1,0:T(8,128)S(1)} %bitcast.229), channel_id=1, source_target_pairs={{0,16},{8,24},{16,32},{24,40},{32,48},{40,56},{48,64},{56,72},{64,... | collective-permute-start | bytes 393224 | tf_op jit(solution)/shard_map/ppermute | solution.py:109
  214.5 14.7 %collective-permute-start.18 = (f32[2,128,128]{2,1,0:T(8,128)S(1)}, f32[2,128,128]{2,1,0:T(8,128)S(1)}, u32[]{:S(2)}, u32[]{:S(2)}) collective-permute-start(f32[2,128,128]{2,1,0:T(8,128)S(1)} %bitcast.225), channel_id=1, source_target_pairs={{0,8},{8,16},{16,24},{24,32},{32,40},{40,48},{48,56},{56,64},{64,7... | collective-permute-start | bytes 393224 | tf_op jit(solution)/shard_map/ppermute | solution.py:109
  235.9 32.0 %all-to-all-start = ((f32[8,4,128,128]{3,1,2,0:T(4,128)}), f32[8,4,128,128]{3,1,2,0:T(4,128)S(1)}, u32[]{:S(2)}, u32[]{:S(2)}) async-start(f32[8,4,128,128]{3,1,2,0:T(4,128)} %copy.139), calls=%async_computation | async-start | bytes 4194304 | tf_op jit(solution)/shard_map/all_to_all | solution.py:130
  (10 other events, 26.7 us)

commit v4 on v3

--- a/solution.py
+++ b/solution.py
@@ -47,57 +47,58 @@
     inside = position[None, :] < lengths[:, None]
     masked = jnp.where(inside[:, :, None], pointing, jnp.zeros_like(pointing))
     template = build_templates(ground_bin, position, lengths, degrees)
-    local = jnp.concatenate([masked, template], axis=2)
 
     def shifted(x, axis, n, d):
         return lax.ppermute(x, axis, [(i, (i + d) % n) for i in range(n)])
 
-    def column_blocks(one, gather_axis, n_gather, reduce_axis, n_reduce, reduce_index):
-        rows_all = jnp.concatenate(
-            [one] + [shifted(one, gather_axis, n_gather, d) for d in range(1, n_gather)], axis=1
-        )
-        rows = rows_all[:, :, :width]
-        tpl = rows_all[:, :, width:]
-        grid = rows.reshape(1, rows.shape[1], n_sy, n_sx, tile_pixels)
+    def column_blocks(one, one_tpl, gather_axis, n_gather, reduce_axis, n_reduce, reduce_index):
+        moved = [shifted((one, one_tpl), gather_axis, n_gather, d) for d in range(1, n_gather)]
+        rows = jnp.concatenate([one] + [m[0] for m in moved], axis=1)
+        tpl = jnp.concatenate([one_tpl] + [m[1] for m in moved], axis=1)
         if reduce_axis == "sy":
-            cols = lax.dynamic_index_in_dim(grid, sx, 3, keepdims=False)
             firsts = [g * n_sx + sx for g in range(n_reduce)]
         else:
-            cols = lax.dynamic_index_in_dim(grid, sy, 2, keepdims=False)
             firsts = [sy * n_sx + g for g in range(n_reduce)]
-        grams = jnp.einsum("snp,sngq->sgpq", rows, cols, preferred_element_type=jnp.float32)
-        projs = jnp.einsum("snp,snt->spt", rows, tpl, preferred_element_type=jnp.float32)
-        norm = jnp.einsum("snt,snu->stu", tpl, tpl, preferred_element_type=jnp.float32)
-        norm = jnp.pad(norm, ((0, 0), (0, 0), (0, col_width)))
-        both = jnp.concatenate(
-            [grams, jnp.broadcast_to(projs[:, None], (1, n_reduce) + projs.shape[1:])], axis=3
+        cols = jnp.concatenate(
+            [lax.dynamic_slice_in_dim(rows, f * tile_pixels, tile_pixels, 2) for f in firsts], axis=2
         )
-        both = jnp.concatenate([both, both[:, :, : half * tile_pixels]], axis=2)
+        grams = jnp.einsum("snp,snq->spq", rows, cols, preferred_element_type=jnp.float32)
+        grams = grams.reshape(k_tiles, tile_pixels, n_reduce, col_width)
+        projs = jnp.einsum("snt,snp->stp", tpl, rows, preferred_element_type=jnp.float32)
+        projs = projs.reshape(template_cols, k_tiles, tile_pixels)
+        norm = jnp.einsum("snt,snu->tu", tpl, tpl, preferred_element_type=jnp.float32)
+        norm = jnp.pad(norm, ((0, 0), (0, col_width - template_cols)))
+        steps = jnp.arange(half)
         payloads = []
         for g in range(n_reduce):
-            slab = lax.dynamic_slice_in_dim(both[:, g], firsts[g] * tile_pixels, half * tile_pixels, 1)
-            payloads.append(jnp.concatenate([slab, norm], axis=1))
+            picks = (firsts[g] + steps) % k_tiles
+            slab = jnp.take(grams[:, :, g], picks, axis=0).reshape(half * tile_pixels, col_width)
+            proj_slab = jnp.swapaxes(jnp.take(projs, picks, axis=1), 0, 1)
+            proj_slab = proj_slab.reshape(half * template_cols, tile_pixels)
+            payloads.append(jnp.concatenate([slab, proj_slab, norm], axis=0))
         payloads = jnp.stack(payloads)
         summed = None
         for d in range(n_reduce):
             part = lax.dynamic_index_in_dim(payloads, (reduce_index + d) % n_reduce, 0, keepdims=False)
             part = part if d == 0 else shifted(part, reduce_axis, n_reduce, d)
             summed = part if summed is None else summed + part
-        gram = summed[:, : half * tile_pixels, :col_width]
-        proj = jnp.swapaxes(summed[:, : half * tile_pixels, col_width:], 1, 2)
-        normal = summed[:, half * tile_pixels :, :template_cols]
-        normal = normal + jnp.eye(template_cols, dtype=jnp.float32)[None, :, :]
+        split = half * tile_pixels
+        gram = summed[:split]
+        proj = summed[split : split + half * template_cols].reshape(half, template_cols, tile_pixels)
+        proj = jnp.swapaxes(proj, 0, 1).reshape(template_cols, split)
+        normal = summed[split + half * template_cols :, :template_cols]
+        normal = normal + jnp.eye(template_cols, dtype=jnp.float32)
         factor = jnp.linalg.cholesky(normal)
         whitened = jax.scipy.linalg.solve_triangular(factor, proj, lower=True)
         correction = jnp.einsum(
-            "stp,stq->spq", whitened, whitened[:, :, :tile_pixels], precision=lax.Precision.HIGHEST
+            "tp,tq->pq", whitened, whitened[:, :tile_pixels], precision=lax.Precision.HIGHEST
         )
-        return gram - correction
+        return (gram - correction)[None]
 
     own = jnp.concatenate(
         [
-            column_blocks(local[0:1], "sx", n_sx, "sy", n_sy, sy),
-            column_blocks(local[1:2], "sy", n_sy, "sx", n_sx, sx),
+            column_blocks(masked[0:1], template[0:1], "sx", n_sx, "sy", n_sy, sy),
+            column_blocks(masked[1:2], template[1:2], "sy", n_sy, "sx", n_sx, sx),
         ],
         axis=0,
     ).reshape(scan_count, half, tile_pixels, col_width)

time: 289 us -> 367 us (1.27)
  local copies, waits for them, and re-layouts: 82.4 us -> 136 us
  other arithmetic: 42.4 us -> 66.7 us
  waiting for transfers between devices: 92.5 us -> 74.4 us
  starting transfers between devices: 44.7 us -> 56.4 us
  matrix products: 20.8 us -> 24.8 us
    gather x0 -> x16, local copies, waits for them, and re-layouts: none -> 26.5 us  [the longest x8 18.4 us: column_blocks(): jnp.take(grams[:, :, g], picks, axis=0)]
    select_n x0 -> x20, other arithmetic: none -> 23.8 us  [the longest x12 14.4 us: column_blocks(): jnp.take(grams[:, :, g], picks, axis=0)]
    ppermute x12 -> x18, waiting for transfers between devices: 57 us -> 36 us  [shifted(): return lax.ppermute(x, axis, [(i, (i + d) % n) for i in range(n)])]
    dot_general x0 -> x4, local copies, waits for them, and re-layouts: none -> 15.7 us  [column_blocks(): jnp.einsum('snp,snq->spq', rows, cols, preferred_element_type=jnp.float32)]
    concatenate x2 -> x9, local copies, waits for them, and re-layouts: 4.46 us -> 14.2 us  [the longest x8 14.2 us: column_blocks(): payloads.append(jnp.concatenate([slab, proj_slab, norm], axis=0))]
    ppermute x12 -> x18, starting transfers between devices: 16.9 us -> 26.2 us  [shifted(): return lax.ppermute(x, axis, [(i, (i + d) % n) for i in range(n)])]
    slice x8 -> x7, local copies, waits for them, and re-layouts: 10.8 us -> 1.48 us  [the longest x1 1.21 us: per_device(): masked[0:1]]
    concatenate x5 -> x3, other arithmetic: 15.2 us -> 7.25 us  [the longest x2 7.18 us: column_blocks(): rows = jnp.concatenate([one] + [m[0] for m in moved], axis=1)]
  transfers between devices with their start and end apart: 21 -> 27, of which waited for: 6 -> 6; matrix products, arithmetic and copies ran while one was open for 39% -> 57% of each run, Pallas kernels for 0% -> 0%
where the time goes in v4:
time: 367 us; the launch traced here: 360 us
  local copies, waits for them, and re-layouts  136 us (37%)
  waiting for transfers between devices  74.4 us (20%)
  other arithmetic  66.7 us (18%)
  starting transfers between devices  56.4 us (15%)
  matrix products  24.8 us (7%)
    ppermute x18, waiting for transfers between devices, shifted(): return lax.ppermute(x, axis, [(i, (i + d) % n) for i in range(n)])  36 us
    ppermute x18, starting transfers between devices, shifted(): return lax.ppermute(x, axis, [(i, (i + d) % n) for i in range(n)])  26.2 us
    all_to_all x1, waiting for transfers between devices, per_device(): lax.all_to_all(send_rows, 'tile', split_axis=0, concat_axis=0, tiled=True)  25.8 us
    gather x8, local copies, waits for them, and re-layouts, column_blocks(): jnp.take(grams[:, :, g], picks, axis=0)  18.4 us
    dynamic_slice x8, local copies, waits for them, and re-layouts, column_blocks(): lax.dynamic_index_in_dim(payloads, (reduce_index + d) % n_reduce, 0, keep...  16.6 us
    dot_general x4, local copies, waits for them, and re-layouts, column_blocks(): jnp.einsum('snp,snq->spq', rows, cols, preferred_element_type=jnp.float32)  15.7 us
    select_n x12, other arithmetic, column_blocks(): jnp.take(grams[:, :, g], picks, axis=0)  14.4 us
    concatenate x8, local copies, waits for them, and re-layouts, column_blocks(): payloads.append(jnp.concatenate([slab, proj_slab, norm], axis=0))  14.2 us
  transfers between devices with their start and end apart: 27, of which 6 were waited for; matrix products, arithmetic and copies ran while one was open for 57% of the time, Pallas kernels for 0%

profile of v4, /device:TPU:1, one launch (start us, length us, event | category | flops | bytes accessed | tf_op | source)
XLA Modules:
  0.0 359.9 jit_solution(543663614438984039)
XLA Ops:
  20.0 30.5 %collective-permute-done.3 = bf16[1,256,32]{1,2,0:T(8,128)(2,1)S(1)} collective-permute-done((bf16[1,256,32]{1,2,0:T(8,128)(2,1)S(1)}, bf16[1,256,32]{1,2,0:T(8,128)(2,1)S(1)}, u32[]{:S(2)}, u32[]{:S(2)}) %collective-permute-start.3) | collective-permute-done | bytes 16416 | tf_op jit(solution)/shard_map/ppermute | solution.py:52
  50.6 3.5 collective-permute-start.5
  66.3 3.4 pad_maximum_fusion
  70.6 6.4 %copy.169 = bf16[2048,1024]{1,0:T(8,128)(2,1)} copy(bf16[2048,1024]{0,1:T(8,128)(2,1)} %get-tuple-element.20) | data formatting | bytes 8388608 | tf_op jit(solution)/shard_map/snp,snq->spq/dot_general | solution.py:65
  77.1 4.2 %fusion.84 = f32[16,128,4,128]{3,1,2,0:T(8,128)S(1)} fusion(bf16[16,128,1024,1]{2,1,3,0:T(8,128)(2,1)} %bitcast.236, bf16[4,128,1024,1]{2,1,0,3:T(8,128)(2,1)S(1)} %bitcast.265), kind=kOutput, calls=%fused_computation.286 | convolution fusion | flops 2147483648 | bytes 9437184 | tf_op jit(solution)/shard_map/snp,snq->spq/dot_general | solution.py:65
  89.4 3.5 fusion.24
  128.9 3.4 collective-permute-start.7
  134.8 3.8 %pad_maximum_fusion.1 = (bf16[1,1024,2048]{2,1,0:T(8,128)(2,1)S(1)}, bf16[2048,1024]{0,1:T(8,128)(2,1)}) fusion(bf16[1,256,2048]{2,1,0:T(8,128)(2,1)} %collective-permute-done.11, bf16[1,256,2048]{2,1,0:T(8,128)(2,1)} %collective-permute-done.10, bf16[1,256,2048]{2,1,0:T(8,128)(2,1)} %collective-permute-done.9, bf16[1,256,2048]{2,1,0:T(8,128)(2,1)} %get-tuple-element.38), kind=kLoop, calls=%fused_computation.20 | loop fusion | flops 16777216 | bytes 12582912 | tf_op jit(solution)/shard_map/concatenate | solution.py:56
  142.3 6.4 %copy.194 = bf16[2048,1024]{1,0:T(8,128)(2,1)} copy(bf16[2048,1024]{0,1:T(8,128)(2,1)} %get-tuple-element.30) | data formatting | bytes 8388608 | tf_op jit(solution)/shard_map/snp,snq->spq/dot_general | solution.py:65
  148.7 4.5 %fusion.85 = f32[16,128,4,128]{3,1,2,0:T(8,128)S(1)} fusion(bf16[16,128,1024,1]{2,1,3,0:T(8,128)(2,1)} %bitcast.238, bf16[4,128,1024,1]{2,1,0,3:T(8,128)(2,1)} %bitcast.266), kind=kOutput, calls=%fused_computation.287 | convolution fusion | flops 2147483648 | bytes 9437184 | tf_op jit(solution)/shard_map/snp,snq->spq/dot_general | solution.py:65
  162.3 3.5 fusion.20
  225.2 11.2 %all-to-all-start.1 = ((s32[8,4,2]{1,2,0:T(2,128)}), s32[8,4,2]{1,2,0:T(2,128)S(1)}, u32[]{:S(2)}, u32[]{:S(2)}) async-start(s32[8,4,2]{1,2,0:T(2,128)} %copy.230), calls=%async_computation.1 | async-start | bytes 16384 | tf_op jit(solution)/shard_map/all_to_all | solution.py:132
  252.6 5.4 %collective-permute-done.17 = f32[1472,128]{1,0:T(8,128)} collective-permute-done((f32[1472,128]{1,0:T(8,128)}, f32[1472,128]{1,0:T(8,128)}, u32[]{:S(2)}, u32[]{:S(2)}) %collective-permute-start.17) | collective-permute-done | bytes 753696 | tf_op jit(solution)/shard_map/ppermute | solution.py:52
  262.1 2.9 cholesky.44
  270.3 2.9 cholesky.55
  278.6 4.2 %collective-permute-start.18 = (f32[2,128,128]{2,1,0:T(8,128)S(1)}, f32[2,128,128]{2,1,0:T(8,128)S(1)}, u32[]{:S(2)}, u32[]{:S(2)}) collective-permute-start(f32[2,128,128]{2,1,0:T(8,128)S(1)} %bitcast.289), channel_id=1, source_target_pairs={{0,56},{8,64},{16,72},{24,80},{32,88},{40,96},{48,104},{56,112},{6... | collective-permute-start | bytes 393224 | tf_op jit(solution)/shard_map/ppermute | solution.py:110
  285.5 3.6 collective-permute-start.22
  292.2 6.9 %collective-permute-done.20 = f32[2,128,128]{2,1,0:T(8,128)S(1)} collective-permute-done((f32[2,128,128]{2,1,0:T(8,128)S(1)}, f32[2,128,128]{2,1,0:T(8,128)S(1)}, u32[]{:S(2)}, u32[]{:S(2)}) %collective-permute-start.20) | collective-permute-done | bytes 131104 | tf_op jit(solution)/shard_map/ppermute | solution.py:110
  299.2 3.8 %collective-permute-done.21 = f32[2,128,128]{2,1,0:T(8,128)S(1)} collective-permute-done((f32[2,128,128]{2,1,0:T(8,128)S(1)}, f32[2,128,128]{2,1,0:T(8,128)S(1)}, u32[]{:S(2)}, u32[]{:S(2)}) %collective-permute-start.21) | collective-permute-done | bytes 131104 | tf_op jit(solution)/shard_map/ppermute | solution.py:110
  305.6 4.3 %copy.226 = f32[8,4,128,128]{3,1,2,0:T(4,128)} copy(f32[8,4,128,128]{3,2,1,0:T(8,128)} %bitcast.247) | data formatting | bytes 4194304 | tf_op jit(solution)/shard_map/reshape | solution.py:128
  309.9 7.9 %all-to-all-start = ((f32[8,4,128,128]{3,1,2,0:T(4,128)}), f32[8,4,128,128]{3,1,2,0:T(4,128)S(1)}, u32[]{:S(2)}, u32[]{:S(2)}) async-start(f32[8,4,128,128]{3,1,2,0:T(4,128)} %copy.226), calls=%async_computation | async-start | bytes 4194304 | tf_op jit(solution)/shard_map/all_to_all | solution.py:131
  317.9 25.8 %all-to-all-done = f32[8,4,128,128]{3,1,2,0:T(4,128)S(1)} async-done(((f32[8,4,128,128]{3,1,2,0:T(4,128)}), f32[8,4,128,128]{3,1,2,0:T(4,128)S(1)}, u32[]{:S(2)}, u32[]{:S(2)}) %all-to-all-start) | async-done | bytes 2097184 | tf_op jit(solution)/shard_map/all_to_all | solution.py:131
  344.4 6.9 %convolution_bitcast_fusion = f32[16,128,8,128]{3,0,2,1:T(8,128)S(1)} fusion(f32[32,128,128,1]{2,0,3,1:T(8,128)S(1)} %bitcast.248, f32[32,8]{0,1:T(8,128)S(1)} %fusion.55, f32[32,16]{0,1:T(8,128)S(1)} %fusion.54), kind=kOutput, calls=%fused_computation.21 | convolution fusion | flops 805310464 | bytes 10488832 | tf_op jit(solution)/shard_map/irkc,ixky->rxcy/dot_general | solution.py:140
  353.9 5.5 %copy.261 = f32[256,8,8,128]{3,1,2,0:T(8,128)} copy(f32[256,8,8,128]{3,2,1,0:T(8,128)S(1)} %bitcast.235) | data formatting | bytes 16777216
  (295 shorter events, 194.0 us)
Async XLA Ops:
  3.8 61.6 %collective-permute-start = (bf16[1,256,2048]{2,1,0:T(8,128)(2,1)S(1)}, bf16[1,256,2048]{2,1,0:T(8,128)(2,1)S(1)}, u32[]{:S(2)}, u32[]{:S(2)}) collective-permute-start(bf16[1,256,2048]{2,1,0:T(8,128)(2,1)S(1)} %get-tuple-element.37), channel_id=1, source_target_pairs={{0,8},{8,16},{16,24},{24,0},{1,9},{9,17},{17,25},{25,1},{2,10},{10... | collective-permute-start | bytes 3145736 | tf_op jit(solution)/shard_map/ppermute | solution.py:52
  5.9 60.4 %collective-permute-start.1 = (bf16[1,256,2048]{2,1,0:T(8,128)(2,1)S(1)}, bf16[1,256,2048]{2,1,0:T(8,128)(2,1)S(1)}, u32[]{:S(2)}, u32[]{:S(2)}) collective-permute-start(bf16[1,256,2048]{2,1,0:T(8,128)(2,1)S(1)} %get-tuple-element.37), channel_id=1, source_target_pairs={{0,16},{8,24},{16,0},{24,8},{1,17},{9,25},{17,1},{25,9},{2,18},{10... | collective-permute-start | bytes 3145736 | tf_op jit(solution)/shard_map/ppermute | solution.py:52
  8.3 58.0 %collective-permute-start.2 = (bf16[1,256,2048]{2,1,0:T(8,128)(2,1)S(1)}, bf16[1,256,2048]{2,1,0:T(8,128)(2,1)}, u32[]{:S(2)}, u32[]{:S(2)}) collective-permute-start(bf16[1,256,2048]{2,1,0:T(8,128)(2,1)S(1)} %get-tuple-element.37), channel_id=1, source_target_pairs={{0,24},{8,0},{16,8},{24,16},{1,25},{9,1},{17,9},{25,17},{2,26},{10... | collective-permute-start | bytes 3145736 | tf_op jit(solution)/shard_map/ppermute | solution.py:52
  9.8 40.8 %collective-permute-start.3 = (bf16[1,256,32]{1,2,0:T(8,128)(2,1)S(1)}, bf16[1,256,32]{1,2,0:T(8,128)(2,1)S(1)}, u32[]{:S(2)}, u32[]{:S(2)}) collective-permute-start(bf16[1,256,32]{1,2,0:T(8,128)(2,1)S(1)} %get-tuple-element.46), channel_id=1, source_target_pairs={{0,8},{8,16},{16,24},{24,0},{1,9},{9,17},{17,25},{25,1},{2,10},{10... | collective-permute-start | bytes 49160 | tf_op jit(solution)/shard_map/ppermute | solution.py:52
  10.2 43.9 %collective-permute-start.4 = (bf16[1,256,32]{1,2,0:T(8,128)(2,1)S(1)}, bf16[1,256,32]{1,2,0:T(8,128)(2,1)S(1)}, u32[]{:S(2)}, u32[]{:S(2)}) collective-permute-start(bf16[1,256,32]{1,2,0:T(8,128)(2,1)S(1)} %get-tuple-element.46), channel_id=1, source_target_pairs={{0,16},{8,24},{16,0},{24,8},{1,17},{9,25},{17,1},{25,9},{2,18},{10... | collective-permute-start | bytes 49160 | tf_op jit(solution)/shard_map/ppermute | solution.py:52
  50.6 6.2 %collective-permute-start.5 = (bf16[1,256,32]{1,2,0:T(8,128)(2,1)S(1)}, bf16[1,256,32]{1,2,0:T(8,128)(2,1)S(1)}, u32[]{:S(2)}, u32[]{:S(2)}) collective-permute-start(bf16[1,256,32]{1,2,0:T(8,128)(2,1)S(1)} %get-tuple-element.46), channel_id=1, source_target_pairs={{0,24},{8,0},{16,8},{24,16},{1,25},{9,1},{17,9},{25,17},{2,26},{10... | collective-permute-start | bytes 49160 | tf_op jit(solution)/shard_map/ppermute | solution.py:52
  61.3 73.3 %collective-permute-start.10 = (bf16[1,256,2048]{2,1,0:T(8,128)(2,1)}, bf16[1,256,2048]{2,1,0:T(8,128)(2,1)}, u32[]{:S(2)}, u32[]{:S(2)}) collective-permute-start(bf16[1,256,2048]{2,1,0:T(8,128)(2,1)} %get-tuple-element.38), channel_id=1, source_target_pairs={{0,64},{32,96},{64,0},{96,32},{1,65},{33,97},{65,1},{97,33},{2,66}... | collective-permute-start | bytes 3145736 | tf_op jit(solution)/shard_map/ppermute | solution.py:52
  63.5 71.2 %collective-permute-start.11 = (bf16[1,256,2048]{2,1,0:T(8,128)(2,1)}, bf16[1,256,2048]{2,1,0:T(8,128)(2,1)}, u32[]{:S(2)}, u32[]{:S(2)}) collective-permute-start(bf16[1,256,2048]{2,1,0:T(8,128)(2,1)} %get-tuple-element.38), channel_id=1, source_target_pairs={{0,96},{32,0},{64,32},{96,64},{1,97},{33,1},{65,33},{97,65},{2,98}... | collective-permute-start | bytes 3145736 | tf_op jit(solution)/shard_map/ppermute | solution.py:52
  65.4 69.4 %collective-permute-start.9 = (bf16[1,256,2048]{2,1,0:T(8,128)(2,1)}, bf16[1,256,2048]{2,1,0:T(8,128)(2,1)}, u32[]{:S(2)}, u32[]{:S(2)}) collective-permute-start(bf16[1,256,2048]{2,1,0:T(8,128)(2,1)} %get-tuple-element.38), channel_id=1, source_target_pairs={{0,32},{32,64},{64,96},{96,0},{1,33},{33,65},{65,97},{97,1},{2,34}... | collective-permute-start | bytes 3145736 | tf_op jit(solution)/shard_map/ppermute | solution.py:52
  126.6 112.1 %collective-permute-start.6 = (f32[1472,128]{1,0:T(8,128)}, f32[1472,128]{1,0:T(8,128)}, u32[]{:S(2)}, u32[]{:S(2)}) collective-permute-start(f32[1472,128]{1,0:T(8,128)} %bitcast.269), channel_id=1, source_target_pairs={{0,32},{32,64},{64,96},{96,0},{1,33},{33,65},{65,97},{97,1},{2,34}... | collective-permute-start | bytes 2261000 | tf_op jit(solution)/shard_map/ppermute | solution.py:52
  128.9 112.7 %collective-permute-start.7 = (f32[1472,128]{1,0:T(8,128)}, f32[1472,128]{1,0:T(8,128)}, u32[]{:S(2)}, u32[]{:S(2)}) collective-permute-start(f32[1472,128]{1,0:T(8,128)} %bitcast.267), channel_id=1, source_target_pairs={{0,64},{32,96},{64,0},{96,32},{1,65},{33,97},{65,1},{97,33},{2,66}... | collective-permute-start | bytes 2261000 | tf_op jit(solution)/shard_map/ppermute | solution.py:52
  134.6 109.3 %collective-permute-start.8 = (f32[1472,128]{1,0:T(8,128)}, f32[1472,128]{1,0:T(8,128)}, u32[]{:S(2)}, u32[]{:S(2)}) collective-permute-start(f32[1472,128]{1,0:T(8,128)} %bitcast.268), channel_id=1, source_target_pairs={{0,96},{32,0},{64,32},{96,64},{1,97},{33,1},{65,33},{97,65},{2,98}... | collective-permute-start | bytes 2261000 | tf_op jit(solution)/shard_map/ppermute | solution.py:52
  219.2 29.6 %collective-permute-start.15 = (f32[1472,128]{1,0:T(8,128)}, f32[1472,128]{1,0:T(8,128)}, u32[]{:S(2)}, u32[]{:S(2)}) collective-permute-start(f32[1472,128]{1,0:T(8,128)} %bitcast.270), channel_id=1, source_target_pairs={{0,8},{8,16},{16,24},{24,0},{1,9},{9,17},{17,25},{25,1},{2,10},{10... | collective-permute-start | bytes 2261000 | tf_op jit(solution)/shard_map/ppermute | solution.py:52
  222.4 28.0 %collective-permute-start.16 = (f32[1472,128]{1,0:T(8,128)}, f32[1472,128]{1,0:T(8,128)}, u32[]{:S(2)}, u32[]{:S(2)}) collective-permute-start(f32[1472,128]{1,0:T(8,128)} %bitcast.271), channel_id=1, source_target_pairs={{0,16},{8,24},{16,0},{24,8},{1,17},{9,25},{17,1},{25,9},{2,18},{10... | collective-permute-start | bytes 2261000 | tf_op jit(solution)/shard_map/ppermute | solution.py:52
  225.2 84.7 %all-to-all-start.1 = ((s32[8,4,2]{1,2,0:T(2,128)}), s32[8,4,2]{1,2,0:T(2,128)S(1)}, u32[]{:S(2)}, u32[]{:S(2)}) async-start(s32[8,4,2]{1,2,0:T(2,128)} %copy.230), calls=%async_computation.1 | async-start | bytes 16384 | tf_op jit(solution)/shard_map/all_to_all | solution.py:132
  238.6 19.4 %collective-permute-start.17 = (f32[1472,128]{1,0:T(8,128)}, f32[1472,128]{1,0:T(8,128)}, u32[]{:S(2)}, u32[]{:S(2)}) collective-permute-start(f32[1472,128]{1,0:T(8,128)} %bitcast.272), channel_id=1, source_target_pairs={{0,24},{8,0},{16,8},{24,16},{1,25},{9,1},{17,9},{25,17},{2,26},{10... | collective-permute-start | bytes 2261000 | tf_op jit(solution)/shard_map/ppermute | solution.py:52
  278.6 10.8 %collective-permute-start.18 = (f32[2,128,128]{2,1,0:T(8,128)S(1)}, f32[2,128,128]{2,1,0:T(8,128)S(1)}, u32[]{:S(2)}, u32[]{:S(2)}) collective-permute-start(f32[2,128,128]{2,1,0:T(8,128)S(1)} %bitcast.289), channel_id=1, source_target_pairs={{0,56},{8,64},{16,72},{24,80},{32,88},{40,96},{48,104},{56,112},{6... | collective-permute-start | bytes 393224 | tf_op jit(solution)/shard_map/ppermute | solution.py:110
  282.9 9.3 %collective-permute-start.19 = (f32[2,128,128]{2,1,0:T(8,128)S(1)}, f32[2,128,128]{2,1,0:T(8,128)S(1)}, u32[]{:S(2)}, u32[]{:S(2)}) collective-permute-start(f32[2,128,128]{2,1,0:T(8,128)S(1)} %bitcast.288), channel_id=1, source_target_pairs={{0,48},{8,56},{16,64},{24,72},{32,80},{40,88},{48,96},{56,104},{64... | collective-permute-start | bytes 393224 | tf_op jit(solution)/shard_map/ppermute | solution.py:110
  283.1 16.1 %collective-permute-start.20 = (f32[2,128,128]{2,1,0:T(8,128)S(1)}, f32[2,128,128]{2,1,0:T(8,128)S(1)}, u32[]{:S(2)}, u32[]{:S(2)}) collective-permute-start(f32[2,128,128]{2,1,0:T(8,128)S(1)} %bitcast.284), channel_id=1, source_target_pairs={{0,40},{8,48},{16,56},{24,64},{32,72},{40,80},{48,88},{56,96},{64,... | collective-permute-start | bytes 393224 | tf_op jit(solution)/shard_map/ppermute | solution.py:110
  283.3 19.7 %collective-permute-start.21 = (f32[2,128,128]{2,1,0:T(8,128)S(1)}, f32[2,128,128]{2,1,0:T(8,128)S(1)}, u32[]{:S(2)}, u32[]{:S(2)}) collective-permute-start(f32[2,128,128]{2,1,0:T(8,128)S(1)} %bitcast.285), channel_id=1, source_target_pairs={{0,32},{8,40},{16,48},{24,56},{32,64},{40,72},{48,80},{56,88},{64,... | collective-permute-start | bytes 393224 | tf_op jit(solution)/shard_map/ppermute | solution.py:110
  285.5 17.5 %collective-permute-start.22 = (f32[2,128,128]{2,1,0:T(8,128)S(1)}, f32[2,128,128]{2,1,0:T(8,128)S(1)}, u32[]{:S(2)}, u32[]{:S(2)}) collective-permute-start(f32[2,128,128]{2,1,0:T(8,128)S(1)} %bitcast.286), channel_id=1, source_target_pairs={{0,24},{8,32},{16,40},{24,48},{32,56},{40,64},{48,72},{56,80},{64,... | collective-permute-start | bytes 393224 | tf_op jit(solution)/shard_map/ppermute | solution.py:110
  289.4 13.6 %collective-permute-start.23 = (f32[2,128,128]{2,1,0:T(8,128)S(1)}, f32[2,128,128]{2,1,0:T(8,128)S(1)}, u32[]{:S(2)}, u32[]{:S(2)}) collective-permute-start(f32[2,128,128]{2,1,0:T(8,128)S(1)} %bitcast.287), channel_id=1, source_target_pairs={{0,16},{8,24},{16,32},{24,40},{32,48},{40,56},{48,64},{56,72},{64,... | collective-permute-start | bytes 393224 | tf_op jit(solution)/shard_map/ppermute | solution.py:110
  292.2 10.9 %collective-permute-start.24 = (f32[2,128,128]{2,1,0:T(8,128)S(1)}, f32[2,128,128]{2,1,0:T(8,128)S(1)}, u32[]{:S(2)}, u32[]{:S(2)}) collective-permute-start(f32[2,128,128]{2,1,0:T(8,128)S(1)} %bitcast.283), channel_id=1, source_target_pairs={{0,8},{8,16},{16,24},{24,32},{32,40},{40,48},{48,56},{56,64},{64,7... | collective-permute-start | bytes 393224 | tf_op jit(solution)/shard_map/ppermute | solution.py:110
  309.9 33.9 %all-to-all-start = ((f32[8,4,128,128]{3,1,2,0:T(4,128)}), f32[8,4,128,128]{3,1,2,0:T(4,128)S(1)}, u32[]{:S(2)}, u32[]{:S(2)}) async-start(f32[8,4,128,128]{3,1,2,0:T(4,128)} %copy.226), calls=%async_computation | async-start | bytes 4194304 | tf_op jit(solution)/shard_map/all_to_all | solution.py:131
  (36 other events, 517.9 us)

commit v5 on v1

--- a/solution.py
+++ b/solution.py
@@ -47,39 +47,54 @@
     inside = position[None, :] < lengths[:, None]
     masked = jnp.where(inside[:, :, None], pointing, jnp.zeros_like(pointing))
     template = build_templates(ground_bin, position, lengths, degrees)
-    proj_part = jnp.einsum("snt,snp->stp", template, masked, preferred_element_type=jnp.float32)
-    norm_part = jnp.einsum("snt,snu->stu", template, template, preferred_element_type=jnp.float32)
-    proj, norm = lax.psum((proj_part, norm_part), SCAN_AXES)
+    pad = jnp.zeros((scan_count, sample_rows, tile_pixels - template_cols), jnp.bfloat16)
+    local = jnp.concatenate([masked, template, pad], axis=2)
 
-    rows_x = lax.all_gather(masked, "sx", axis=1, tiled=True)
-    wrapped = jnp.concatenate([rows_x, rows_x[:, :, : half * tile_pixels]], axis=2)
-    parts = []
-    for y in range(n_sy):
-        col = y * n_sx + sx
-        row_blocks = lax.dynamic_slice_in_dim(wrapped, col * tile_pixels, half * tile_pixels, 2)
-        col_block = lax.dynamic_slice_in_dim(rows_x, col * tile_pixels, tile_pixels, 2)
-        parts.append(
-            jnp.einsum("snp,snq->spq", row_blocks, col_block, preferred_element_type=jnp.float32)
+    def shifted(x, axis, n, d):
+        return lax.ppermute(x, axis, [(i, (i + d) % n) for i in range(n)])
+
+    def column_sums(one, gather_axis, n_gather, reduce_axis, n_reduce, reduce_index):
+        rows_all = jnp.concatenate(
+            [one] + [shifted(one, gather_axis, n_gather, d) for d in range(1, n_gather)], axis=1
         )
-    gram_part = lax.psum_scatter(jnp.stack(parts), "sy", scatter_dimension=0, tiled=False)
+        rows = rows_all[:, :, :width]
+        tpl = rows_all[:, :, width : width + template_cols]
+        if reduce_axis == "sy":
+            firsts = [((reduce_index + d) % n_reduce) * n_sx + sx for d in range(n_reduce)]
+        else:
+            firsts = [sy * n_sx + (reduce_index + d) % n_reduce for d in range(n_reduce)]
+        cols = jnp.concatenate(
+            [lax.dynamic_slice_in_dim(rows, f * tile_pixels, tile_pixels, 2) for f in firsts], axis=2
+        )
+        grams = jnp.einsum("snp,snq->pq", rows, cols, preferred_element_type=jnp.float32)
+        projs = jnp.einsum("snt,snp->tp", tpl, rows, preferred_element_type=jnp.float32)
+        projs = jnp.swapaxes(projs.reshape(template_cols, k_tiles, tile_pixels), 0, 1)
+        projs = projs.reshape(k_tiles * template_cols, tile_pixels)
+        norm = jnp.einsum("snt,snu->tu", tpl, tpl, preferred_element_type=jnp.float32)
+        norm = jnp.pad(norm, ((0, 0), (0, col_width - template_cols)))
+        summed = None
+        for d in range(n_reduce):
+            part = jnp.concatenate([grams[:, d * col_width : (d + 1) * col_width], projs, norm], axis=0)
+            part = part if d == 0 else shifted(part, reduce_axis, n_reduce, d)
+            summed = part if summed is None else summed + part
+        return summed
 
-    normal = norm + jnp.eye(template_cols, dtype=jnp.float32)[None, :, :]
+    summed = jnp.stack(
+        [
+            column_sums(local[0:1], "sx", n_sx, "sy", n_sy, sy),
+            column_sums(local[1:2], "sy", n_sy, "sx", n_sx, sx),
+        ]
+    )
+    gram = summed[:, :width]
+    proj = summed[:, width : width + k_tiles * template_cols].reshape(scan_count, k_tiles, template_cols, tile_pixels)
+    proj = jnp.swapaxes(proj, 1, 2).reshape(scan_count, template_cols, width)
+    normal = summed[:, width + k_tiles * template_cols :, :template_cols]
+    normal = normal + jnp.eye(template_cols, dtype=jnp.float32)[None]
     factor = jnp.linalg.cholesky(normal)
     whitened = jax.scipy.linalg.solve_triangular(factor, proj, lower=True)
-    w_wrapped = jnp.concatenate([whitened, whitened[:, :, : half * tile_pixels]], axis=2)
-    w_rows = lax.dynamic_slice_in_dim(w_wrapped, scan_index * tile_pixels, half * tile_pixels, 2)
     w_col = lax.dynamic_slice_in_dim(whitened, scan_index * tile_pixels, tile_pixels, 2)
-    correction = jnp.einsum("stp,stq->spq", w_rows, w_col, precision=lax.Precision.HIGHEST)
-    own = (gram_part - correction).reshape(scan_count, half, tile_pixels, col_width)
-
-    received = []
-    for d in range(k_tiles - half, 0, -1):
-        block = jnp.swapaxes(own[:, d], 1, 2)
-        perm = [(i, (i + d) % n_scan) for i in range(n_scan)]
-        received.append(lax.ppermute(block, SCAN_AXES, perm))
-    relative = jnp.concatenate([own, jnp.stack(received, axis=1)], axis=1)
-    column = jnp.roll(relative, scan_index, axis=1)
-    contrib = column.reshape(scan_count, width, col_width)
+    correction = jnp.einsum("stp,stq->spq", whitened, w_col, precision=lax.Precision.HIGHEST)
+    contrib = gram - correction
 
     k_cols = 1
     tile_rows = contrib.reshape(scan_count * k_tiles, tile_pixels, col_width)

time: 297 us -> 264 us (0.89)
  the two profiles are of different devices: /device:TPU:1 before, /device:TPU:4 now
where the time goes in v5:
time: 264 us; the launch traced here: 263 us
  waiting for transfers between devices  117 us (44%)
  local copies, waits for them, and re-layouts  50 us (19%)
  starting transfers between devices  41.3 us (16%)
  other arithmetic  35.1 us (13%)
  matrix products  19.4 us (7%)
    ppermute x12, waiting for transfers between devices, shifted(): return lax.ppermute(x, axis, [(i, (i + d) % n) for i in range(n)])  89.5 us
    ppermute x12, starting transfers between devices, shifted(): return lax.ppermute(x, axis, [(i, (i + d) % n) for i in range(n)])  31.6 us
    all_to_all x1, waiting for transfers between devices, per_device(): lax.all_to_all(send_rows, 'tile', split_axis=0, concat_axis=0, tiled=True)  27.1 us
    ppermute x4, local copies, waits for them, and re-layouts, shifted(): return lax.ppermute(x, axis, [(i, (i + d) % n) for i in range(n)])  11.4 us
    unnamed x18, local copies, waits for them, and re-layouts  9.46 us
    concatenate x1, local copies, waits for them, and re-layouts, per_device(): local = jnp.concatenate([masked, template, pad], axis=2)  7.35 us
    dot_general x1, matrix products, per_device(): jnp.einsum('irkc,ixky->rxcy', placing, recv_rows, precision=lax.Precision...  6.85 us
    another operation x4, other arithmetic, per_device(): factor = jnp.linalg.cholesky(normal)  6.03 us
  transfers between devices with their start and end apart: 14, of which 7 were waited for; matrix products, arithmetic and copies ran while one was open for 27% of the time, Pallas kernels for 0%

profile of v5, /device:TPU:4, one launch (start us, length us, event | category | flops | bytes accessed | tf_op | source)
XLA Modules:
  0.0 262.7 jit_solution(8731146356838726576)
XLA Ops:
  2.1 3.9 %copy.131 = bf16[2,256,2048]{1,2,0:T(8,128)(2,1)} copy(bf16[2,256,2048]{2,1,0:T(8,128)(2,1)} %param.6) | data formatting | bytes 4194304 | tf_op args[0]
  8.0 7.3 %concatenate.45 = bf16[2,256,2176]{1,2,0:T(8,128)(2,1)} concatenate(bf16[2,256,2048]{1,2,0:T(8,128)(2,1)S(1)} %broadcast_select_fusion, bf16[2,256,1]{1,2,0:T(2,128)(2,1)S(1)} %get-tuple-element.38, bf16[2,256,1]{1,2,0:T(2,128)(2,1)S(1)} %get-tuple-element.37, bf16[2,256,1]{1,2,0:T(2,128)(2,1)S(1)} %get-tuple-element.36, bf16[2,256,1]{1,2,0:T(2,128)(2,1)S(1)} %get-tuple-element.35, ...), dimensions={2} | concatenate | bytes 4456448 | tf_op jit(solution)/shard_map/concatenate | solution.py:51
  17.7 2.7 %collective-permute-start.1 = (bf16[1,256,2176]{1,2,0:T(8,128)(2,1)S(1)}, bf16[1,256,2176]{1,2,0:T(8,128)(2,1)}, u32[]{:S(2)}, u32[]{:S(2)}) collective-permute-start(bf16[1,256,2176]{1,2,0:T(8,128)(2,1)S(1)} %get-tuple-element.24), channel_id=1, source_target_pairs={{0,16},{8,24},{16,0},{24,8},{1,17},{9,25},{17,1},{25,9},{2,18},{10... | collective-permute-start | bytes 3342344 | tf_op jit(solution)/shard_map/ppermute | solution.py:54
  20.4 3.0 %collective-permute-start.8 = (bf16[1,256,2176]{1,2,0:T(8,128)(2,1)S(1)}, bf16[1,256,2176]{1,2,0:T(8,128)(2,1)S(1)}, u32[]{:S(2)}, u32[]{:S(2)}) collective-permute-start(bf16[1,256,2176]{1,2,0:T(8,128)(2,1)S(1)} %get-tuple-element.23), channel_id=1, source_target_pairs={{0,96},{32,0},{64,32},{96,64},{1,97},{33,1},{65,33},{97,65},{2,98}... | collective-permute-start | bytes 3342344 | tf_op jit(solution)/shard_map/ppermute | solution.py:54
  26.5 18.2 %collective-permute-done.2 = bf16[1,256,2176]{1,2,0:T(8,128)(2,1)} collective-permute-done((bf16[1,256,2176]{1,2,0:T(8,128)(2,1)S(1)}, bf16[1,256,2176]{1,2,0:T(8,128)(2,1)}, u32[]{:S(2)}, u32[]{:S(2)}) %collective-permute-start.2) | collective-permute-done | bytes 1114144 | tf_op jit(solution)/shard_map/ppermute | solution.py:54
  46.8 22.4 %collective-permute-done = bf16[1,256,2176]{1,2,0:T(8,128)(2,1)} collective-permute-done((bf16[1,256,2176]{1,2,0:T(8,128)(2,1)S(1)}, bf16[1,256,2176]{1,2,0:T(8,128)(2,1)}, u32[]{:S(2)}, u32[]{:S(2)}) %collective-permute-start) | collective-permute-done | bytes 1114144 | tf_op jit(solution)/shard_map/ppermute | solution.py:54
  92.7 16.8 %collective-permute-start.9 = (f32[2592,128]{1,0:T(8,128)}, f32[2592,128]{1,0:T(8,128)}, u32[]{:S(2)}, u32[]{:S(2)}) collective-permute-start(f32[2592,128]{1,0:T(8,128)} %get-tuple-element.26), channel_id=1, source_target_pairs={{0,8},{8,16},{16,24},{24,0},{1,9},{9,17},{17,25},{25,1},{2,10},{10... | collective-permute-start | bytes 3981320 | tf_op jit(solution)/shard_map/ppermute | solution.py:54
  110.9 5.3 %all-to-all-start.1 = ((s32[8,4,2]{1,2,0:T(2,128)}), s32[8,4,2]{1,2,0:T(2,128)S(1)}, u32[]{:S(2)}, u32[]{:S(2)}) async-start(s32[8,4,2]{1,2,0:T(2,128)} %copy.149), calls=%async_computation.1 | async-start | bytes 16384 | tf_op jit(solution)/shard_map/all_to_all | solution.py:116
  122.8 16.6 %collective-permute-done.9 = f32[2592,128]{1,0:T(8,128)} collective-permute-done((f32[2592,128]{1,0:T(8,128)}, f32[2592,128]{1,0:T(8,128)}, u32[]{:S(2)}, u32[]{:S(2)}) %collective-permute-start.9) | collective-permute-done | bytes 1327136 | tf_op jit(solution)/shard_map/ppermute | solution.py:54
  142.8 6.9 %collective-permute-done.4 = f32[2592,128]{1,0:T(8,128)} collective-permute-done((f32[2592,128]{1,0:T(8,128)}, f32[2592,128]{1,0:T(8,128)}, u32[]{:S(2)}, u32[]{:S(2)}) %collective-permute-start.4) | collective-permute-done | bytes 1327136 | tf_op jit(solution)/shard_map/ppermute | solution.py:54
  149.7 2.8 %copy.133 = f32[2592,128]{0,1:T(8,128)} copy(f32[2592,128]{1,0:T(8,128)} %collective-permute-done.4) | data formatting | bytes 2654208 | tf_op jit(solution)/shard_map/ppermute | solution.py:54
  152.6 24.8 %collective-permute-done.5 = f32[2592,128]{1,0:T(8,128)} collective-permute-done((f32[2592,128]{1,0:T(8,128)}, f32[2592,128]{1,0:T(8,128)}, u32[]{:S(2)}, u32[]{:S(2)}) %collective-permute-start.5) | collective-permute-done | bytes 1327136 | tf_op jit(solution)/shard_map/ppermute | solution.py:54
  177.4 2.8 %copy.134 = f32[2592,128]{0,1:T(8,128)} copy(f32[2592,128]{1,0:T(8,128)} %collective-permute-done.5) | data formatting | bytes 2654208 | tf_op jit(solution)/shard_map/ppermute | solution.py:54
  180.2 2.8 %copy.136 = f32[2592,128]{0,1:T(8,128)} copy(f32[2592,128]{1,0:T(8,128)} %collective-permute-done.10) | data formatting | bytes 2654208 | tf_op jit(solution)/shard_map/ppermute | solution.py:54
  185.0 2.8 %copy.137 = f32[2592,128]{0,1:T(8,128)} copy(f32[2592,128]{1,0:T(8,128)} %collective-permute-done.11) | data formatting | bytes 2654208 | tf_op jit(solution)/shard_map/ppermute | solution.py:54
  190.4 5.9 %custom-call.8 = f32[2,32,32]{2,1,0:T(8,128)S(1)} custom-call(f32[2,32,32]{2,1,0:T(8,128)S(1)} %fusion.45), custom_call_target="Cholesky" | custom-call | tf_op jit(solution)/shard_map/jit(cholesky)/cholesky | solution.py:93
  196.5 4.9 %custom-call.9 = f32[2,1,32,32]{2,3,1,0:T(8,128)S(1)} custom-call(f32[2,1,32,32]{3,2,1,0:T(8,128)S(1)} %select_bitcast_fusion), custom_call_target="InvertDiagBlocksLowerTriangular" | custom-call | tf_op jit(solution)/shard_map/jit(_solve_triangular)/vmap()/triangular_solve | solution.py:94
  204.1 3.2 %fusion.5 = f32[2,2048,128]{1,2,0:T(8,128)} fusion(f32[1,2592,128]{1,2,0:T(8,128)S(1)} %add_bitcast_fusion.1, f32[1,2592,128]{1,2,0:T(8,128)S(1)} %add_bitcast_fusion, f32[2,32,2048]{2,1,0:T(8,128)S(1)} %fusion.29, s32[]{:T(128)S(6)} %select_n.200), kind=kOutput, calls=%fused_computation.23 | convolution fusion | flops 202375168 | bytes 5406724 | tf_op jit(solution)/shard_map/stp,stq->spq/dot_general | solution.py:96
  211.2 4.3 %copy.145 = f32[8,4,128,128]{3,1,2,0:T(4,128)} copy(f32[8,4,128,128]{3,2,1,0:T(8,128)} %bitcast.90) | data formatting | bytes 4194304 | tf_op jit(solution)/shard_map/reshape | solution.py:112
  215.4 4.4 %all-to-all-start = ((f32[8,4,128,128]{3,1,2,0:T(4,128)}), f32[8,4,128,128]{3,1,2,0:T(4,128)S(1)}, u32[]{:S(2)}, u32[]{:S(2)}) async-start(f32[8,4,128,128]{3,1,2,0:T(4,128)} %copy.145), calls=%async_computation | async-start | bytes 4194304 | tf_op jit(solution)/shard_map/all_to_all | solution.py:115
  220.0 27.1 %all-to-all-done = f32[8,4,128,128]{3,1,2,0:T(4,128)S(1)} async-done(((f32[8,4,128,128]{3,1,2,0:T(4,128)}), f32[8,4,128,128]{3,1,2,0:T(4,128)S(1)}, u32[]{:S(2)}, u32[]{:S(2)}) %all-to-all-start) | async-done | bytes 2097184 | tf_op jit(solution)/shard_map/all_to_all | solution.py:115
  247.6 6.9 %convolution_bitcast_fusion = f32[16,128,8,128]{3,0,2,1:T(8,128)S(1)} fusion(f32[32,128,128,1]{2,0,3,1:T(8,128)S(1)} %bitcast.91, f32[32,8]{0,1:T(8,128)S(1)} %fusion.63, f32[32,16]{0,1:T(8,128)S(1)} %fusion.61), kind=kOutput, calls=%fused_computation.13 | convolution fusion | flops 805310464 | bytes 10488832 | tf_op jit(solution)/shard_map/irkc,ixky->rxcy/dot_general | solution.py:124
  254.5 2.7 %copy.151 = f32[16,128,8,128]{3,2,1,0:T(8,128)S(1)} copy(f32[16,128,8,128]{3,0,2,1:T(8,128)S(1)} %convolution_bitcast_fusion) | data formatting | bytes 16777216 | tf_op jit(solution)/shard_map/irkc,ixky->rxcy/transpose | solution.py:124
  257.2 5.5 %copy.164 = f32[256,8,8,128]{3,1,2,0:T(8,128)} copy(f32[256,8,8,128]{3,2,1,0:T(8,128)S(1)} %bitcast.86) | data formatting | bytes 16777216
  (105 shorter events, 58.2 us)
Async XLA Ops:
  2.1 4.0 %copy-start.5 = (s32[2,256]{1,0:T(2,128)S(1)}, s32[2,256]{1,0:T(2,128)}, u32[]{:S(2)}) copy-start(s32[2,256]{1,0:T(2,128)} %param.7) | copy-start | bytes 6148
  15.3 8.7 %copy-start.6 = (s32[2,16]{1,0:T(2,128)S(1)}, s32[2,16]{1,0:T(2,128)}, u32[]{:S(2)}) copy-start(s32[2,16]{1,0:T(2,128)} %param.10) | copy-start | bytes 388
  15.3 9.4 %copy-start.7 = (s32[128]{0:T(128)S(1)}, s32[128]{0:T(128)}, u32[]{:S(2)}) copy-start(s32[128]{0:T(128)} %param.11) | copy-start | bytes 1540
  17.1 27.6 %collective-permute-start.2 = (bf16[1,256,2176]{1,2,0:T(8,128)(2,1)S(1)}, bf16[1,256,2176]{1,2,0:T(8,128)(2,1)}, u32[]{:S(2)}, u32[]{:S(2)}) collective-permute-start(bf16[1,256,2176]{1,2,0:T(8,128)(2,1)S(1)} %get-tuple-element.24), channel_id=1, source_target_pairs={{0,24},{8,0},{16,8},{24,16},{1,25},{9,1},{17,9},{25,17},{2,26},{10... | collective-permute-start | bytes 3342344 | tf_op jit(solution)/shard_map/ppermute | solution.py:54
  17.7 29.1 %collective-permute-start.1 = (bf16[1,256,2176]{1,2,0:T(8,128)(2,1)S(1)}, bf16[1,256,2176]{1,2,0:T(8,128)(2,1)}, u32[]{:S(2)}, u32[]{:S(2)}) collective-permute-start(bf16[1,256,2176]{1,2,0:T(8,128)(2,1)S(1)} %get-tuple-element.24), channel_id=1, source_target_pairs={{0,16},{8,24},{16,0},{24,8},{1,17},{9,25},{17,1},{25,9},{2,18},{10... | collective-permute-start | bytes 3342344 | tf_op jit(solution)/shard_map/ppermute | solution.py:54
  20.4 48.8 %collective-permute-start = (bf16[1,256,2176]{1,2,0:T(8,128)(2,1)S(1)}, bf16[1,256,2176]{1,2,0:T(8,128)(2,1)}, u32[]{:S(2)}, u32[]{:S(2)}) collective-permute-start(bf16[1,256,2176]{1,2,0:T(8,128)(2,1)S(1)} %get-tuple-element.24), channel_id=1, source_target_pairs={{0,8},{8,16},{16,24},{24,0},{1,9},{9,17},{17,25},{25,1},{2,10},{10... | collective-permute-start | bytes 3342344 | tf_op jit(solution)/shard_map/ppermute | solution.py:54
  20.4 61.2 %collective-permute-start.8 = (bf16[1,256,2176]{1,2,0:T(8,128)(2,1)S(1)}, bf16[1,256,2176]{1,2,0:T(8,128)(2,1)S(1)}, u32[]{:S(2)}, u32[]{:S(2)}) collective-permute-start(bf16[1,256,2176]{1,2,0:T(8,128)(2,1)S(1)} %get-tuple-element.23), channel_id=1, source_target_pairs={{0,96},{32,0},{64,32},{96,64},{1,97},{33,1},{65,33},{97,65},{2,98}... | collective-permute-start | bytes 3342344 | tf_op jit(solution)/shard_map/ppermute | solution.py:54
  23.4 58.2 %collective-permute-start.7 = (bf16[1,256,2176]{1,2,0:T(8,128)(2,1)S(1)}, bf16[1,256,2176]{1,2,0:T(8,128)(2,1)}, u32[]{:S(2)}, u32[]{:S(2)}) collective-permute-start(bf16[1,256,2176]{1,2,0:T(8,128)(2,1)S(1)} %get-tuple-element.23), channel_id=1, source_target_pairs={{0,64},{32,96},{64,0},{96,32},{1,65},{33,97},{65,1},{97,33},{2,66}... | collective-permute-start | bytes 3342344 | tf_op jit(solution)/shard_map/ppermute | solution.py:54
  44.7 36.9 %collective-permute-start.6 = (bf16[1,256,2176]{1,2,0:T(8,128)(2,1)S(1)}, bf16[1,256,2176]{1,2,0:T(8,128)(2,1)S(1)}, u32[]{:S(2)}, u32[]{:S(2)}) collective-permute-start(bf16[1,256,2176]{1,2,0:T(8,128)(2,1)S(1)} %get-tuple-element.23), channel_id=1, source_target_pairs={{0,32},{32,64},{64,96},{96,0},{1,33},{33,65},{65,97},{97,1},{2,34}... | collective-permute-start | bytes 3342344 | tf_op jit(solution)/shard_map/ppermute | solution.py:54
  74.0 4.0 %copy-start.1 = (f32[32,16,128]{2,0,1:T(8,128)}, f32[32,16,128]{2,0,1:T(8,128)S(1)}, u32[]{:S(2)}) copy-start(f32[32,16,128]{2,0,1:T(8,128)S(1)} %fusion.37) | copy-start | bytes 786436
  80.0 39.4 %collective-permute-start.3 = (f32[2592,128]{1,0:T(8,128)}, f32[2592,128]{1,0:T(8,128)}, u32[]{:S(2)}, u32[]{:S(2)}) collective-permute-start(f32[2592,128]{1,0:T(8,128)} %get-tuple-element.29), channel_id=1, source_target_pairs={{0,32},{32,64},{64,96},{96,0},{1,33},{33,65},{65,97},{97,1},{2,34}... | collective-permute-start | bytes 3981320 | tf_op jit(solution)/shard_map/ppermute | solution.py:54
  90.5 2.2 copy-start.3
  90.6 30.3 %copy-start = (f32[2048,128]{1,0:T(8,128)S(1)}, f32[2048,128]{1,0:T(8,128)}, u32[]{:S(2)}) copy-start(f32[2048,128]{1,0:T(8,128)} %get-tuple-element.18) | copy-start | bytes 3145732
  90.6 30.3 %copy-start.2 = (f32[32,16,128]{2,0,1:T(8,128)S(1)}, f32[32,16,128]{2,0,1:T(8,128)}, u32[]{:S(2)}) copy-start(f32[32,16,128]{2,0,1:T(8,128)} %copy-done.1) | copy-start | bytes 786436
  92.7 46.7 %collective-permute-start.9 = (f32[2592,128]{1,0:T(8,128)}, f32[2592,128]{1,0:T(8,128)}, u32[]{:S(2)}, u32[]{:S(2)}) collective-permute-start(f32[2592,128]{1,0:T(8,128)} %get-tuple-element.26), channel_id=1, source_target_pairs={{0,8},{8,16},{16,24},{24,0},{1,9},{9,17},{17,25},{25,1},{2,10},{10... | collective-permute-start | bytes 3981320 | tf_op jit(solution)/shard_map/ppermute | solution.py:54
  110.9 104.6 %all-to-all-start.1 = ((s32[8,4,2]{1,2,0:T(2,128)}), s32[8,4,2]{1,2,0:T(2,128)S(1)}, u32[]{:S(2)}, u32[]{:S(2)}) async-start(s32[8,4,2]{1,2,0:T(2,128)} %copy.149), calls=%async_computation.1 | async-start | bytes 16384 | tf_op jit(solution)/shard_map/all_to_all | solution.py:116
  116.3 33.4 %collective-permute-start.4 = (f32[2592,128]{1,0:T(8,128)}, f32[2592,128]{1,0:T(8,128)}, u32[]{:S(2)}, u32[]{:S(2)}) collective-permute-start(f32[2592,128]{1,0:T(8,128)} %get-tuple-element.28), channel_id=1, source_target_pairs={{0,64},{32,96},{64,0},{96,32},{1,65},{33,97},{65,1},{97,33},{2,66}... | collective-permute-start | bytes 3981320 | tf_op jit(solution)/shard_map/ppermute | solution.py:54
  118.4 59.0 %collective-permute-start.5 = (f32[2592,128]{1,0:T(8,128)}, f32[2592,128]{1,0:T(8,128)}, u32[]{:S(2)}, u32[]{:S(2)}) collective-permute-start(f32[2592,128]{1,0:T(8,128)} %get-tuple-element.30), channel_id=1, source_target_pairs={{0,96},{32,0},{64,32},{96,64},{1,97},{33,1},{65,33},{97,65},{2,98}... | collective-permute-start | bytes 3981320 | tf_op jit(solution)/shard_map/ppermute | solution.py:54
  119.4 60.8 %collective-permute-start.10 = (f32[2592,128]{1,0:T(8,128)}, f32[2592,128]{1,0:T(8,128)}, u32[]{:S(2)}, u32[]{:S(2)}) collective-permute-start(f32[2592,128]{1,0:T(8,128)} %get-tuple-element.25), channel_id=1, source_target_pairs={{0,16},{8,24},{16,0},{24,8},{1,17},{9,25},{17,1},{25,9},{2,18},{10... | collective-permute-start | bytes 3981320 | tf_op jit(solution)/shard_map/ppermute | solution.py:54
  119.4 65.6 %collective-permute-start.11 = (f32[2592,128]{1,0:T(8,128)}, f32[2592,128]{1,0:T(8,128)}, u32[]{:S(2)}, u32[]{:S(2)}) collective-permute-start(f32[2592,128]{1,0:T(8,128)} %get-tuple-element.27), channel_id=1, source_target_pairs={{0,24},{8,0},{16,8},{24,16},{1,25},{9,1},{17,9},{25,17},{2,26},{10... | collective-permute-start | bytes 3981320 | tf_op jit(solution)/shard_map/ppermute | solution.py:54
  122.4 17.1 %copy-start.4 = (f32[32,16,128]{2,0,1:T(8,128)S(1)}, f32[32,16,128]{2,0,1:T(8,128)}, u32[]{:S(2)}) copy-start(f32[32,16,128]{2,0,1:T(8,128)} %copy-done.3) | copy-start | bytes 786436
  215.4 31.6 %all-to-all-start = ((f32[8,4,128,128]{3,1,2,0:T(4,128)}), f32[8,4,128,128]{3,1,2,0:T(4,128)S(1)}, u32[]{:S(2)}, u32[]{:S(2)}) async-start(f32[8,4,128,128]{3,1,2,0:T(4,128)} %copy.145), calls=%async_computation | async-start | bytes 4194304 | tf_op jit(solution)/shard_map/all_to_all | solution.py:115

commit v6 on v5

--- a/solution.py
+++ b/solution.py
@@ -1,6 +1,8 @@
 import jax
 import jax.numpy as jnp
 from jax import lax
+from jax.experimental import pallas as pl
+from jax.experimental.pallas import tpu as pltpu
 from jax.sharding import Mesh, PartitionSpec as P
 
 DEG_MAX = 8
@@ -116,13 +118,38 @@
         lax.all_to_all(send_labels, "tile", split_axis=0, concat_axis=0, tiled=True),
     )
     item_total = n_tile * capacity
-    recv_rows = recv_rows.reshape(item_total, tile_pixels, k_cols, tile_pixels)
+    recv_rows = recv_rows.reshape(item_total, tile_pixels, tile_pixels)
     recv_labels = recv_labels.reshape(item_total, 1 + k_cols)
-    row_select = (recv_labels[:, 0:1] == jnp.arange(n_scan)[None, :]).astype(jnp.float32)
-    col_select = (recv_labels[:, 1:, None] == jnp.arange(n_tile)[None, None, :]).astype(jnp.float32)
-    placing = row_select[:, :, None, None] * col_select[:, None, :, :]
-    placed = jnp.einsum("irkc,ixky->rxcy", placing, recv_rows, precision=lax.Precision.HIGHEST)
-    return placed.reshape(n_scan * tile_pixels, n_tile * tile_pixels)
+    return place(recv_rows, recv_labels[:, 0], recv_labels[:, 1], n_scan, n_tile)
+
+
+def place(recv, row_block, col_block, n_rows, n_cols):
+    items, tile_pixels, _ = recv.shape
+
+    def kernel(row_ref, col_ref, recv_ref, out_ref):
+        r = pl.program_id(0)
+        out_ref[...] = jnp.zeros(out_ref.shape, out_ref.dtype)
+
+        def body(i, carry):
+            for c in range(n_cols):
+                @pl.when(jnp.logical_and(row_ref[i] == r, col_ref[i] == c))
+                def _():
+                    out_ref[:, c * tile_pixels : (c + 1) * tile_pixels] += recv_ref[i]
+
+            return carry
+
+        lax.fori_loop(0, items, body, 0)
+
+    return pl.pallas_call(
+        kernel,
+        grid_spec=pltpu.PrefetchScalarGridSpec(
+            num_scalar_prefetch=2,
+            grid=(n_rows,),
+            in_specs=[pl.BlockSpec((items, tile_pixels, tile_pixels), lambda r, a, b: (0, 0, 0))],
+            out_specs=pl.BlockSpec((tile_pixels, n_cols * tile_pixels), lambda r, a, b: (r, 0)),
+        ),
+        out_shape=jax.ShapeDtypeStruct((n_rows * tile_pixels, n_cols * tile_pixels), jnp.float32),
+    )(row_block, col_block, recv)
 
 
 def solution(mesh):

time: 264 us -> 291 us (1.10)
  the two profiles are of different devices: /device:TPU:4 before, /device:TPU:1 now
where the time goes in v6:
time: 291 us; the launch traced here: 285 us
  waiting for transfers between devices  108 us (37%)
  Pallas kernels  45.9 us (16%)
  starting transfers between devices  44.1 us (15%)
  local copies, waits for them, and re-layouts  39 us (13%)
  other arithmetic  35.1 us (12%)
  matrix products  12.5 us (4%)
    ppermute x12, waiting for transfers between devices, shifted(): return lax.ppermute(x, axis, [(i, (i + d) % n) for i in range(n)])  82.7 us
    pallas_call x1, Pallas kernels, place(): pl.pallas_call(kernel, grid_spec=pltpu.PrefetchScalarGridSpec(num_scalar_...  45.9 us
    ppermute x12, starting transfers between devices, shifted(): return lax.ppermute(x, axis, [(i, (i + d) % n) for i in range(n)])  31.7 us
    all_to_all x1, waiting for transfers between devices, per_device(): lax.all_to_all(send_rows, 'tile', split_axis=0, concat_axis=0, tiled=True)  25.5 us
    ppermute x4, local copies, waits for them, and re-layouts, shifted(): return lax.ppermute(x, axis, [(i, (i + d) % n) for i in range(n)])  11.4 us
    concatenate x1, local copies, waits for them, and re-layouts, per_device(): local = jnp.concatenate([masked, template, pad], axis=2)  7.35 us
    all_to_all x1, starting transfers between devices, per_device(): lax.all_to_all(send_labels, 'tile', split_axis=0, concat_axis=0, tiled=True)  6.53 us
    another operation x4, other arithmetic, per_device(): factor = jnp.linalg.cholesky(normal)  6.03 us
  transfers between devices with their start and end apart: 14, of which 8 were waited for; matrix products, arithmetic and copies ran while one was open for 24% of the time, Pallas kernels for 0%

profile of v6, /device:TPU:1, one launch (start us, length us, event | category | flops | bytes accessed | tf_op | source)
XLA Modules:
  0.0 285.1 jit_solution(6703805420615059773)
XLA Ops:
  2.1 3.9 %copy.127 = bf16[2,256,2048]{1,2,0:T(8,128)(2,1)} copy(bf16[2,256,2048]{2,1,0:T(8,128)(2,1)} %param.6) | data formatting | bytes 4194304 | tf_op args[0]
  8.0 7.3 %concatenate.46 = bf16[2,256,2176]{1,2,0:T(8,128)(2,1)} concatenate(bf16[2,256,2048]{1,2,0:T(8,128)(2,1)S(1)} %broadcast_select_fusion, bf16[2,256,1]{1,2,0:T(2,128)(2,1)S(1)} %get-tuple-element.38, bf16[2,256,1]{1,2,0:T(2,128)(2,1)S(1)} %get-tuple-element.37, bf16[2,256,1]{1,2,0:T(2,128)(2,1)S(1)} %get-tuple-element.36, bf16[2,256,1]{1,2,0:T(2,128)(2,1)S(1)} %get-tuple-element.35, ...), dimensions={2} | concatenate | bytes 4456448 | tf_op jit(solution)/shard_map/concatenate | solution.py:53
  17.1 3.4 %collective-permute-start.2 = (bf16[1,256,2176]{1,2,0:T(8,128)(2,1)S(1)}, bf16[1,256,2176]{1,2,0:T(8,128)(2,1)}, u32[]{:S(2)}, u32[]{:S(2)}) collective-permute-start(bf16[1,256,2176]{1,2,0:T(8,128)(2,1)S(1)} %get-tuple-element.24), channel_id=1, source_target_pairs={{0,24},{8,0},{16,8},{24,16},{1,25},{9,1},{17,9},{25,17},{2,26},{10... | collective-permute-start | bytes 3342344 | tf_op jit(solution)/shard_map/ppermute | solution.py:56
  21.6 2.7 collective-permute-start.8
  27.1 17.7 %collective-permute-done.2 = bf16[1,256,2176]{1,2,0:T(8,128)(2,1)} collective-permute-done((bf16[1,256,2176]{1,2,0:T(8,128)(2,1)S(1)}, bf16[1,256,2176]{1,2,0:T(8,128)(2,1)}, u32[]{:S(2)}, u32[]{:S(2)}) %collective-permute-start.2) | collective-permute-done | bytes 1114144 | tf_op jit(solution)/shard_map/ppermute | solution.py:56
  47.3 25.1 %collective-permute-done = bf16[1,256,2176]{1,2,0:T(8,128)(2,1)} collective-permute-done((bf16[1,256,2176]{1,2,0:T(8,128)(2,1)S(1)}, bf16[1,256,2176]{1,2,0:T(8,128)(2,1)}, u32[]{:S(2)}, u32[]{:S(2)}) %collective-permute-start) | collective-permute-done | bytes 1114144 | tf_op jit(solution)/shard_map/ppermute | solution.py:56
  84.6 2.6 pad_maximum_fusion.1
  97.0 6.5 %all-to-all-start = ((s32[8,4,2]{1,2,0:T(2,128)}), s32[8,4,2]{1,2,0:T(2,128)S(1)}, u32[]{:S(2)}, u32[]{:S(2)}) async-start(s32[8,4,2]{1,2,0:T(2,128)} %copy.125), calls=%async_computation | async-start | bytes 16384 | tf_op jit(solution)/shard_map/all_to_all | solution.py:118
  107.0 16.1 %collective-permute-start.10 = (f32[2592,128]{1,0:T(8,128)}, f32[2592,128]{1,0:T(8,128)}, u32[]{:S(2)}, u32[]{:S(2)}) collective-permute-start(f32[2592,128]{1,0:T(8,128)} %get-tuple-element.25), channel_id=1, source_target_pairs={{0,16},{8,24},{16,0},{24,8},{1,17},{9,25},{17,1},{25,9},{2,18},{10... | collective-permute-start | bytes 3981320 | tf_op jit(solution)/shard_map/ppermute | solution.py:56
  123.1 2.5 collective-permute-start.11
  127.5 6.2 %collective-permute-done.9 = f32[2592,128]{1,0:T(8,128)} collective-permute-done((f32[2592,128]{1,0:T(8,128)}, f32[2592,128]{1,0:T(8,128)}, u32[]{:S(2)}, u32[]{:S(2)}) %collective-permute-start.9) | collective-permute-done | bytes 1327136 | tf_op jit(solution)/shard_map/ppermute | solution.py:56
  137.0 7.6 %collective-permute-done.4 = f32[2592,128]{1,0:T(8,128)} collective-permute-done((f32[2592,128]{1,0:T(8,128)}, f32[2592,128]{1,0:T(8,128)}, u32[]{:S(2)}, u32[]{:S(2)}) %collective-permute-start.4) | collective-permute-done | bytes 1327136 | tf_op jit(solution)/shard_map/ppermute | solution.py:56
  144.7 2.8 copy.129
  147.5 16.3 %collective-permute-done.5 = f32[2592,128]{1,0:T(8,128)} collective-permute-done((f32[2592,128]{1,0:T(8,128)}, f32[2592,128]{1,0:T(8,128)}, u32[]{:S(2)}, u32[]{:S(2)}) %collective-permute-start.5) | collective-permute-done | bytes 1327136 | tf_op jit(solution)/shard_map/ppermute | solution.py:56
  163.9 2.8 copy.130
  166.7 2.8 copy.132
  171.5 8.2 %collective-permute-done.11 = f32[2592,128]{1,0:T(8,128)} collective-permute-done((f32[2592,128]{1,0:T(8,128)}, f32[2592,128]{1,0:T(8,128)}, u32[]{:S(2)}, u32[]{:S(2)}) %collective-permute-start.11) | collective-permute-done | bytes 1327136 | tf_op jit(solution)/shard_map/ppermute | solution.py:56
  179.7 2.8 copy.133
  185.0 5.9 %custom-call.8 = f32[2,32,32]{2,1,0:T(8,128)S(1)} custom-call(f32[2,32,32]{2,1,0:T(8,128)S(1)} %fusion.43), custom_call_target="Cholesky" | custom-call | tf_op jit(solution)/shard_map/jit(cholesky)/cholesky | solution.py:95
  191.1 4.9 %custom-call.9 = f32[2,1,32,32]{2,3,1,0:T(8,128)S(1)} custom-call(f32[2,1,32,32]{3,2,1,0:T(8,128)S(1)} %select_bitcast_fusion), custom_call_target="InvertDiagBlocksLowerTriangular" | custom-call | tf_op jit(solution)/shard_map/jit(_solve_triangular)/vmap()/triangular_solve | solution.py:96
  198.7 3.2 %fusion.5 = f32[2,2048,128]{1,2,0:T(8,128)} fusion(f32[1,2592,128]{1,2,0:T(8,128)S(1)} %add_bitcast_fusion.1, f32[1,2592,128]{1,2,0:T(8,128)S(1)} %add_bitcast_fusion, f32[2,32,2048]{2,1,0:T(8,128)S(1)} %fusion.29, s32[]{:T(128)S(6)} %select_n.204), kind=kOutput, calls=%fused_computation.21 | convolution fusion | flops 202375168 | bytes 5406724 | tf_op jit(solution)/shard_map/stp,stq->spq/dot_general | solution.py:98
  205.8 5.8 %all-to-all-start.1 = ((f32[8,4,128,128]{3,2,1,0:T(8,128)}), f32[8,4,128,128]{3,2,1,0:T(8,128)S(1)}, u32[]{:S(2)}, u32[]{:S(2)}) async-start(f32[8,4,128,128]{3,2,1,0:T(8,128)} %bitcast.29), calls=%async_computation.1 | async-start | bytes 4194304 | tf_op jit(solution)/shard_map/all_to_all | solution.py:117
  212.3 25.5 %all-to-all-done.1 = f32[8,4,128,128]{3,2,1,0:T(8,128)S(1)} async-done(((f32[8,4,128,128]{3,2,1,0:T(8,128)}), f32[8,4,128,128]{3,2,1,0:T(8,128)S(1)}, u32[]{:S(2)}, u32[]{:S(2)}) %all-to-all-start.1) | async-done | bytes 2097184 | tf_op jit(solution)/shard_map/all_to_all | solution.py:117
  239.2 45.9 %shard_map.64 = f32[2048,1024]{1,0:T(8,128)} custom-call(s32[32]{0:T(128)} %get-tuple-element.40.row_ref, s32[32]{0:T(128)} %get-tuple-element.39.col_ref, f32[32,128,128]{2,1,0:T(8,128)} %bitcast.74), custom_call_target="tpu_custom_call" | custom-call | tf_op jit(solution)/shard_map/pallas_call | solution.py:143
  (101 shorter events, 56.0 us)
Async XLA Ops:
  2.1 4.0 %copy-start.6 = (s32[2,256]{1,0:T(2,128)S(1)}, s32[2,256]{1,0:T(2,128)}, u32[]{:S(2)}) copy-start(s32[2,256]{1,0:T(2,128)} %param.7) | copy-start | bytes 6148
  15.3 9.3 %copy-start.7 = (s32[2,16]{1,0:T(2,128)S(1)}, s32[2,16]{1,0:T(2,128)}, u32[]{:S(2)}) copy-start(s32[2,16]{1,0:T(2,128)} %param.10) | copy-start | bytes 388
  15.3 10.0 %copy-start.8 = (s32[128]{0:T(128)S(1)}, s32[128]{0:T(128)}, u32[]{:S(2)}) copy-start(s32[128]{0:T(128)} %param.11) | copy-start | bytes 1540
  17.1 27.7 %collective-permute-start.2 = (bf16[1,256,2176]{1,2,0:T(8,128)(2,1)S(1)}, bf16[1,256,2176]{1,2,0:T(8,128)(2,1)}, u32[]{:S(2)}, u32[]{:S(2)}) collective-permute-start(bf16[1,256,2176]{1,2,0:T(8,128)(2,1)S(1)} %get-tuple-element.24), channel_id=1, source_target_pairs={{0,24},{8,0},{16,8},{24,16},{1,25},{9,1},{17,9},{25,17},{2,26},{10... | collective-permute-start | bytes 3342344 | tf_op jit(solution)/shard_map/ppermute | solution.py:56
  20.5 26.8 %collective-permute-start.1 = (bf16[1,256,2176]{1,2,0:T(8,128)(2,1)S(1)}, bf16[1,256,2176]{1,2,0:T(8,128)(2,1)}, u32[]{:S(2)}, u32[]{:S(2)}) collective-permute-start(bf16[1,256,2176]{1,2,0:T(8,128)(2,1)S(1)} %get-tuple-element.24), channel_id=1, source_target_pairs={{0,16},{8,24},{16,0},{24,8},{1,17},{9,25},{17,1},{25,9},{2,18},{10... | collective-permute-start | bytes 3342344 | tf_op jit(solution)/shard_map/ppermute | solution.py:56
  21.0 51.4 %collective-permute-start = (bf16[1,256,2176]{1,2,0:T(8,128)(2,1)S(1)}, bf16[1,256,2176]{1,2,0:T(8,128)(2,1)}, u32[]{:S(2)}, u32[]{:S(2)}) collective-permute-start(bf16[1,256,2176]{1,2,0:T(8,128)(2,1)S(1)} %get-tuple-element.24), channel_id=1, source_target_pairs={{0,8},{8,16},{16,24},{24,0},{1,9},{9,17},{17,25},{25,1},{2,10},{10... | collective-permute-start | bytes 3342344 | tf_op jit(solution)/shard_map/ppermute | solution.py:56
  21.6 63.0 %collective-permute-start.8 = (bf16[1,256,2176]{1,2,0:T(8,128)(2,1)S(1)}, bf16[1,256,2176]{1,2,0:T(8,128)(2,1)S(1)}, u32[]{:S(2)}, u32[]{:S(2)}) collective-permute-start(bf16[1,256,2176]{1,2,0:T(8,128)(2,1)S(1)} %get-tuple-element.23), channel_id=1, source_target_pairs={{0,96},{32,0},{64,32},{96,64},{1,97},{33,1},{65,33},{97,65},{2,98}... | collective-permute-start | bytes 3342344 | tf_op jit(solution)/shard_map/ppermute | solution.py:56
  24.3 60.3 %collective-permute-start.7 = (bf16[1,256,2176]{1,2,0:T(8,128)(2,1)S(1)}, bf16[1,256,2176]{1,2,0:T(8,128)(2,1)}, u32[]{:S(2)}, u32[]{:S(2)}) collective-permute-start(bf16[1,256,2176]{1,2,0:T(8,128)(2,1)S(1)} %get-tuple-element.23), channel_id=1, source_target_pairs={{0,64},{32,96},{64,0},{96,32},{1,65},{33,97},{65,1},{97,33},{2,66}... | collective-permute-start | bytes 3342344 | tf_op jit(solution)/shard_map/ppermute | solution.py:56
  44.8 39.8 %collective-permute-start.6 = (bf16[1,256,2176]{1,2,0:T(8,128)(2,1)S(1)}, bf16[1,256,2176]{1,2,0:T(8,128)(2,1)S(1)}, u32[]{:S(2)}, u32[]{:S(2)}) collective-permute-start(bf16[1,256,2176]{1,2,0:T(8,128)(2,1)S(1)} %get-tuple-element.23), channel_id=1, source_target_pairs={{0,32},{32,64},{64,96},{96,0},{1,33},{33,65},{65,97},{97,1},{2,34}... | collective-permute-start | bytes 3342344 | tf_op jit(solution)/shard_map/ppermute | solution.py:56
  77.2 4.0 %copy-start.2 = (f32[32,16,128]{2,0,1:T(8,128)}, f32[32,16,128]{2,0,1:T(8,128)S(1)}, u32[]{:S(2)}) copy-start(f32[32,16,128]{2,0,1:T(8,128)S(1)} %fusion.36) | copy-start | bytes 786436
  83.3 39.8 %collective-permute-start.3 = (f32[2592,128]{1,0:T(8,128)}, f32[2592,128]{1,0:T(8,128)}, u32[]{:S(2)}, u32[]{:S(2)}) collective-permute-start(f32[2592,128]{1,0:T(8,128)} %get-tuple-element.29), channel_id=1, source_target_pairs={{0,32},{32,64},{64,96},{96,0},{1,33},{33,65},{65,97},{97,1},{2,34}... | collective-permute-start | bytes 3981320 | tf_op jit(solution)/shard_map/ppermute | solution.py:56
  93.5 2.2 copy-start.4
  93.6 32.0 %copy-start.1 = (f32[2048,128]{1,0:T(8,128)S(1)}, f32[2048,128]{1,0:T(8,128)}, u32[]{:S(2)}) copy-start(f32[2048,128]{1,0:T(8,128)} %get-tuple-element.18) | copy-start | bytes 3145732
  93.6 32.0 %copy-start.3 = (f32[32,16,128]{2,0,1:T(8,128)S(1)}, f32[32,16,128]{2,0,1:T(8,128)}, u32[]{:S(2)}) copy-start(f32[32,16,128]{2,0,1:T(8,128)} %copy-done.2) | copy-start | bytes 786436
  95.7 38.0 %collective-permute-start.9 = (f32[2592,128]{1,0:T(8,128)}, f32[2592,128]{1,0:T(8,128)}, u32[]{:S(2)}, u32[]{:S(2)}) collective-permute-start(f32[2592,128]{1,0:T(8,128)} %get-tuple-element.26), channel_id=1, source_target_pairs={{0,8},{8,16},{16,24},{24,0},{1,9},{9,17},{17,25},{25,1},{2,10},{10... | collective-permute-start | bytes 3981320 | tf_op jit(solution)/shard_map/ppermute | solution.py:56
  97.0 108.8 %all-to-all-start = ((s32[8,4,2]{1,2,0:T(2,128)}), s32[8,4,2]{1,2,0:T(2,128)S(1)}, u32[]{:S(2)}, u32[]{:S(2)}) async-start(s32[8,4,2]{1,2,0:T(2,128)} %copy.125), calls=%async_computation | async-start | bytes 16384 | tf_op jit(solution)/shard_map/all_to_all | solution.py:118
  103.7 41.0 %collective-permute-start.4 = (f32[2592,128]{1,0:T(8,128)}, f32[2592,128]{1,0:T(8,128)}, u32[]{:S(2)}, u32[]{:S(2)}) collective-permute-start(f32[2592,128]{1,0:T(8,128)} %get-tuple-element.28), channel_id=1, source_target_pairs={{0,64},{32,96},{64,0},{96,32},{1,65},{33,97},{65,1},{97,33},{2,66}... | collective-permute-start | bytes 3981320 | tf_op jit(solution)/shard_map/ppermute | solution.py:56
  105.9 57.9 %collective-permute-start.5 = (f32[2592,128]{1,0:T(8,128)}, f32[2592,128]{1,0:T(8,128)}, u32[]{:S(2)}, u32[]{:S(2)}) collective-permute-start(f32[2592,128]{1,0:T(8,128)} %get-tuple-element.30), channel_id=1, source_target_pairs={{0,96},{32,0},{64,32},{96,64},{1,97},{33,1},{65,33},{97,65},{2,98}... | collective-permute-start | bytes 3981320 | tf_op jit(solution)/shard_map/ppermute | solution.py:56
  107.0 59.7 %collective-permute-start.10 = (f32[2592,128]{1,0:T(8,128)}, f32[2592,128]{1,0:T(8,128)}, u32[]{:S(2)}, u32[]{:S(2)}) collective-permute-start(f32[2592,128]{1,0:T(8,128)} %get-tuple-element.25), channel_id=1, source_target_pairs={{0,16},{8,24},{16,0},{24,8},{1,17},{9,25},{17,1},{25,9},{2,18},{10... | collective-permute-start | bytes 3981320 | tf_op jit(solution)/shard_map/ppermute | solution.py:56
  123.1 56.6 %collective-permute-start.11 = (f32[2592,128]{1,0:T(8,128)}, f32[2592,128]{1,0:T(8,128)}, u32[]{:S(2)}, u32[]{:S(2)}) collective-permute-start(f32[2592,128]{1,0:T(8,128)} %get-tuple-element.27), channel_id=1, source_target_pairs={{0,24},{8,0},{16,8},{24,16},{1,25},{9,1},{17,9},{25,17},{2,26},{10... | collective-permute-start | bytes 3981320 | tf_op jit(solution)/shard_map/ppermute | solution.py:56
  127.0 6.6 %copy-start.5 = (f32[32,16,128]{2,0,1:T(8,128)S(1)}, f32[32,16,128]{2,0,1:T(8,128)}, u32[]{:S(2)}) copy-start(f32[32,16,128]{2,0,1:T(8,128)} %copy-done.4) | copy-start | bytes 786436
  205.8 32.0 %all-to-all-start.1 = ((f32[8,4,128,128]{3,2,1,0:T(8,128)}), f32[8,4,128,128]{3,2,1,0:T(8,128)S(1)}, u32[]{:S(2)}, u32[]{:S(2)}) async-start(f32[8,4,128,128]{3,2,1,0:T(8,128)} %bitcast.29), calls=%async_computation.1 | async-start | bytes 4194304 | tf_op jit(solution)/shard_map/all_to_all | solution.py:117
  237.9 1.3 copy-start

commit v7 on v6

--- a/solution.py
+++ b/solution.py
@@ -130,15 +130,11 @@
         r = pl.program_id(0)
         out_ref[...] = jnp.zeros(out_ref.shape, out_ref.dtype)
 
-        def body(i, carry):
-            for c in range(n_cols):
-                @pl.when(jnp.logical_and(row_ref[i] == r, col_ref[i] == c))
-                def _():
-                    out_ref[:, c * tile_pixels : (c + 1) * tile_pixels] += recv_ref[i]
-
-            return carry
-
-        lax.fori_loop(0, items, body, 0)
+        for i in range(items):
+            @pl.when(row_ref[i] == r)
+            def _():
+                at = pl.ds(pl.multiple_of(col_ref[i] * tile_pixels, tile_pixels), tile_pixels)
+                out_ref[:, at] += recv_ref[i]
 
     return pl.pallas_call(
         kernel,

time: 291 us -> 256 us (0.88)
  the two profiles are of different devices: /device:TPU:1 before, /device:TPU:4 now
where the time goes in v7:
time: 256 us
  waiting for transfers between devices  116 us (45%)
  starting transfers between devices  41.3 us (16%)
  local copies, waits for them, and re-layouts  39 us (15%)
  other arithmetic  35.1 us (14%)
  matrix products  12.5 us (5%)
  Pallas kernels  11.5 us (4%)
    ppermute x12, waiting for transfers between devices, shifted(): return lax.ppermute(x, axis, [(i, (i + d) % n) for i in range(n)])  89.4 us
    ppermute x12, starting transfers between devices, shifted(): return lax.ppermute(x, axis, [(i, (i + d) % n) for i in range(n)])  31.5 us
    all_to_all x1, waiting for transfers between devices, per_device(): lax.all_to_all(send_rows, 'tile', split_axis=0, concat_axis=0, tiled=True)  26.5 us
    pallas_call x1, Pallas kernels, place(): pl.pallas_call(kernel, grid_spec=pltpu.PrefetchScalarGridSpec(num_scalar_...  11.5 us
    ppermute x4, local copies, waits for them, and re-layouts, shifted(): return lax.ppermute(x, axis, [(i, (i + d) % n) for i in range(n)])  11.4 us
    concatenate x1, local copies, waits for them, and re-layouts, per_device(): local = jnp.concatenate([masked, template, pad], axis=2)  7.35 us
    another operation x4, other arithmetic, per_device(): factor = jnp.linalg.cholesky(normal)  6.03 us
    all_to_all x1, starting transfers between devices, per_device(): lax.all_to_all(send_labels, 'tile', split_axis=0, concat_axis=0, tiled=True)  5.31 us
  transfers between devices with their start and end apart: 14, of which 7 were waited for; matrix products, arithmetic and copies ran while one was open for 27% of the time, Pallas kernels for 0%

profile of v7, /device:TPU:4, one launch (start us, length us, event | category | flops | bytes accessed | tf_op | source)
XLA Modules:
  0.0 255.6 jit_solution(15803879881077045302)
XLA Ops:
  2.1 3.9 %copy.127 = bf16[2,256,2048]{1,2,0:T(8,128)(2,1)} copy(bf16[2,256,2048]{2,1,0:T(8,128)(2,1)} %param.6) | data formatting | bytes 4194304 | tf_op args[0]
  8.0 7.3 %concatenate.46 = bf16[2,256,2176]{1,2,0:T(8,128)(2,1)} concatenate(bf16[2,256,2048]{1,2,0:T(8,128)(2,1)S(1)} %broadcast_select_fusion, bf16[2,256,1]{1,2,0:T(2,128)(2,1)S(1)} %get-tuple-element.38, bf16[2,256,1]{1,2,0:T(2,128)(2,1)S(1)} %get-tuple-element.37, bf16[2,256,1]{1,2,0:T(2,128)(2,1)S(1)} %get-tuple-element.36, bf16[2,256,1]{1,2,0:T(2,128)(2,1)S(1)} %get-tuple-element.35, ...), dimensions={2} | concatenate | bytes 4456448 | tf_op jit(solution)/shard_map/concatenate | solution.py:53
  17.7 2.7 %collective-permute-start.1 = (bf16[1,256,2176]{1,2,0:T(8,128)(2,1)S(1)}, bf16[1,256,2176]{1,2,0:T(8,128)(2,1)}, u32[]{:S(2)}, u32[]{:S(2)}) collective-permute-start(bf16[1,256,2176]{1,2,0:T(8,128)(2,1)S(1)} %get-tuple-element.24), channel_id=1, source_target_pairs={{0,16},{8,24},{16,0},{24,8},{1,17},{9,25},{17,1},{25,9},{2,18},{10... | collective-permute-start | bytes 3342344 | tf_op jit(solution)/shard_map/ppermute | solution.py:56
  20.4 3.0 %collective-permute-start.8 = (bf16[1,256,2176]{1,2,0:T(8,128)(2,1)S(1)}, bf16[1,256,2176]{1,2,0:T(8,128)(2,1)S(1)}, u32[]{:S(2)}, u32[]{:S(2)}) collective-permute-start(bf16[1,256,2176]{1,2,0:T(8,128)(2,1)S(1)} %get-tuple-element.23), channel_id=1, source_target_pairs={{0,96},{32,0},{64,32},{96,64},{1,97},{33,1},{65,33},{97,65},{2,98}... | collective-permute-start | bytes 3342344 | tf_op jit(solution)/shard_map/ppermute | solution.py:56
  26.5 18.2 %collective-permute-done.2 = bf16[1,256,2176]{1,2,0:T(8,128)(2,1)} collective-permute-done((bf16[1,256,2176]{1,2,0:T(8,128)(2,1)S(1)}, bf16[1,256,2176]{1,2,0:T(8,128)(2,1)}, u32[]{:S(2)}, u32[]{:S(2)}) %collective-permute-start.2) | collective-permute-done | bytes 1114144 | tf_op jit(solution)/shard_map/ppermute | solution.py:56
  46.8 22.4 %collective-permute-done = bf16[1,256,2176]{1,2,0:T(8,128)(2,1)} collective-permute-done((bf16[1,256,2176]{1,2,0:T(8,128)(2,1)S(1)}, bf16[1,256,2176]{1,2,0:T(8,128)(2,1)}, u32[]{:S(2)}, u32[]{:S(2)}) %collective-permute-start) | collective-permute-done | bytes 1114144 | tf_op jit(solution)/shard_map/ppermute | solution.py:56
  74.1 2.4 fusion.2
  81.6 2.6 %pad_maximum_fusion.1 = bf16[1,1024,2176]{1,2,0:T(8,128)(2,1)S(1)} fusion(bf16[1,256,2176]{1,2,0:T(8,128)(2,1)S(1)} %collective-permute-done.8, bf16[1,256,2176]{1,2,0:T(8,128)(2,1)} %collective-permute-done.7, bf16[1,256,2176]{1,2,0:T(8,128)(2,1)S(1)} %collective-permute-done.6, bf16[1,256,2176]{1,2,0:T(8,128)(2,1)S(1)} %get-tuple-element.23), kind=kLoop, calls=%fused_computation.3 | loop fusion | flops 17825792 | bytes 8912896 | tf_op jit(solution)/shard_map/concatenate | solution.py:59
  84.8 2.4 fusion
  92.7 16.8 %collective-permute-start.9 = (f32[2592,128]{1,0:T(8,128)}, f32[2592,128]{1,0:T(8,128)}, u32[]{:S(2)}, u32[]{:S(2)}) collective-permute-start(f32[2592,128]{1,0:T(8,128)} %get-tuple-element.26), channel_id=1, source_target_pairs={{0,8},{8,16},{16,24},{24,0},{1,9},{9,17},{17,25},{25,1},{2,10},{10... | collective-permute-start | bytes 3981320 | tf_op jit(solution)/shard_map/ppermute | solution.py:56
  110.9 5.3 %all-to-all-start = ((s32[8,4,2]{1,2,0:T(2,128)}), s32[8,4,2]{1,2,0:T(2,128)S(1)}, u32[]{:S(2)}, u32[]{:S(2)}) async-start(s32[8,4,2]{1,2,0:T(2,128)} %copy.125), calls=%async_computation | async-start | bytes 16384 | tf_op jit(solution)/shard_map/all_to_all | solution.py:118
  122.8 16.6 %collective-permute-done.9 = f32[2592,128]{1,0:T(8,128)} collective-permute-done((f32[2592,128]{1,0:T(8,128)}, f32[2592,128]{1,0:T(8,128)}, u32[]{:S(2)}, u32[]{:S(2)}) %collective-permute-start.9) | collective-permute-done | bytes 1327136 | tf_op jit(solution)/shard_map/ppermute | solution.py:56
  142.8 6.9 %collective-permute-done.4 = f32[2592,128]{1,0:T(8,128)} collective-permute-done((f32[2592,128]{1,0:T(8,128)}, f32[2592,128]{1,0:T(8,128)}, u32[]{:S(2)}, u32[]{:S(2)}) %collective-permute-start.4) | collective-permute-done | bytes 1327136 | tf_op jit(solution)/shard_map/ppermute | solution.py:56
  149.7 2.8 %copy.129 = f32[2592,128]{0,1:T(8,128)} copy(f32[2592,128]{1,0:T(8,128)} %collective-permute-done.4) | data formatting | bytes 2654208 | tf_op jit(solution)/shard_map/ppermute | solution.py:56
  152.6 24.8 %collective-permute-done.5 = f32[2592,128]{1,0:T(8,128)} collective-permute-done((f32[2592,128]{1,0:T(8,128)}, f32[2592,128]{1,0:T(8,128)}, u32[]{:S(2)}, u32[]{:S(2)}) %collective-permute-start.5) | collective-permute-done | bytes 1327136 | tf_op jit(solution)/shard_map/ppermute | solution.py:56
  177.3 2.8 %copy.130 = f32[2592,128]{0,1:T(8,128)} copy(f32[2592,128]{1,0:T(8,128)} %collective-permute-done.5) | data formatting | bytes 2654208 | tf_op jit(solution)/shard_map/ppermute | solution.py:56
  180.2 2.8 %copy.132 = f32[2592,128]{0,1:T(8,128)} copy(f32[2592,128]{1,0:T(8,128)} %collective-permute-done.10) | data formatting | bytes 2654208 | tf_op jit(solution)/shard_map/ppermute | solution.py:56
  185.0 2.8 %copy.133 = f32[2592,128]{0,1:T(8,128)} copy(f32[2592,128]{1,0:T(8,128)} %collective-permute-done.11) | data formatting | bytes 2654208 | tf_op jit(solution)/shard_map/ppermute | solution.py:56
  190.4 5.9 %custom-call.8 = f32[2,32,32]{2,1,0:T(8,128)S(1)} custom-call(f32[2,32,32]{2,1,0:T(8,128)S(1)} %fusion.43), custom_call_target="Cholesky" | custom-call | tf_op jit(solution)/shard_map/jit(cholesky)/cholesky | solution.py:95
  196.5 4.9 %custom-call.9 = f32[2,1,32,32]{2,3,1,0:T(8,128)S(1)} custom-call(f32[2,1,32,32]{3,2,1,0:T(8,128)S(1)} %select_bitcast_fusion), custom_call_target="InvertDiagBlocksLowerTriangular" | custom-call | tf_op jit(solution)/shard_map/jit(_solve_triangular)/vmap()/triangular_solve | solution.py:96
  204.1 3.2 %fusion.5 = f32[2,2048,128]{1,2,0:T(8,128)} fusion(f32[1,2592,128]{1,2,0:T(8,128)S(1)} %add_bitcast_fusion.1, f32[1,2592,128]{1,2,0:T(8,128)S(1)} %add_bitcast_fusion, f32[2,32,2048]{2,1,0:T(8,128)S(1)} %fusion.29, s32[]{:T(128)S(6)} %select_n.204), kind=kOutput, calls=%fused_computation.21 | convolution fusion | flops 202375168 | bytes 5406724 | tf_op jit(solution)/shard_map/stp,stq->spq/dot_general | solution.py:98
  211.2 4.4 %all-to-all-start.1 = ((f32[8,4,128,128]{3,2,1,0:T(8,128)}), f32[8,4,128,128]{3,2,1,0:T(8,128)S(1)}, u32[]{:S(2)}, u32[]{:S(2)}) async-start(f32[8,4,128,128]{3,2,1,0:T(8,128)} %bitcast.29), calls=%async_computation.1 | async-start | bytes 4194304 | tf_op jit(solution)/shard_map/all_to_all | solution.py:117
  216.2 26.5 %all-to-all-done.1 = f32[8,4,128,128]{3,2,1,0:T(8,128)S(1)} async-done(((f32[8,4,128,128]{3,2,1,0:T(8,128)}), f32[8,4,128,128]{3,2,1,0:T(8,128)S(1)}, u32[]{:S(2)}, u32[]{:S(2)}) %all-to-all-start.1) | async-done | bytes 2097184 | tf_op jit(solution)/shard_map/all_to_all | solution.py:117
  244.1 11.5 %shard_map.64 = f32[2048,1024]{1,0:T(8,128)} custom-call(s32[32]{0:T(128)} %get-tuple-element.40.row_ref, s32[32]{0:T(128)} %get-tuple-element.39.col_ref, f32[32,128,128]{2,1,0:T(8,128)} %bitcast.74), custom_call_target="tpu_custom_call" | custom-call | tf_op jit(solution)/shard_map/pallas_call | solution.py:139
  (101 shorter events, 52.1 us)
Async XLA Ops:
  2.1 4.0 %copy-start.6 = (s32[2,256]{1,0:T(2,128)S(1)}, s32[2,256]{1,0:T(2,128)}, u32[]{:S(2)}) copy-start(s32[2,256]{1,0:T(2,128)} %param.7) | copy-start | bytes 6148
  15.3 8.7 %copy-start.7 = (s32[2,16]{1,0:T(2,128)S(1)}, s32[2,16]{1,0:T(2,128)}, u32[]{:S(2)}) copy-start(s32[2,16]{1,0:T(2,128)} %param.10) | copy-start | bytes 388
  15.3 9.4 %copy-start.8 = (s32[128]{0:T(128)S(1)}, s32[128]{0:T(128)}, u32[]{:S(2)}) copy-start(s32[128]{0:T(128)} %param.11) | copy-start | bytes 1540
  17.1 27.6 %collective-permute-start.2 = (bf16[1,256,2176]{1,2,0:T(8,128)(2,1)S(1)}, bf16[1,256,2176]{1,2,0:T(8,128)(2,1)}, u32[]{:S(2)}, u32[]{:S(2)}) collective-permute-start(bf16[1,256,2176]{1,2,0:T(8,128)(2,1)S(1)} %get-tuple-element.24), channel_id=1, source_target_pairs={{0,24},{8,0},{16,8},{24,16},{1,25},{9,1},{17,9},{25,17},{2,26},{10... | collective-permute-start | bytes 3342344 | tf_op jit(solution)/shard_map/ppermute | solution.py:56
  17.7 29.1 %collective-permute-start.1 = (bf16[1,256,2176]{1,2,0:T(8,128)(2,1)S(1)}, bf16[1,256,2176]{1,2,0:T(8,128)(2,1)}, u32[]{:S(2)}, u32[]{:S(2)}) collective-permute-start(bf16[1,256,2176]{1,2,0:T(8,128)(2,1)S(1)} %get-tuple-element.24), channel_id=1, source_target_pairs={{0,16},{8,24},{16,0},{24,8},{1,17},{9,25},{17,1},{25,9},{2,18},{10... | collective-permute-start | bytes 3342344 | tf_op jit(solution)/shard_map/ppermute | solution.py:56
  20.4 48.8 %collective-permute-start = (bf16[1,256,2176]{1,2,0:T(8,128)(2,1)S(1)}, bf16[1,256,2176]{1,2,0:T(8,128)(2,1)}, u32[]{:S(2)}, u32[]{:S(2)}) collective-permute-start(bf16[1,256,2176]{1,2,0:T(8,128)(2,1)S(1)} %get-tuple-element.24), channel_id=1, source_target_pairs={{0,8},{8,16},{16,24},{24,0},{1,9},{9,17},{17,25},{25,1},{2,10},{10... | collective-permute-start | bytes 3342344 | tf_op jit(solution)/shard_map/ppermute | solution.py:56
  20.4 61.2 %collective-permute-start.8 = (bf16[1,256,2176]{1,2,0:T(8,128)(2,1)S(1)}, bf16[1,256,2176]{1,2,0:T(8,128)(2,1)S(1)}, u32[]{:S(2)}, u32[]{:S(2)}) collective-permute-start(bf16[1,256,2176]{1,2,0:T(8,128)(2,1)S(1)} %get-tuple-element.23), channel_id=1, source_target_pairs={{0,96},{32,0},{64,32},{96,64},{1,97},{33,1},{65,33},{97,65},{2,98}... | collective-permute-start | bytes 3342344 | tf_op jit(solution)/shard_map/ppermute | solution.py:56
  23.4 58.2 %collective-permute-start.7 = (bf16[1,256,2176]{1,2,0:T(8,128)(2,1)S(1)}, bf16[1,256,2176]{1,2,0:T(8,128)(2,1)}, u32[]{:S(2)}, u32[]{:S(2)}) collective-permute-start(bf16[1,256,2176]{1,2,0:T(8,128)(2,1)S(1)} %get-tuple-element.23), channel_id=1, source_target_pairs={{0,64},{32,96},{64,0},{96,32},{1,65},{33,97},{65,1},{97,33},{2,66}... | collective-permute-start | bytes 3342344 | tf_op jit(solution)/shard_map/ppermute | solution.py:56
  44.7 36.9 %collective-permute-start.6 = (bf16[1,256,2176]{1,2,0:T(8,128)(2,1)S(1)}, bf16[1,256,2176]{1,2,0:T(8,128)(2,1)S(1)}, u32[]{:S(2)}, u32[]{:S(2)}) collective-permute-start(bf16[1,256,2176]{1,2,0:T(8,128)(2,1)S(1)} %get-tuple-element.23), channel_id=1, source_target_pairs={{0,32},{32,64},{64,96},{96,0},{1,33},{33,65},{65,97},{97,1},{2,34}... | collective-permute-start | bytes 3342344 | tf_op jit(solution)/shard_map/ppermute | solution.py:56
  74.0 4.0 %copy-start.2 = (f32[32,16,128]{2,0,1:T(8,128)}, f32[32,16,128]{2,0,1:T(8,128)S(1)}, u32[]{:S(2)}) copy-start(f32[32,16,128]{2,0,1:T(8,128)S(1)} %fusion.36) | copy-start | bytes 786436
  80.1 39.4 %collective-permute-start.3 = (f32[2592,128]{1,0:T(8,128)}, f32[2592,128]{1,0:T(8,128)}, u32[]{:S(2)}, u32[]{:S(2)}) collective-permute-start(f32[2592,128]{1,0:T(8,128)} %get-tuple-element.29), channel_id=1, source_target_pairs={{0,32},{32,64},{64,96},{96,0},{1,33},{33,65},{65,97},{97,1},{2,34}... | collective-permute-start | bytes 3981320 | tf_op jit(solution)/shard_map/ppermute | solution.py:56
  90.5 2.2 copy-start.4
  90.6 30.2 %copy-start.1 = (f32[2048,128]{1,0:T(8,128)S(1)}, f32[2048,128]{1,0:T(8,128)}, u32[]{:S(2)}) copy-start(f32[2048,128]{1,0:T(8,128)} %get-tuple-element.18) | copy-start | bytes 3145732
  90.6 30.2 %copy-start.3 = (f32[32,16,128]{2,0,1:T(8,128)S(1)}, f32[32,16,128]{2,0,1:T(8,128)}, u32[]{:S(2)}) copy-start(f32[32,16,128]{2,0,1:T(8,128)} %copy-done.2) | copy-start | bytes 786436
  92.7 46.6 %collective-permute-start.9 = (f32[2592,128]{1,0:T(8,128)}, f32[2592,128]{1,0:T(8,128)}, u32[]{:S(2)}, u32[]{:S(2)}) collective-permute-start(f32[2592,128]{1,0:T(8,128)} %get-tuple-element.26), channel_id=1, source_target_pairs={{0,8},{8,16},{16,24},{24,0},{1,9},{9,17},{17,25},{25,1},{2,10},{10... | collective-permute-start | bytes 3981320 | tf_op jit(solution)/shard_map/ppermute | solution.py:56
  110.9 100.3 %all-to-all-start = ((s32[8,4,2]{1,2,0:T(2,128)}), s32[8,4,2]{1,2,0:T(2,128)S(1)}, u32[]{:S(2)}, u32[]{:S(2)}) async-start(s32[8,4,2]{1,2,0:T(2,128)} %copy.125), calls=%async_computation | async-start | bytes 16384 | tf_op jit(solution)/shard_map/all_to_all | solution.py:118
  116.3 33.4 %collective-permute-start.4 = (f32[2592,128]{1,0:T(8,128)}, f32[2592,128]{1,0:T(8,128)}, u32[]{:S(2)}, u32[]{:S(2)}) collective-permute-start(f32[2592,128]{1,0:T(8,128)} %get-tuple-element.28), channel_id=1, source_target_pairs={{0,64},{32,96},{64,0},{96,32},{1,65},{33,97},{65,1},{97,33},{2,66}... | collective-permute-start | bytes 3981320 | tf_op jit(solution)/shard_map/ppermute | solution.py:56
  118.4 59.0 %collective-permute-start.5 = (f32[2592,128]{1,0:T(8,128)}, f32[2592,128]{1,0:T(8,128)}, u32[]{:S(2)}, u32[]{:S(2)}) collective-permute-start(f32[2592,128]{1,0:T(8,128)} %get-tuple-element.30), channel_id=1, source_target_pairs={{0,96},{32,0},{64,32},{96,64},{1,97},{33,1},{65,33},{97,65},{2,98}... | collective-permute-start | bytes 3981320 | tf_op jit(solution)/shard_map/ppermute | solution.py:56
  119.4 60.8 %collective-permute-start.10 = (f32[2592,128]{1,0:T(8,128)}, f32[2592,128]{1,0:T(8,128)}, u32[]{:S(2)}, u32[]{:S(2)}) collective-permute-start(f32[2592,128]{1,0:T(8,128)} %get-tuple-element.25), channel_id=1, source_target_pairs={{0,16},{8,24},{16,0},{24,8},{1,17},{9,25},{17,1},{25,9},{2,18},{10... | collective-permute-start | bytes 3981320 | tf_op jit(solution)/shard_map/ppermute | solution.py:56
  119.4 65.6 %collective-permute-start.11 = (f32[2592,128]{1,0:T(8,128)}, f32[2592,128]{1,0:T(8,128)}, u32[]{:S(2)}, u32[]{:S(2)}) collective-permute-start(f32[2592,128]{1,0:T(8,128)} %get-tuple-element.27), channel_id=1, source_target_pairs={{0,24},{8,0},{16,8},{24,16},{1,25},{9,1},{17,9},{25,17},{2,26},{10... | collective-permute-start | bytes 3981320 | tf_op jit(solution)/shard_map/ppermute | solution.py:56
  122.4 17.0 %copy-start.5 = (f32[32,16,128]{2,0,1:T(8,128)S(1)}, f32[32,16,128]{2,0,1:T(8,128)}, u32[]{:S(2)}) copy-start(f32[32,16,128]{2,0,1:T(8,128)} %copy-done.4) | copy-start | bytes 786436
  211.2 31.6 %all-to-all-start.1 = ((f32[8,4,128,128]{3,2,1,0:T(8,128)}), f32[8,4,128,128]{3,2,1,0:T(8,128)S(1)}, u32[]{:S(2)}, u32[]{:S(2)}) async-start(f32[8,4,128,128]{3,2,1,0:T(8,128)} %bitcast.29), calls=%async_computation.1 | async-start | bytes 4194304 | tf_op jit(solution)/shard_map/all_to_all | solution.py:117
  242.7 1.3 copy-start

commit v8 on v7

--- a/solution.py
+++ b/solution.py
@@ -52,6 +52,16 @@
     pad = jnp.zeros((scan_count, sample_rows, tile_pixels - template_cols), jnp.bfloat16)
     local = jnp.concatenate([masked, template, pad], axis=2)
 
+    bins_all = lax.all_gather(ground_bin.astype(jnp.bfloat16), SCAN_AXES, axis=1, tiled=True)
+    template_all = build_templates(
+        bins_all.astype(jnp.int32), jnp.arange(n_scan * sample_rows), lengths, degrees
+    )
+    normal = jnp.einsum("snt,snu->stu", template_all, template_all, preferred_element_type=jnp.float32)
+    normal = normal + jnp.eye(template_cols, dtype=jnp.float32)[None]
+    factor = jnp.linalg.cholesky(normal)
+    eye = jnp.broadcast_to(jnp.eye(template_cols, dtype=jnp.float32), normal.shape)
+    inverse = jax.scipy.linalg.solve_triangular(factor, eye, lower=True)
+
     def shifted(x, axis, n, d):
         return lax.ppermute(x, axis, [(i, (i + d) % n) for i in range(n)])
 
@@ -72,11 +82,9 @@
         projs = jnp.einsum("snt,snp->tp", tpl, rows, preferred_element_type=jnp.float32)
         projs = jnp.swapaxes(projs.reshape(template_cols, k_tiles, tile_pixels), 0, 1)
         projs = projs.reshape(k_tiles * template_cols, tile_pixels)
-        norm = jnp.einsum("snt,snu->tu", tpl, tpl, preferred_element_type=jnp.float32)
-        norm = jnp.pad(norm, ((0, 0), (0, col_width - template_cols)))
         summed = None
         for d in range(n_reduce):
-            part = jnp.concatenate([grams[:, d * col_width : (d + 1) * col_width], projs, norm], axis=0)
+            part = jnp.concatenate([grams[:, d * col_width : (d + 1) * col_width], projs], axis=0)
             part = part if d == 0 else shifted(part, reduce_axis, n_reduce, d)
             summed = part if summed is None else summed + part
         return summed
@@ -90,10 +98,7 @@
     gram = summed[:, :width]
     proj = summed[:, width : width + k_tiles * template_cols].reshape(scan_count, k_tiles, template_cols, tile_pixels)
     proj = jnp.swapaxes(proj, 1, 2).reshape(scan_count, template_cols, width)
-    normal = summed[:, width + k_tiles * template_cols :, :template_cols]
-    normal = normal + jnp.eye(template_cols, dtype=jnp.float32)[None]
-    factor = jnp.linalg.cholesky(normal)
-    whitened = jax.scipy.linalg.solve_triangular(factor, proj, lower=True)
+    whitened = jnp.einsum("stu,sup->stp", inverse, proj, precision=lax.Precision.HIGHEST)
     w_col = lax.dynamic_slice_in_dim(whitened, scan_index * tile_pixels, tile_pixels, 2)
     correction = jnp.einsum("stp,stq->spq", whitened, w_col, precision=lax.Precision.HIGHEST)
     contrib = gram - correction

time: 256 us -> 255 us (level)
  the two profiles are of different devices: /device:TPU:4 before, /device:TPU:1 now
where the time goes in v8:
time: 255 us; the launch traced here: 254 us
  waiting for transfers between devices  71.6 us (28%)
  starting transfers between devices  52.4 us (21%)
  blocking collectives  49.1 us (19%)
  other arithmetic  29.7 us (12%)
  local copies, waits for them, and re-layouts  24.7 us (10%)
  matrix products  14.8 us (6%)
  Pallas kernels  11.5 us (5%)
    all_gather x1, blocking collectives, per_device(): lax.all_gather(ground_bin.astype(jnp.bfloat16), SCAN_AXES, axis=1, tiled=...  49.1 us
    ppermute x12, waiting for transfers between devices, shifted(): return lax.ppermute(x, axis, [(i, (i + d) % n) for i in range(n)])  46.1 us
    all_to_all x1, starting transfers between devices, per_device(): lax.all_to_all(send_rows, 'tile', split_axis=0, concat_axis=0, tiled=True)  32.1 us
    all_to_all x1, waiting for transfers between devices, per_device(): lax.all_to_all(send_rows, 'tile', split_axis=0, concat_axis=0, tiled=True)  25.5 us
    ppermute x12, starting transfers between devices, shifted(): return lax.ppermute(x, axis, [(i, (i + d) % n) for i in range(n)])  12.9 us
    pallas_call x1, Pallas kernels, place(): pl.pallas_call(kernel, grid_spec=pltpu.PrefetchScalarGridSpec(num_scalar_...  11.5 us
    all_to_all x1, starting transfers between devices, per_device(): lax.all_to_all(send_labels, 'tile', split_axis=0, concat_axis=0, tiled=True)  7.38 us
    concatenate x1, local copies, waits for them, and re-layouts, per_device(): local = jnp.concatenate([masked, template, pad], axis=2)  7.35 us
  transfers between devices with their start and end apart: 14, of which 4 were waited for; matrix products, arithmetic and copies ran while one was open for 20% of the time, Pallas kernels for 0%

profile of v8, /device:TPU:1, one launch (start us, length us, event | category | flops | bytes accessed | tf_op | source)
XLA Modules:
  0.0 254.4 jit_solution(1030494205364885525)
XLA Ops:
  0.0 3.9 %copy.37 = bf16[2,256,2048]{1,2,0:T(8,128)(2,1)} copy(bf16[2,256,2048]{2,1,0:T(8,128)(2,1)} %param.6) | data formatting | bytes 4194304 | tf_op args[0]
  6.1 7.3 %concatenate.50 = bf16[2,256,2176]{1,2,0:T(8,128)(2,1)} concatenate(bf16[2,256,2048]{1,2,0:T(8,128)(2,1)S(1)} %broadcast_select_fusion, bf16[2,256,1]{1,2,0:T(2,128)(2,1)S(1)} %get-tuple-element.46, bf16[2,256,1]{1,2,0:T(2,128)(2,1)S(1)} %get-tuple-element.45, bf16[2,256,1]{1,2,0:T(2,128)(2,1)S(1)} %get-tuple-element.44, bf16[2,256,1]{1,2,0:T(2,128)(2,1)S(1)} %get-tuple-element.43, ...), dimensions={2} | concatenate | bytes 4456448 | tf_op jit(solution)/shard_map/concatenate | solution.py:53
  15.2 3.4 %collective-permute-start.2 = (bf16[1,256,2176]{1,2,0:T(8,128)(2,1)S(1)}, bf16[1,256,2176]{1,2,0:T(8,128)(2,1)}, u32[]{:S(2)}, u32[]{:S(2)}) collective-permute-start(bf16[1,256,2176]{1,2,0:T(8,128)(2,1)S(1)} %get-tuple-element.24), channel_id=1, source_target_pairs={{0,24},{8,0},{16,8},{24,16},{1,25},{9,1},{17,9},{25,17},{2,26},{10... | collective-permute-start | bytes 3342344 | tf_op jit(solution)/shard_map/ppermute | solution.py:66
  19.7 2.7 %collective-permute-start.8 = (bf16[1,256,2176]{1,2,0:T(8,128)(2,1)S(1)}, bf16[1,256,2176]{1,2,0:T(8,128)(2,1)}, u32[]{:S(2)}, u32[]{:S(2)}) collective-permute-start(bf16[1,256,2176]{1,2,0:T(8,128)(2,1)S(1)} %get-tuple-element.23), channel_id=1, source_target_pairs={{0,96},{32,0},{64,32},{96,64},{1,97},{33,1},{65,33},{97,65},{2,98}... | collective-permute-start | bytes 3342344 | tf_op jit(solution)/shard_map/ppermute | solution.py:66
  26.5 7.4 %all-to-all-start = ((s32[8,4,2]{1,2,0:T(2,128)}), s32[8,4,2]{1,2,0:T(2,128)S(1)}, u32[]{:S(2)}, u32[]{:S(2)}) async-start(s32[8,4,2]{1,2,0:T(2,128)} %copy.35), calls=%async_computation | async-start | bytes 16384 | tf_op jit(solution)/shard_map/all_to_all | solution.py:123
  33.9 49.1 %all_gather.3 = bf16[2,4096]{1,0:T(2,128)(2,1)S(1)} all-gather(bf16[2,256]{1,0:T(2,128)(2,1)S(1)} %convert_element_type.59), channel_id=1, replica_groups=mesh['sy'=4,'sx'=4,'tile'=8] {'sy','sx'}, dimensions={1}, use_global_device_ids=true | all-gather | bytes 17408 | tf_op jit(solution)/shard_map/all_gather | solution.py:55
  85.0 5.9 %custom-call.8 = f32[2,32,32]{2,1,0:T(8,128)S(1)} custom-call(f32[2,32,32]{2,1,0:T(8,128)S(1)} %fusion.57), custom_call_target="Cholesky" | custom-call | tf_op jit(solution)/shard_map/jit(cholesky)/cholesky | solution.py:61
  91.0 2.2 pad_maximum_fusion
  93.8 2.4 fusion.2
  96.2 2.1 fusion.45
  100.4 2.6 %collective-permute-start.5 = (f32[2560,128]{1,0:T(8,128)S(1)}, f32[2560,128]{1,0:T(8,128)S(1)}, u32[]{:S(2)}, u32[]{:S(2)}) collective-permute-start(f32[2560,128]{1,0:T(8,128)S(1)} %get-tuple-element.30), channel_id=1, source_target_pairs={{0,96},{32,0},{64,32},{96,64},{1,97},{33,1},{65,33},{97,65},{2,98}... | collective-permute-start | bytes 3932168 | tf_op jit(solution)/shard_map/ppermute | solution.py:66
  103.6 13.6 %collective-permute-done.6 = bf16[1,256,2176]{1,2,0:T(8,128)(2,1)S(1)} collective-permute-done((bf16[1,256,2176]{1,2,0:T(8,128)(2,1)S(1)}, bf16[1,256,2176]{1,2,0:T(8,128)(2,1)S(1)}, u32[]{:S(2)}, u32[]{:S(2)}) %collective-permute-start.6) | collective-permute-done | bytes 1114144 | tf_op jit(solution)/shard_map/ppermute | solution.py:66
  117.3 2.8 %pad_maximum_fusion.1 = bf16[1,1024,2176]{1,2,0:T(8,128)(2,1)S(1)} fusion(bf16[1,256,2176]{1,2,0:T(8,128)(2,1)} %collective-permute-done.8, bf16[1,256,2176]{1,2,0:T(8,128)(2,1)} %collective-permute-done.7, bf16[1,256,2176]{1,2,0:T(8,128)(2,1)S(1)} %collective-permute-done.6, bf16[1,256,2176]{1,2,0:T(8,128)(2,1)S(1)} %get-tuple-element.23), kind=kLoop, calls=%fused_computation.3 | loop fusion | flops 17825792 | bytes 8912896 | tf_op jit(solution)/shard_map/concatenate | solution.py:69
  120.6 2.4 fusion
  124.3 2.1 fusion.38
  131.8 4.9 %custom-call.9 = f32[2,1,32,32]{2,3,1,0:T(8,128)S(1)} custom-call(f32[2,1,32,32]{3,2,1,0:T(8,128)S(1)} %select_bitcast_fusion), custom_call_target="InvertDiagBlocksLowerTriangular" | custom-call | tf_op jit(solution)/shard_map/jit(_solve_triangular)/vmap()/triangular_solve | solution.py:63
  137.2 32.2 %collective-permute-done.3 = f32[2560,128]{1,0:T(8,128)} collective-permute-done((f32[2560,128]{1,0:T(8,128)}, f32[2560,128]{1,0:T(8,128)}, u32[]{:S(2)}, u32[]{:S(2)}) %collective-permute-start.3) | collective-permute-done | bytes 1310752 | tf_op jit(solution)/shard_map/ppermute | solution.py:66
  169.4 2.4 fusion.13
  171.9 2.3 fusion.9
  174.9 4.8 %fusion.5 = f32[2,2048,128]{2,1,0:T(8,128)} fusion(f32[1,2560,128]{2,1,0:T(8,128)S(1)} %fusion.13, f32[1,2560,128]{2,1,0:T(8,128)S(1)} %fusion.9, f32[2,32,2048]{2,1,0:T(8,128)S(1)} %fusion.27, s32[]{:T(128)S(6)} %select_n.293), kind=kOutput, calls=%fused_computation.19 | convolution fusion | flops 202375168 | bytes 5275652 | tf_op jit(solution)/shard_map/stp,stq->spq/dot_general | solution.py:103
  179.6 3.6 %gather_fusion.1 = f32[32,128,128]{2,1,0:T(8,128)} fusion(f32[32,128,128]{2,1,0:T(8,128)} %bitcast.74, s32[1024]{0:T(1024)S(1)} %pad_clamp_fusion), kind=kCustom, calls=%fused_computation.1 | custom fusion | bytes 4194432 | tf_op jit(solution)/shard_map/gather | solution.py:119
  183.2 32.1 %all-to-all-start.1 = ((f32[8,4,128,128]{3,2,1,0:T(8,128)}), f32[8,4,128,128]{3,2,1,0:T(8,128)S(1)}, u32[]{:S(2)}, u32[]{:S(2)}) async-start(f32[8,4,128,128]{3,2,1,0:T(8,128)} %bitcast.29), calls=%async_computation.1 | async-start | bytes 4194304 | tf_op jit(solution)/shard_map/all_to_all | solution.py:122
  216.0 25.5 %all-to-all-done.1 = f32[8,4,128,128]{3,2,1,0:T(8,128)S(1)} async-done(((f32[8,4,128,128]{3,2,1,0:T(8,128)}), f32[8,4,128,128]{3,2,1,0:T(8,128)S(1)}, u32[]{:S(2)}, u32[]{:S(2)}) %all-to-all-start.1) | async-done | bytes 2097184 | tf_op jit(solution)/shard_map/all_to_all | solution.py:122
  242.8 11.5 %shard_map.64 = f32[2048,1024]{1,0:T(8,128)} custom-call(s32[32]{0:T(128)} %get-tuple-element.48.row_ref, s32[32]{0:T(128)} %get-tuple-element.47.col_ref, f32[32,128,128]{2,1,0:T(8,128)} %bitcast.75), custom_call_target="tpu_custom_call" | custom-call | tf_op jit(solution)/shard_map/pallas_call | solution.py:144
  (99 shorter events, 24.5 us)
Async XLA Ops:
  0.0 4.0 %copy-start.7 = (s32[2]{0:T(128)S(1)}, s32[2]{0:T(128)}, u32[]{:S(2)}) copy-start(s32[2]{0:T(128)} %param.9) | copy-start | bytes 28
  0.0 4.0 %copy-start.8 = (s32[2]{0:T(128)S(1)}, s32[2]{0:T(128)}, u32[]{:S(2)}) copy-start(s32[2]{0:T(128)} %param.8) | copy-start | bytes 28
  4.1 1.8 copy-start.5
  13.4 9.3 %copy-start.6 = (s32[2,16]{1,0:T(2,128)S(1)}, s32[2,16]{1,0:T(2,128)}, u32[]{:S(2)}) copy-start(s32[2,16]{1,0:T(2,128)} %param.10) | copy-start | bytes 388
  13.4 10.0 %copy-start.9 = (s32[128]{0:T(128)S(1)}, s32[128]{0:T(128)}, u32[]{:S(2)}) copy-start(s32[128]{0:T(128)} %param.11) | copy-start | bytes 1540
  15.2 75.8 %collective-permute-start.2 = (bf16[1,256,2176]{1,2,0:T(8,128)(2,1)S(1)}, bf16[1,256,2176]{1,2,0:T(8,128)(2,1)}, u32[]{:S(2)}, u32[]{:S(2)}) collective-permute-start(bf16[1,256,2176]{1,2,0:T(8,128)(2,1)S(1)} %get-tuple-element.24), channel_id=1, source_target_pairs={{0,24},{8,0},{16,8},{24,16},{1,25},{9,1},{17,9},{25,17},{2,26},{10... | collective-permute-start | bytes 3342344 | tf_op jit(solution)/shard_map/ppermute | solution.py:66
  18.5 72.5 %collective-permute-start.1 = (bf16[1,256,2176]{1,2,0:T(8,128)(2,1)S(1)}, bf16[1,256,2176]{1,2,0:T(8,128)(2,1)}, u32[]{:S(2)}, u32[]{:S(2)}) collective-permute-start(bf16[1,256,2176]{1,2,0:T(8,128)(2,1)S(1)} %get-tuple-element.24), channel_id=1, source_target_pairs={{0,16},{8,24},{16,0},{24,8},{1,17},{9,25},{17,1},{25,9},{2,18},{10... | collective-permute-start | bytes 3342344 | tf_op jit(solution)/shard_map/ppermute | solution.py:66
  19.1 72.0 %collective-permute-start = (bf16[1,256,2176]{1,2,0:T(8,128)(2,1)S(1)}, bf16[1,256,2176]{1,2,0:T(8,128)(2,1)}, u32[]{:S(2)}, u32[]{:S(2)}) collective-permute-start(bf16[1,256,2176]{1,2,0:T(8,128)(2,1)S(1)} %get-tuple-element.24), channel_id=1, source_target_pairs={{0,8},{8,16},{16,24},{24,0},{1,9},{9,17},{17,25},{25,1},{2,10},{10... | collective-permute-start | bytes 3342344 | tf_op jit(solution)/shard_map/ppermute | solution.py:66
  19.7 83.4 %collective-permute-start.8 = (bf16[1,256,2176]{1,2,0:T(8,128)(2,1)S(1)}, bf16[1,256,2176]{1,2,0:T(8,128)(2,1)}, u32[]{:S(2)}, u32[]{:S(2)}) collective-permute-start(bf16[1,256,2176]{1,2,0:T(8,128)(2,1)S(1)} %get-tuple-element.23), channel_id=1, source_target_pairs={{0,96},{32,0},{64,32},{96,64},{1,97},{33,1},{65,33},{97,65},{2,98}... | collective-permute-start | bytes 3342344 | tf_op jit(solution)/shard_map/ppermute | solution.py:66
  22.4 81.2 %collective-permute-start.7 = (bf16[1,256,2176]{1,2,0:T(8,128)(2,1)S(1)}, bf16[1,256,2176]{1,2,0:T(8,128)(2,1)}, u32[]{:S(2)}, u32[]{:S(2)}) collective-permute-start(bf16[1,256,2176]{1,2,0:T(8,128)(2,1)S(1)} %get-tuple-element.23), channel_id=1, source_target_pairs={{0,64},{32,96},{64,0},{96,32},{1,65},{33,97},{65,1},{97,33},{2,66}... | collective-permute-start | bytes 3342344 | tf_op jit(solution)/shard_map/ppermute | solution.py:66
  26.5 156.8 %all-to-all-start = ((s32[8,4,2]{1,2,0:T(2,128)}), s32[8,4,2]{1,2,0:T(2,128)S(1)}, u32[]{:S(2)}, u32[]{:S(2)}) async-start(s32[8,4,2]{1,2,0:T(2,128)} %copy.35), calls=%async_computation | async-start | bytes 16384 | tf_op jit(solution)/shard_map/all_to_all | solution.py:123
  90.9 26.3 %collective-permute-start.6 = (bf16[1,256,2176]{1,2,0:T(8,128)(2,1)S(1)}, bf16[1,256,2176]{1,2,0:T(8,128)(2,1)S(1)}, u32[]{:S(2)}, u32[]{:S(2)}) collective-permute-start(bf16[1,256,2176]{1,2,0:T(8,128)(2,1)S(1)} %get-tuple-element.23), channel_id=1, source_target_pairs={{0,32},{32,64},{64,96},{96,0},{1,33},{33,65},{65,97},{97,1},{2,34}... | collective-permute-start | bytes 3342344 | tf_op jit(solution)/shard_map/ppermute | solution.py:66
  100.4 29.2 %collective-permute-start.5 = (f32[2560,128]{1,0:T(8,128)S(1)}, f32[2560,128]{1,0:T(8,128)S(1)}, u32[]{:S(2)}, u32[]{:S(2)}) collective-permute-start(f32[2560,128]{1,0:T(8,128)S(1)} %get-tuple-element.30), channel_id=1, source_target_pairs={{0,96},{32,0},{64,32},{96,64},{1,97},{33,1},{65,33},{97,65},{2,98}... | collective-permute-start | bytes 3932168 | tf_op jit(solution)/shard_map/ppermute | solution.py:66
  103.0 34.2 %collective-permute-start.4 = (f32[2560,128]{1,0:T(8,128)}, f32[2560,128]{1,0:T(8,128)}, u32[]{:S(2)}, u32[]{:S(2)}) collective-permute-start(f32[2560,128]{1,0:T(8,128)} %get-tuple-element.29), channel_id=1, source_target_pairs={{0,64},{32,96},{64,0},{96,32},{1,65},{33,97},{65,1},{97,33},{2,66}... | collective-permute-start | bytes 3932168 | tf_op jit(solution)/shard_map/ppermute | solution.py:66
  103.0 66.4 %collective-permute-start.3 = (f32[2560,128]{1,0:T(8,128)}, f32[2560,128]{1,0:T(8,128)}, u32[]{:S(2)}, u32[]{:S(2)}) collective-permute-start(f32[2560,128]{1,0:T(8,128)} %get-tuple-element.28), channel_id=1, source_target_pairs={{0,32},{32,64},{64,96},{96,0},{1,33},{33,65},{65,97},{97,1},{2,34}... | collective-permute-start | bytes 3932168 | tf_op jit(solution)/shard_map/ppermute | solution.py:66
  126.4 2.1 copy-start.2
  128.4 43.4 %collective-permute-start.11 = (f32[2560,128]{1,0:T(8,128)}, f32[2560,128]{1,0:T(8,128)}, u32[]{:S(2)}, u32[]{:S(2)}) collective-permute-start(f32[2560,128]{1,0:T(8,128)} %get-tuple-element.27), channel_id=1, source_target_pairs={{0,24},{8,0},{16,8},{24,16},{1,25},{9,1},{17,9},{25,17},{2,26},{10... | collective-permute-start | bytes 3932168 | tf_op jit(solution)/shard_map/ppermute | solution.py:66
  128.4 43.4 %collective-permute-start.10 = (f32[2560,128]{1,0:T(8,128)}, f32[2560,128]{1,0:T(8,128)}, u32[]{:S(2)}, u32[]{:S(2)}) collective-permute-start(f32[2560,128]{1,0:T(8,128)} %get-tuple-element.26), channel_id=1, source_target_pairs={{0,16},{8,24},{16,0},{24,8},{1,17},{9,25},{17,1},{25,9},{2,18},{10... | collective-permute-start | bytes 3932168 | tf_op jit(solution)/shard_map/ppermute | solution.py:66
  129.6 1.1 copy-start.4
  130.8 41.1 %collective-permute-start.9 = (f32[2560,128]{1,0:T(8,128)}, f32[2560,128]{1,0:T(8,128)}, u32[]{:S(2)}, u32[]{:S(2)}) collective-permute-start(f32[2560,128]{1,0:T(8,128)} %get-tuple-element.25), channel_id=1, source_target_pairs={{0,8},{8,16},{16,24},{24,0},{1,9},{9,17},{17,25},{25,1},{2,10},{10... | collective-permute-start | bytes 3932168 | tf_op jit(solution)/shard_map/ppermute | solution.py:66
  169.4 2.5 copy-start.1
  169.4 2.5 copy-start.3
  183.2 58.3 %all-to-all-start.1 = ((f32[8,4,128,128]{3,2,1,0:T(8,128)}), f32[8,4,128,128]{3,2,1,0:T(8,128)S(1)}, u32[]{:S(2)}, u32[]{:S(2)}) async-start(f32[8,4,128,128]{3,2,1,0:T(8,128)} %bitcast.29), calls=%async_computation.1 | async-start | bytes 4194304 | tf_op jit(solution)/shard_map/all_to_all | solution.py:122
  241.5 1.3 copy-start

commit v9 on v8

--- a/solution.py
+++ b/solution.py
@@ -125,32 +125,38 @@
     item_total = n_tile * capacity
     recv_rows = recv_rows.reshape(item_total, tile_pixels, tile_pixels)
     recv_labels = recv_labels.reshape(item_total, 1 + k_cols)
-    return place(recv_rows, recv_labels[:, 0], recv_labels[:, 1], n_scan, n_tile)
+    row_block = recv_labels[:, 0]
+    order = jnp.argsort(row_block).astype(jnp.int32)
+    counts = jnp.sum(row_block[:, None] == jnp.arange(n_scan)[None, :], axis=0)
+    starts = jnp.concatenate([jnp.zeros((1,), jnp.int32), jnp.cumsum(counts).astype(jnp.int32)])
+    return place(recv_rows, order, starts, recv_labels[:, 1], n_scan, n_tile)
 
 
-def place(recv, row_block, col_block, n_rows, n_cols):
+def place(recv, order, starts, col_block, n_rows, n_cols):
     items, tile_pixels, _ = recv.shape
 
-    def kernel(row_ref, col_ref, recv_ref, out_ref):
+    def kernel(order_ref, starts_ref, col_ref, recv_ref, out_ref):
         r = pl.program_id(0)
         out_ref[...] = jnp.zeros(out_ref.shape, out_ref.dtype)
 
-        for i in range(items):
-            @pl.when(row_ref[i] == r)
-            def _():
-                at = pl.ds(pl.multiple_of(col_ref[i] * tile_pixels, tile_pixels), tile_pixels)
-                out_ref[:, at] += recv_ref[i]
+        def body(k, carry):
+            i = order_ref[k]
+            at = pl.ds(pl.multiple_of(col_ref[i] * tile_pixels, tile_pixels), tile_pixels)
+            out_ref[:, at] += recv_ref[i]
+            return carry
+
+        lax.fori_loop(starts_ref[r], starts_ref[r + 1], body, 0)
 
     return pl.pallas_call(
         kernel,
         grid_spec=pltpu.PrefetchScalarGridSpec(
-            num_scalar_prefetch=2,
+            num_scalar_prefetch=3,
             grid=(n_rows,),
-            in_specs=[pl.BlockSpec((items, tile_pixels, tile_pixels), lambda r, a, b: (0, 0, 0))],
-            out_specs=pl.BlockSpec((tile_pixels, n_cols * tile_pixels), lambda r, a, b: (r, 0)),
+            in_specs=[pl.BlockSpec((items, tile_pixels, tile_pixels), lambda r, a, b, c: (0, 0, 0))],
+            out_specs=pl.BlockSpec((tile_pixels, n_cols * tile_pixels), lambda r, a, b, c: (r, 0)),
         ),
         out_shape=jax.ShapeDtypeStruct((n_rows * tile_pixels, n_cols * tile_pixels), jnp.float32),
-    )(row_block, col_block, recv)
+    )(order, starts, col_block, recv)
 
 
 def solution(mesh):

time: 255 us -> 253 us (level)
    all_to_all x1, waiting for transfers between devices: 25.5 us -> 23 us  [per_device(): lax.all_to_all(send_rows, 'tile', split_axis=0, concat_axis=0, tiled=True)]
  transfers between devices with their start and end apart: 14 -> 14, of which waited for: 4 -> 4; matrix products, arithmetic and copies ran while one was open for 20% -> 21% of each run, Pallas kernels for 0% -> 0%
where the time goes in v9:
time: 253 us; the launch traced here: 252 us
  waiting for transfers between devices  69.1 us (27%)
  starting transfers between devices  52.4 us (21%)
  blocking collectives  49.1 us (19%)
  other arithmetic  32.2 us (13%)
  local copies, waits for them, and re-layouts  24.8 us (10%)
  matrix products  14.8 us (6%)
  Pallas kernels  9.41 us (4%)
    all_gather x1, blocking collectives, per_device(): lax.all_gather(ground_bin.astype(jnp.bfloat16), SCAN_AXES, axis=1, tiled=...  49.1 us
    ppermute x12, waiting for transfers between devices, shifted(): return lax.ppermute(x, axis, [(i, (i + d) % n) for i in range(n)])  46.1 us
    all_to_all x1, starting transfers between devices, per_device(): lax.all_to_all(send_rows, 'tile', split_axis=0, concat_axis=0, tiled=True)  32.1 us
    all_to_all x1, waiting for transfers between devices, per_device(): lax.all_to_all(send_rows, 'tile', split_axis=0, concat_axis=0, tiled=True)  23 us
    ppermute x12, starting transfers between devices, shifted(): return lax.ppermute(x, axis, [(i, (i + d) % n) for i in range(n)])  12.9 us
    pallas_call x1, Pallas kernels, place(): pl.pallas_call(kernel, grid_spec=pltpu.PrefetchScalarGridSpec(num_scalar_...  9.41 us
    all_to_all x1, starting transfers between devices, per_device(): lax.all_to_all(send_labels, 'tile', split_axis=0, concat_axis=0, tiled=True)  7.38 us
    concatenate x1, local copies, waits for them, and re-layouts, per_device(): local = jnp.concatenate([masked, template, pad], axis=2)  7.35 us
  transfers between devices with their start and end apart: 14, of which 4 were waited for; matrix products, arithmetic and copies ran while one was open for 21% of the time, Pallas kernels for 0%

profile of v9, /device:TPU:1, one launch (start us, length us, event | category | flops | bytes accessed | tf_op | source)
XLA Modules:
  0.0 252.3 jit_solution(11527049933944863937)
XLA Ops:
  0.0 3.9 %copy.41 = bf16[2,256,2048]{1,2,0:T(8,128)(2,1)} copy(bf16[2,256,2048]{2,1,0:T(8,128)(2,1)} %param.6) | data formatting | bytes 4194304 | tf_op args[0]
  6.1 7.3 %concatenate.54 = bf16[2,256,2176]{1,2,0:T(8,128)(2,1)} concatenate(bf16[2,256,2048]{1,2,0:T(8,128)(2,1)S(1)} %broadcast_select_fusion, bf16[2,256,1]{1,2,0:T(2,128)(2,1)S(1)} %get-tuple-element.48, bf16[2,256,1]{1,2,0:T(2,128)(2,1)S(1)} %get-tuple-element.47, bf16[2,256,1]{1,2,0:T(2,128)(2,1)S(1)} %get-tuple-element.46, bf16[2,256,1]{1,2,0:T(2,128)(2,1)S(1)} %get-tuple-element.45, ...), dimensions={2} | concatenate | bytes 4456448 | tf_op jit(solution)/shard_map/concatenate | solution.py:53
  15.2 3.4 %collective-permute-start.2 = (bf16[1,256,2176]{1,2,0:T(8,128)(2,1)S(1)}, bf16[1,256,2176]{1,2,0:T(8,128)(2,1)}, u32[]{:S(2)}, u32[]{:S(2)}) collective-permute-start(bf16[1,256,2176]{1,2,0:T(8,128)(2,1)S(1)} %get-tuple-element.26), channel_id=1, source_target_pairs={{0,24},{8,0},{16,8},{24,16},{1,25},{9,1},{17,9},{25,17},{2,26},{10... | collective-permute-start | bytes 3342344 | tf_op jit(solution)/shard_map/ppermute | solution.py:66
  19.7 2.7 %collective-permute-start.8 = (bf16[1,256,2176]{1,2,0:T(8,128)(2,1)S(1)}, bf16[1,256,2176]{1,2,0:T(8,128)(2,1)}, u32[]{:S(2)}, u32[]{:S(2)}) collective-permute-start(bf16[1,256,2176]{1,2,0:T(8,128)(2,1)S(1)} %get-tuple-element.25), channel_id=1, source_target_pairs={{0,96},{32,0},{64,32},{96,64},{1,97},{33,1},{65,33},{97,65},{2,98}... | collective-permute-start | bytes 3342344 | tf_op jit(solution)/shard_map/ppermute | solution.py:66
  26.5 7.4 %all-to-all-start = ((s32[8,4,2]{1,2,0:T(2,128)}), s32[8,4,2]{1,2,0:T(2,128)S(1)}, u32[]{:S(2)}, u32[]{:S(2)}) async-start(s32[8,4,2]{1,2,0:T(2,128)} %copy.38), calls=%async_computation | async-start | bytes 16384 | tf_op jit(solution)/shard_map/all_to_all | solution.py:123
  33.9 49.1 %all_gather.3 = bf16[2,4096]{1,0:T(2,128)(2,1)S(1)} all-gather(bf16[2,256]{1,0:T(2,128)(2,1)S(1)} %convert_element_type.63), channel_id=1, replica_groups=mesh['sy'=4,'sx'=4,'tile'=8] {'sy','sx'}, dimensions={1}, use_global_device_ids=true | all-gather | bytes 17408 | tf_op jit(solution)/shard_map/all_gather | solution.py:55
  85.0 5.9 %custom-call.8 = f32[2,32,32]{2,1,0:T(8,128)S(1)} custom-call(f32[2,32,32]{2,1,0:T(8,128)S(1)} %fusion.57), custom_call_target="Cholesky" | custom-call | tf_op jit(solution)/shard_map/jit(cholesky)/cholesky | solution.py:61
  91.0 2.2 pad_maximum_fusion
  93.8 2.4 fusion.2
  96.2 2.1 fusion.45
  100.4 2.6 %collective-permute-start.5 = (f32[2560,128]{1,0:T(8,128)S(1)}, f32[2560,128]{1,0:T(8,128)S(1)}, u32[]{:S(2)}, u32[]{:S(2)}) collective-permute-start(f32[2560,128]{1,0:T(8,128)S(1)} %get-tuple-element.32), channel_id=1, source_target_pairs={{0,96},{32,0},{64,32},{96,64},{1,97},{33,1},{65,33},{97,65},{2,98}... | collective-permute-start | bytes 3932168 | tf_op jit(solution)/shard_map/ppermute | solution.py:66
  103.6 13.7 %collective-permute-done.6 = bf16[1,256,2176]{1,2,0:T(8,128)(2,1)S(1)} collective-permute-done((bf16[1,256,2176]{1,2,0:T(8,128)(2,1)S(1)}, bf16[1,256,2176]{1,2,0:T(8,128)(2,1)S(1)}, u32[]{:S(2)}, u32[]{:S(2)}) %collective-permute-start.6) | collective-permute-done | bytes 1114144 | tf_op jit(solution)/shard_map/ppermute | solution.py:66
  117.3 2.8 %pad_maximum_fusion.1 = bf16[1,1024,2176]{1,2,0:T(8,128)(2,1)S(1)} fusion(bf16[1,256,2176]{1,2,0:T(8,128)(2,1)} %collective-permute-done.8, bf16[1,256,2176]{1,2,0:T(8,128)(2,1)} %collective-permute-done.7, bf16[1,256,2176]{1,2,0:T(8,128)(2,1)S(1)} %collective-permute-done.6, bf16[1,256,2176]{1,2,0:T(8,128)(2,1)S(1)} %get-tuple-element.25), kind=kLoop, calls=%fused_computation.3 | loop fusion | flops 17825792 | bytes 8912896 | tf_op jit(solution)/shard_map/concatenate | solution.py:69
  120.6 2.4 fusion
  124.3 2.1 fusion.38
  131.8 4.9 %custom-call.9 = f32[2,1,32,32]{2,3,1,0:T(8,128)S(1)} custom-call(f32[2,1,32,32]{3,2,1,0:T(8,128)S(1)} %select_bitcast_fusion), custom_call_target="InvertDiagBlocksLowerTriangular" | custom-call | tf_op jit(solution)/shard_map/jit(_solve_triangular)/vmap()/triangular_solve | solution.py:63
  137.2 32.2 %collective-permute-done.3 = f32[2560,128]{1,0:T(8,128)} collective-permute-done((f32[2560,128]{1,0:T(8,128)}, f32[2560,128]{1,0:T(8,128)}, u32[]{:S(2)}, u32[]{:S(2)}) %collective-permute-start.3) | collective-permute-done | bytes 1310752 | tf_op jit(solution)/shard_map/ppermute | solution.py:66
  169.4 2.4 fusion.13
  171.9 2.3 fusion.9
  174.9 4.8 %fusion.5 = f32[2,2048,128]{2,1,0:T(8,128)} fusion(f32[1,2560,128]{2,1,0:T(8,128)S(1)} %fusion.13, f32[1,2560,128]{2,1,0:T(8,128)S(1)} %fusion.9, f32[2,32,2048]{2,1,0:T(8,128)S(1)} %fusion.27, s32[]{:T(128)S(6)} %select_n.293), kind=kOutput, calls=%fused_computation.19 | convolution fusion | flops 202375168 | bytes 5275652 | tf_op jit(solution)/shard_map/stp,stq->spq/dot_general | solution.py:103
  179.6 3.6 %gather_fusion.1 = f32[32,128,128]{2,1,0:T(8,128)} fusion(f32[32,128,128]{2,1,0:T(8,128)} %bitcast.75, s32[1024]{0:T(1024)S(1)} %pad_clamp_fusion), kind=kCustom, calls=%fused_computation.1 | custom fusion | bytes 4194432 | tf_op jit(solution)/shard_map/gather | solution.py:119
  183.2 32.1 %all-to-all-start.1 = ((f32[8,4,128,128]{3,2,1,0:T(8,128)}), f32[8,4,128,128]{3,2,1,0:T(8,128)S(1)}, u32[]{:S(2)}, u32[]{:S(2)}) async-start(f32[8,4,128,128]{3,2,1,0:T(8,128)} %bitcast.30), calls=%async_computation.1 | async-start | bytes 4194304 | tf_op jit(solution)/shard_map/all_to_all | solution.py:122
  218.6 23.0 %all-to-all-done.1 = f32[8,4,128,128]{3,2,1,0:T(8,128)S(1)} async-done(((f32[8,4,128,128]{3,2,1,0:T(8,128)}), f32[8,4,128,128]{3,2,1,0:T(8,128)S(1)}, u32[]{:S(2)}, u32[]{:S(2)}) %all-to-all-start.1) | async-done | bytes 2097184 | tf_op jit(solution)/shard_map/all_to_all | solution.py:122
  242.9 9.4 %shard_map.64 = f32[2048,1024]{1,0:T(8,128)} custom-call(s32[32]{0:T(128)} %get-tuple-element.8.order_ref, s32[17]{0:T(128)} %pad_add_fusion.1.starts_ref, s32[32]{0:T(128)} %get-tuple-element.49.col_ref, f32[32,128,128]{2,1,0:T(8,128)} %bitcast.76), custom_call_target="tpu_custom_call" | custom-call | tf_op jit(solution)/shard_map/pallas_call | solution.py:150
  (106 shorter events, 27.0 us)
Async XLA Ops:
  0.0 4.0 %copy-start.7 = (s32[2]{0:T(128)S(1)}, s32[2]{0:T(128)}, u32[]{:S(2)}) copy-start(s32[2]{0:T(128)} %param.9) | copy-start | bytes 28
  0.0 4.0 %copy-start.8 = (s32[2]{0:T(128)S(1)}, s32[2]{0:T(128)}, u32[]{:S(2)}) copy-start(s32[2]{0:T(128)} %param.8) | copy-start | bytes 28
  4.1 1.8 copy-start.5
  13.4 9.3 %copy-start.6 = (s32[2,16]{1,0:T(2,128)S(1)}, s32[2,16]{1,0:T(2,128)}, u32[]{:S(2)}) copy-start(s32[2,16]{1,0:T(2,128)} %param.10) | copy-start | bytes 388
  13.4 10.0 %copy-start.9 = (s32[128]{0:T(128)S(1)}, s32[128]{0:T(128)}, u32[]{:S(2)}) copy-start(s32[128]{0:T(128)} %param.11) | copy-start | bytes 1540
  15.2 75.8 %collective-permute-start.2 = (bf16[1,256,2176]{1,2,0:T(8,128)(2,1)S(1)}, bf16[1,256,2176]{1,2,0:T(8,128)(2,1)}, u32[]{:S(2)}, u32[]{:S(2)}) collective-permute-start(bf16[1,256,2176]{1,2,0:T(8,128)(2,1)S(1)} %get-tuple-element.26), channel_id=1, source_target_pairs={{0,24},{8,0},{16,8},{24,16},{1,25},{9,1},{17,9},{25,17},{2,26},{10... | collective-permute-start | bytes 3342344 | tf_op jit(solution)/shard_map/ppermute | solution.py:66
  18.5 72.5 %collective-permute-start.1 = (bf16[1,256,2176]{1,2,0:T(8,128)(2,1)S(1)}, bf16[1,256,2176]{1,2,0:T(8,128)(2,1)}, u32[]{:S(2)}, u32[]{:S(2)}) collective-permute-start(bf16[1,256,2176]{1,2,0:T(8,128)(2,1)S(1)} %get-tuple-element.26), channel_id=1, source_target_pairs={{0,16},{8,24},{16,0},{24,8},{1,17},{9,25},{17,1},{25,9},{2,18},{10... | collective-permute-start | bytes 3342344 | tf_op jit(solution)/shard_map/ppermute | solution.py:66
  19.1 72.0 %collective-permute-start = (bf16[1,256,2176]{1,2,0:T(8,128)(2,1)S(1)}, bf16[1,256,2176]{1,2,0:T(8,128)(2,1)}, u32[]{:S(2)}, u32[]{:S(2)}) collective-permute-start(bf16[1,256,2176]{1,2,0:T(8,128)(2,1)S(1)} %get-tuple-element.26), channel_id=1, source_target_pairs={{0,8},{8,16},{16,24},{24,0},{1,9},{9,17},{17,25},{25,1},{2,10},{10... | collective-permute-start | bytes 3342344 | tf_op jit(solution)/shard_map/ppermute | solution.py:66
  19.7 83.4 %collective-permute-start.8 = (bf16[1,256,2176]{1,2,0:T(8,128)(2,1)S(1)}, bf16[1,256,2176]{1,2,0:T(8,128)(2,1)}, u32[]{:S(2)}, u32[]{:S(2)}) collective-permute-start(bf16[1,256,2176]{1,2,0:T(8,128)(2,1)S(1)} %get-tuple-element.25), channel_id=1, source_target_pairs={{0,96},{32,0},{64,32},{96,64},{1,97},{33,1},{65,33},{97,65},{2,98}... | collective-permute-start | bytes 3342344 | tf_op jit(solution)/shard_map/ppermute | solution.py:66
  22.4 81.2 %collective-permute-start.7 = (bf16[1,256,2176]{1,2,0:T(8,128)(2,1)S(1)}, bf16[1,256,2176]{1,2,0:T(8,128)(2,1)}, u32[]{:S(2)}, u32[]{:S(2)}) collective-permute-start(bf16[1,256,2176]{1,2,0:T(8,128)(2,1)S(1)} %get-tuple-element.25), channel_id=1, source_target_pairs={{0,64},{32,96},{64,0},{96,32},{1,65},{33,97},{65,1},{97,33},{2,66}... | collective-permute-start | bytes 3342344 | tf_op jit(solution)/shard_map/ppermute | solution.py:66
  26.5 156.8 %all-to-all-start = ((s32[8,4,2]{1,2,0:T(2,128)}), s32[8,4,2]{1,2,0:T(2,128)S(1)}, u32[]{:S(2)}, u32[]{:S(2)}) async-start(s32[8,4,2]{1,2,0:T(2,128)} %copy.38), calls=%async_computation | async-start | bytes 16384 | tf_op jit(solution)/shard_map/all_to_all | solution.py:123
  90.9 26.3 %collective-permute-start.6 = (bf16[1,256,2176]{1,2,0:T(8,128)(2,1)S(1)}, bf16[1,256,2176]{1,2,0:T(8,128)(2,1)S(1)}, u32[]{:S(2)}, u32[]{:S(2)}) collective-permute-start(bf16[1,256,2176]{1,2,0:T(8,128)(2,1)S(1)} %get-tuple-element.25), channel_id=1, source_target_pairs={{0,32},{32,64},{64,96},{96,0},{1,33},{33,65},{65,97},{97,1},{2,34}... | collective-permute-start | bytes 3342344 | tf_op jit(solution)/shard_map/ppermute | solution.py:66
  100.4 29.3 %collective-permute-start.5 = (f32[2560,128]{1,0:T(8,128)S(1)}, f32[2560,128]{1,0:T(8,128)S(1)}, u32[]{:S(2)}, u32[]{:S(2)}) collective-permute-start(f32[2560,128]{1,0:T(8,128)S(1)} %get-tuple-element.32), channel_id=1, source_target_pairs={{0,96},{32,0},{64,32},{96,64},{1,97},{33,1},{65,33},{97,65},{2,98}... | collective-permute-start | bytes 3932168 | tf_op jit(solution)/shard_map/ppermute | solution.py:66
  103.0 34.2 %collective-permute-start.4 = (f32[2560,128]{1,0:T(8,128)}, f32[2560,128]{1,0:T(8,128)}, u32[]{:S(2)}, u32[]{:S(2)}) collective-permute-start(f32[2560,128]{1,0:T(8,128)} %get-tuple-element.31), channel_id=1, source_target_pairs={{0,64},{32,96},{64,0},{96,32},{1,65},{33,97},{65,1},{97,33},{2,66}... | collective-permute-start | bytes 3932168 | tf_op jit(solution)/shard_map/ppermute | solution.py:66
  103.0 66.4 %collective-permute-start.3 = (f32[2560,128]{1,0:T(8,128)}, f32[2560,128]{1,0:T(8,128)}, u32[]{:S(2)}, u32[]{:S(2)}) collective-permute-start(f32[2560,128]{1,0:T(8,128)} %get-tuple-element.30), channel_id=1, source_target_pairs={{0,32},{32,64},{64,96},{96,0},{1,33},{33,65},{65,97},{97,1},{2,34}... | collective-permute-start | bytes 3932168 | tf_op jit(solution)/shard_map/ppermute | solution.py:66
  126.4 2.1 copy-start.2
  128.5 43.4 %collective-permute-start.11 = (f32[2560,128]{1,0:T(8,128)}, f32[2560,128]{1,0:T(8,128)}, u32[]{:S(2)}, u32[]{:S(2)}) collective-permute-start(f32[2560,128]{1,0:T(8,128)} %get-tuple-element.29), channel_id=1, source_target_pairs={{0,24},{8,0},{16,8},{24,16},{1,25},{9,1},{17,9},{25,17},{2,26},{10... | collective-permute-start | bytes 3932168 | tf_op jit(solution)/shard_map/ppermute | solution.py:66
  128.5 43.4 %collective-permute-start.10 = (f32[2560,128]{1,0:T(8,128)}, f32[2560,128]{1,0:T(8,128)}, u32[]{:S(2)}, u32[]{:S(2)}) collective-permute-start(f32[2560,128]{1,0:T(8,128)} %get-tuple-element.28), channel_id=1, source_target_pairs={{0,16},{8,24},{16,0},{24,8},{1,17},{9,25},{17,1},{25,9},{2,18},{10... | collective-permute-start | bytes 3932168 | tf_op jit(solution)/shard_map/ppermute | solution.py:66
  129.7 1.1 copy-start.4
  130.8 41.1 %collective-permute-start.9 = (f32[2560,128]{1,0:T(8,128)}, f32[2560,128]{1,0:T(8,128)}, u32[]{:S(2)}, u32[]{:S(2)}) collective-permute-start(f32[2560,128]{1,0:T(8,128)} %get-tuple-element.27), channel_id=1, source_target_pairs={{0,8},{8,16},{16,24},{24,0},{1,9},{9,17},{17,25},{25,1},{2,10},{10... | collective-permute-start | bytes 3932168 | tf_op jit(solution)/shard_map/ppermute | solution.py:66
  169.4 2.5 copy-start.1
  169.4 2.5 copy-start.3
  183.2 58.3 %all-to-all-start.1 = ((f32[8,4,128,128]{3,2,1,0:T(8,128)}), f32[8,4,128,128]{3,2,1,0:T(8,128)S(1)}, u32[]{:S(2)}, u32[]{:S(2)}) async-start(f32[8,4,128,128]{3,2,1,0:T(8,128)} %bitcast.30), calls=%async_computation.1 | async-start | bytes 4194304 | tf_op jit(solution)/shard_map/all_to_all | solution.py:122
  241.5 1.3 copy-start

commit v10 on v9

--- a/solution.py
+++ b/solution.py
@@ -135,25 +135,28 @@
 def place(recv, order, starts, col_block, n_rows, n_cols):
     items, tile_pixels, _ = recv.shape
 
+    group = 4 if n_rows % 4 == 0 else 1
+
     def kernel(order_ref, starts_ref, col_ref, recv_ref, out_ref):
         r = pl.program_id(0)
         out_ref[...] = jnp.zeros(out_ref.shape, out_ref.dtype)
+        for q in range(group):
 
-        def body(k, carry):
-            i = order_ref[k]
-            at = pl.ds(pl.multiple_of(col_ref[i] * tile_pixels, tile_pixels), tile_pixels)
-            out_ref[:, at] += recv_ref[i]
-            return carry
+            def body(k, carry, q=q):
+                i = order_ref[k]
+                at = pl.ds(pl.multiple_of(col_ref[i] * tile_pixels, tile_pixels), tile_pixels)
+                out_ref[q * tile_pixels : (q + 1) * tile_pixels, at] += recv_ref[i]
+                return carry
 
-        lax.fori_loop(starts_ref[r], starts_ref[r + 1], body, 0)
+            lax.fori_loop(starts_ref[r * group + q], starts_ref[r * group + q + 1], body, 0)
 
     return pl.pallas_call(
         kernel,
         grid_spec=pltpu.PrefetchScalarGridSpec(
             num_scalar_prefetch=3,
-            grid=(n_rows,),
+            grid=(n_rows // group,),
             in_specs=[pl.BlockSpec((items, tile_pixels, tile_pixels), lambda r, a, b, c: (0, 0, 0))],
-            out_specs=pl.BlockSpec((tile_pixels, n_cols * tile_pixels), lambda r, a, b, c: (r, 0)),
+            out_specs=pl.BlockSpec((group * tile_pixels, n_cols * tile_pixels), lambda r, a, b, c: (r, 0)),
         ),
         out_shape=jax.ShapeDtypeStruct((n_rows * tile_pixels, n_cols * tile_pixels), jnp.float32),
     )(order, starts, col_block, recv)

time: 253 us -> 250 us (0.988)
  Pallas kernels: 9.41 us -> 6.22 us
    pallas_call x1, Pallas kernels: 9.41 us -> 6.22 us  [place(): pl.pallas_call(kernel, grid_spec=pltpu.PrefetchScalarGridSpec(num_scalar_...]
  transfers between devices with their start and end apart: 14 -> 14, of which waited for: 4 -> 4; matrix products, arithmetic and copies ran while one was open for 21% -> 22% of each run, Pallas kernels for 0% -> 0%
where the time goes in v10:
time: 250 us; the launch traced here: 249 us
  waiting for transfers between devices  69.1 us (28%)
  starting transfers between devices  52.4 us (21%)
  blocking collectives  49.1 us (20%)
  other arithmetic  32.2 us (13%)
  local copies, waits for them, and re-layouts  24.8 us (10%)
  matrix products  14.8 us (6%)
  Pallas kernels  6.22 us (2%)
    all_gather x1, blocking collectives, per_device(): lax.all_gather(ground_bin.astype(jnp.bfloat16), SCAN_AXES, axis=1, tiled=...  49.1 us
    ppermute x12, waiting for transfers between devices, shifted(): return lax.ppermute(x, axis, [(i, (i + d) % n) for i in range(n)])  46.1 us
    all_to_all x1, starting transfers between devices, per_device(): lax.all_to_all(send_rows, 'tile', split_axis=0, concat_axis=0, tiled=True)  32.1 us
    all_to_all x1, waiting for transfers between devices, per_device(): lax.all_to_all(send_rows, 'tile', split_axis=0, concat_axis=0, tiled=True)  23 us
    ppermute x12, starting transfers between devices, shifted(): return lax.ppermute(x, axis, [(i, (i + d) % n) for i in range(n)])  12.9 us
    all_to_all x1, starting transfers between devices, per_device(): lax.all_to_all(send_labels, 'tile', split_axis=0, concat_axis=0, tiled=True)  7.38 us
    concatenate x1, local copies, waits for them, and re-layouts, per_device(): local = jnp.concatenate([masked, template, pad], axis=2)  7.35 us
    unnamed x21, local copies, waits for them, and re-layouts  6.44 us
  transfers between devices with their start and end apart: 14, of which 4 were waited for; matrix products, arithmetic and copies ran while one was open for 22% of the time, Pallas kernels for 0%

profile of v10, /device:TPU:1, one launch (start us, length us, event | category | flops | bytes accessed | tf_op | source)
XLA Modules:
  0.0 249.1 jit_solution(568282001201037195)
XLA Ops:
  0.0 3.9 %copy.41 = bf16[2,256,2048]{1,2,0:T(8,128)(2,1)} copy(bf16[2,256,2048]{2,1,0:T(8,128)(2,1)} %param.6) | data formatting | bytes 4194304 | tf_op args[0]
  6.1 7.3 %concatenate.54 = bf16[2,256,2176]{1,2,0:T(8,128)(2,1)} concatenate(bf16[2,256,2048]{1,2,0:T(8,128)(2,1)S(1)} %broadcast_select_fusion, bf16[2,256,1]{1,2,0:T(2,128)(2,1)S(1)} %get-tuple-element.48, bf16[2,256,1]{1,2,0:T(2,128)(2,1)S(1)} %get-tuple-element.47, bf16[2,256,1]{1,2,0:T(2,128)(2,1)S(1)} %get-tuple-element.46, bf16[2,256,1]{1,2,0:T(2,128)(2,1)S(1)} %get-tuple-element.45, ...), dimensions={2} | concatenate | bytes 4456448 | tf_op jit(solution)/shard_map/concatenate | solution.py:53
  15.2 3.4 %collective-permute-start.2 = (bf16[1,256,2176]{1,2,0:T(8,128)(2,1)S(1)}, bf16[1,256,2176]{1,2,0:T(8,128)(2,1)}, u32[]{:S(2)}, u32[]{:S(2)}) collective-permute-start(bf16[1,256,2176]{1,2,0:T(8,128)(2,1)S(1)} %get-tuple-element.26), channel_id=1, source_target_pairs={{0,24},{8,0},{16,8},{24,16},{1,25},{9,1},{17,9},{25,17},{2,26},{10... | collective-permute-start | bytes 3342344 | tf_op jit(solution)/shard_map/ppermute | solution.py:66
  19.7 2.7 %collective-permute-start.8 = (bf16[1,256,2176]{1,2,0:T(8,128)(2,1)S(1)}, bf16[1,256,2176]{1,2,0:T(8,128)(2,1)}, u32[]{:S(2)}, u32[]{:S(2)}) collective-permute-start(bf16[1,256,2176]{1,2,0:T(8,128)(2,1)S(1)} %get-tuple-element.25), channel_id=1, source_target_pairs={{0,96},{32,0},{64,32},{96,64},{1,97},{33,1},{65,33},{97,65},{2,98}... | collective-permute-start | bytes 3342344 | tf_op jit(solution)/shard_map/ppermute | solution.py:66
  26.5 7.4 %all-to-all-start = ((s32[8,4,2]{1,2,0:T(2,128)}), s32[8,4,2]{1,2,0:T(2,128)S(1)}, u32[]{:S(2)}, u32[]{:S(2)}) async-start(s32[8,4,2]{1,2,0:T(2,128)} %copy.38), calls=%async_computation | async-start | bytes 16384 | tf_op jit(solution)/shard_map/all_to_all | solution.py:123
  33.9 49.1 %all_gather.3 = bf16[2,4096]{1,0:T(2,128)(2,1)S(1)} all-gather(bf16[2,256]{1,0:T(2,128)(2,1)S(1)} %convert_element_type.63), channel_id=1, replica_groups=mesh['sy'=4,'sx'=4,'tile'=8] {'sy','sx'}, dimensions={1}, use_global_device_ids=true | all-gather | bytes 17408 | tf_op jit(solution)/shard_map/all_gather | solution.py:55
  85.0 5.9 %custom-call.8 = f32[2,32,32]{2,1,0:T(8,128)S(1)} custom-call(f32[2,32,32]{2,1,0:T(8,128)S(1)} %fusion.57), custom_call_target="Cholesky" | custom-call | tf_op jit(solution)/shard_map/jit(cholesky)/cholesky | solution.py:61
  91.0 2.2 pad_maximum_fusion
  93.8 2.4 fusion.2
  96.2 2.1 fusion.45
  100.4 2.6 %collective-permute-start.5 = (f32[2560,128]{1,0:T(8,128)S(1)}, f32[2560,128]{1,0:T(8,128)S(1)}, u32[]{:S(2)}, u32[]{:S(2)}) collective-permute-start(f32[2560,128]{1,0:T(8,128)S(1)} %get-tuple-element.32), channel_id=1, source_target_pairs={{0,96},{32,0},{64,32},{96,64},{1,97},{33,1},{65,33},{97,65},{2,98}... | collective-permute-start | bytes 3932168 | tf_op jit(solution)/shard_map/ppermute | solution.py:66
  103.6 13.7 %collective-permute-done.6 = bf16[1,256,2176]{1,2,0:T(8,128)(2,1)S(1)} collective-permute-done((bf16[1,256,2176]{1,2,0:T(8,128)(2,1)S(1)}, bf16[1,256,2176]{1,2,0:T(8,128)(2,1)S(1)}, u32[]{:S(2)}, u32[]{:S(2)}) %collective-permute-start.6) | collective-permute-done | bytes 1114144 | tf_op jit(solution)/shard_map/ppermute | solution.py:66
  117.3 2.8 %pad_maximum_fusion.1 = bf16[1,1024,2176]{1,2,0:T(8,128)(2,1)S(1)} fusion(bf16[1,256,2176]{1,2,0:T(8,128)(2,1)} %collective-permute-done.8, bf16[1,256,2176]{1,2,0:T(8,128)(2,1)} %collective-permute-done.7, bf16[1,256,2176]{1,2,0:T(8,128)(2,1)S(1)} %collective-permute-done.6, bf16[1,256,2176]{1,2,0:T(8,128)(2,1)S(1)} %get-tuple-element.25), kind=kLoop, calls=%fused_computation.3 | loop fusion | flops 17825792 | bytes 8912896 | tf_op jit(solution)/shard_map/concatenate | solution.py:69
  120.6 2.4 fusion
  124.3 2.1 fusion.38
  131.8 4.9 %custom-call.9 = f32[2,1,32,32]{2,3,1,0:T(8,128)S(1)} custom-call(f32[2,1,32,32]{3,2,1,0:T(8,128)S(1)} %select_bitcast_fusion), custom_call_target="InvertDiagBlocksLowerTriangular" | custom-call | tf_op jit(solution)/shard_map/jit(_solve_triangular)/vmap()/triangular_solve | solution.py:63
  137.2 32.2 %collective-permute-done.3 = f32[2560,128]{1,0:T(8,128)} collective-permute-done((f32[2560,128]{1,0:T(8,128)}, f32[2560,128]{1,0:T(8,128)}, u32[]{:S(2)}, u32[]{:S(2)}) %collective-permute-start.3) | collective-permute-done | bytes 1310752 | tf_op jit(solution)/shard_map/ppermute | solution.py:66
  169.4 2.4 fusion.13
  171.9 2.3 fusion.9
  174.9 4.8 %fusion.5 = f32[2,2048,128]{2,1,0:T(8,128)} fusion(f32[1,2560,128]{2,1,0:T(8,128)S(1)} %fusion.13, f32[1,2560,128]{2,1,0:T(8,128)S(1)} %fusion.9, f32[2,32,2048]{2,1,0:T(8,128)S(1)} %fusion.27, s32[]{:T(128)S(6)} %select_n.293), kind=kOutput, calls=%fused_computation.19 | convolution fusion | flops 202375168 | bytes 5275652 | tf_op jit(solution)/shard_map/stp,stq->spq/dot_general | solution.py:103
  179.6 3.6 %gather_fusion.1 = f32[32,128,128]{2,1,0:T(8,128)} fusion(f32[32,128,128]{2,1,0:T(8,128)} %bitcast.75, s32[1024]{0:T(1024)S(1)} %pad_clamp_fusion), kind=kCustom, calls=%fused_computation.1 | custom fusion | bytes 4194432 | tf_op jit(solution)/shard_map/gather | solution.py:119
  183.2 32.1 %all-to-all-start.1 = ((f32[8,4,128,128]{3,2,1,0:T(8,128)}), f32[8,4,128,128]{3,2,1,0:T(8,128)S(1)}, u32[]{:S(2)}, u32[]{:S(2)}) async-start(f32[8,4,128,128]{3,2,1,0:T(8,128)} %bitcast.30), calls=%async_computation.1 | async-start | bytes 4194304 | tf_op jit(solution)/shard_map/all_to_all | solution.py:122
  218.6 23.0 %all-to-all-done.1 = f32[8,4,128,128]{3,2,1,0:T(8,128)S(1)} async-done(((f32[8,4,128,128]{3,2,1,0:T(8,128)}), f32[8,4,128,128]{3,2,1,0:T(8,128)S(1)}, u32[]{:S(2)}, u32[]{:S(2)}) %all-to-all-start.1) | async-done | bytes 2097184 | tf_op jit(solution)/shard_map/all_to_all | solution.py:122
  242.9 6.2 %shard_map.64 = f32[2048,1024]{1,0:T(8,128)} custom-call(s32[32]{0:T(128)} %get-tuple-element.8.order_ref, s32[17]{0:T(128)} %pad_add_fusion.1.starts_ref, s32[32]{0:T(128)} %get-tuple-element.49.col_ref, f32[32,128,128]{2,1,0:T(8,128)} %bitcast.76), custom_call_target="tpu_custom_call" | custom-call | tf_op jit(solution)/shard_map/pallas_call | solution.py:153
  (106 shorter events, 27.0 us)
Async XLA Ops:
  0.0 4.0 %copy-start.7 = (s32[2]{0:T(128)S(1)}, s32[2]{0:T(128)}, u32[]{:S(2)}) copy-start(s32[2]{0:T(128)} %param.9) | copy-start | bytes 28
  0.0 4.0 %copy-start.8 = (s32[2]{0:T(128)S(1)}, s32[2]{0:T(128)}, u32[]{:S(2)}) copy-start(s32[2]{0:T(128)} %param.8) | copy-start | bytes 28
  4.1 1.8 copy-start.5
  13.4 9.3 %copy-start.6 = (s32[2,16]{1,0:T(2,128)S(1)}, s32[2,16]{1,0:T(2,128)}, u32[]{:S(2)}) copy-start(s32[2,16]{1,0:T(2,128)} %param.10) | copy-start | bytes 388
  13.4 10.0 %copy-start.9 = (s32[128]{0:T(128)S(1)}, s32[128]{0:T(128)}, u32[]{:S(2)}) copy-start(s32[128]{0:T(128)} %param.11) | copy-start | bytes 1540
  15.2 75.8 %collective-permute-start.2 = (bf16[1,256,2176]{1,2,0:T(8,128)(2,1)S(1)}, bf16[1,256,2176]{1,2,0:T(8,128)(2,1)}, u32[]{:S(2)}, u32[]{:S(2)}) collective-permute-start(bf16[1,256,2176]{1,2,0:T(8,128)(2,1)S(1)} %get-tuple-element.26), channel_id=1, source_target_pairs={{0,24},{8,0},{16,8},{24,16},{1,25},{9,1},{17,9},{25,17},{2,26},{10... | collective-permute-start | bytes 3342344 | tf_op jit(solution)/shard_map/ppermute | solution.py:66
  18.5 72.5 %collective-permute-start.1 = (bf16[1,256,2176]{1,2,0:T(8,128)(2,1)S(1)}, bf16[1,256,2176]{1,2,0:T(8,128)(2,1)}, u32[]{:S(2)}, u32[]{:S(2)}) collective-permute-start(bf16[1,256,2176]{1,2,0:T(8,128)(2,1)S(1)} %get-tuple-element.26), channel_id=1, source_target_pairs={{0,16},{8,24},{16,0},{24,8},{1,17},{9,25},{17,1},{25,9},{2,18},{10... | collective-permute-start | bytes 3342344 | tf_op jit(solution)/shard_map/ppermute | solution.py:66
  19.1 72.0 %collective-permute-start = (bf16[1,256,2176]{1,2,0:T(8,128)(2,1)S(1)}, bf16[1,256,2176]{1,2,0:T(8,128)(2,1)}, u32[]{:S(2)}, u32[]{:S(2)}) collective-permute-start(bf16[1,256,2176]{1,2,0:T(8,128)(2,1)S(1)} %get-tuple-element.26), channel_id=1, source_target_pairs={{0,8},{8,16},{16,24},{24,0},{1,9},{9,17},{17,25},{25,1},{2,10},{10... | collective-permute-start | bytes 3342344 | tf_op jit(solution)/shard_map/ppermute | solution.py:66
  19.7 83.4 %collective-permute-start.8 = (bf16[1,256,2176]{1,2,0:T(8,128)(2,1)S(1)}, bf16[1,256,2176]{1,2,0:T(8,128)(2,1)}, u32[]{:S(2)}, u32[]{:S(2)}) collective-permute-start(bf16[1,256,2176]{1,2,0:T(8,128)(2,1)S(1)} %get-tuple-element.25), channel_id=1, source_target_pairs={{0,96},{32,0},{64,32},{96,64},{1,97},{33,1},{65,33},{97,65},{2,98}... | collective-permute-start | bytes 3342344 | tf_op jit(solution)/shard_map/ppermute | solution.py:66
  22.4 81.2 %collective-permute-start.7 = (bf16[1,256,2176]{1,2,0:T(8,128)(2,1)S(1)}, bf16[1,256,2176]{1,2,0:T(8,128)(2,1)}, u32[]{:S(2)}, u32[]{:S(2)}) collective-permute-start(bf16[1,256,2176]{1,2,0:T(8,128)(2,1)S(1)} %get-tuple-element.25), channel_id=1, source_target_pairs={{0,64},{32,96},{64,0},{96,32},{1,65},{33,97},{65,1},{97,33},{2,66}... | collective-permute-start | bytes 3342344 | tf_op jit(solution)/shard_map/ppermute | solution.py:66
  26.5 156.8 %all-to-all-start = ((s32[8,4,2]{1,2,0:T(2,128)}), s32[8,4,2]{1,2,0:T(2,128)S(1)}, u32[]{:S(2)}, u32[]{:S(2)}) async-start(s32[8,4,2]{1,2,0:T(2,128)} %copy.38), calls=%async_computation | async-start | bytes 16384 | tf_op jit(solution)/shard_map/all_to_all | solution.py:123
  90.9 26.3 %collective-permute-start.6 = (bf16[1,256,2176]{1,2,0:T(8,128)(2,1)S(1)}, bf16[1,256,2176]{1,2,0:T(8,128)(2,1)S(1)}, u32[]{:S(2)}, u32[]{:S(2)}) collective-permute-start(bf16[1,256,2176]{1,2,0:T(8,128)(2,1)S(1)} %get-tuple-element.25), channel_id=1, source_target_pairs={{0,32},{32,64},{64,96},{96,0},{1,33},{33,65},{65,97},{97,1},{2,34}... | collective-permute-start | bytes 3342344 | tf_op jit(solution)/shard_map/ppermute | solution.py:66
  100.4 29.3 %collective-permute-start.5 = (f32[2560,128]{1,0:T(8,128)S(1)}, f32[2560,128]{1,0:T(8,128)S(1)}, u32[]{:S(2)}, u32[]{:S(2)}) collective-permute-start(f32[2560,128]{1,0:T(8,128)S(1)} %get-tuple-element.32), channel_id=1, source_target_pairs={{0,96},{32,0},{64,32},{96,64},{1,97},{33,1},{65,33},{97,65},{2,98}... | collective-permute-start | bytes 3932168 | tf_op jit(solution)/shard_map/ppermute | solution.py:66
  103.0 34.2 %collective-permute-start.4 = (f32[2560,128]{1,0:T(8,128)}, f32[2560,128]{1,0:T(8,128)}, u32[]{:S(2)}, u32[]{:S(2)}) collective-permute-start(f32[2560,128]{1,0:T(8,128)} %get-tuple-element.31), channel_id=1, source_target_pairs={{0,64},{32,96},{64,0},{96,32},{1,65},{33,97},{65,1},{97,33},{2,66}... | collective-permute-start | bytes 3932168 | tf_op jit(solution)/shard_map/ppermute | solution.py:66
  103.0 66.4 %collective-permute-start.3 = (f32[2560,128]{1,0:T(8,128)}, f32[2560,128]{1,0:T(8,128)}, u32[]{:S(2)}, u32[]{:S(2)}) collective-permute-start(f32[2560,128]{1,0:T(8,128)} %get-tuple-element.30), channel_id=1, source_target_pairs={{0,32},{32,64},{64,96},{96,0},{1,33},{33,65},{65,97},{97,1},{2,34}... | collective-permute-start | bytes 3932168 | tf_op jit(solution)/shard_map/ppermute | solution.py:66
  126.4 2.1 copy-start.2
  128.5 43.4 %collective-permute-start.11 = (f32[2560,128]{1,0:T(8,128)}, f32[2560,128]{1,0:T(8,128)}, u32[]{:S(2)}, u32[]{:S(2)}) collective-permute-start(f32[2560,128]{1,0:T(8,128)} %get-tuple-element.29), channel_id=1, source_target_pairs={{0,24},{8,0},{16,8},{24,16},{1,25},{9,1},{17,9},{25,17},{2,26},{10... | collective-permute-start | bytes 3932168 | tf_op jit(solution)/shard_map/ppermute | solution.py:66
  128.5 43.4 %collective-permute-start.10 = (f32[2560,128]{1,0:T(8,128)}, f32[2560,128]{1,0:T(8,128)}, u32[]{:S(2)}, u32[]{:S(2)}) collective-permute-start(f32[2560,128]{1,0:T(8,128)} %get-tuple-element.28), channel_id=1, source_target_pairs={{0,16},{8,24},{16,0},{24,8},{1,17},{9,25},{17,1},{25,9},{2,18},{10... | collective-permute-start | bytes 3932168 | tf_op jit(solution)/shard_map/ppermute | solution.py:66
  129.7 1.1 copy-start.4
  130.8 41.1 %collective-permute-start.9 = (f32[2560,128]{1,0:T(8,128)}, f32[2560,128]{1,0:T(8,128)}, u32[]{:S(2)}, u32[]{:S(2)}) collective-permute-start(f32[2560,128]{1,0:T(8,128)} %get-tuple-element.27), channel_id=1, source_target_pairs={{0,8},{8,16},{16,24},{24,0},{1,9},{9,17},{17,25},{25,1},{2,10},{10... | collective-permute-start | bytes 3932168 | tf_op jit(solution)/shard_map/ppermute | solution.py:66
  169.4 2.5 copy-start.1
  169.4 2.5 copy-start.3
  183.2 58.3 %all-to-all-start.1 = ((f32[8,4,128,128]{3,2,1,0:T(8,128)}), f32[8,4,128,128]{3,2,1,0:T(8,128)S(1)}, u32[]{:S(2)}, u32[]{:S(2)}) async-start(f32[8,4,128,128]{3,2,1,0:T(8,128)} %bitcast.30), calls=%async_computation.1 | async-start | bytes 4194304 | tf_op jit(solution)/shard_map/all_to_all | solution.py:122
  241.5 1.3 copy-start
